TPU v7x, 256 devices: a whole 4x4x8 slice. The times are simulated.
256 devices in a mesh: shot: 16 (over y_lo, z), gx: 16 (over y_hi, x, core).
Axes of the slice: x: 4, y: 4 (y_hi: 2, y_lo: 2; y = y_hi * 2 + y_lo), z: 8, core: 2. Of those that a mesh axis runs over, the one named last changes fastest.
Arguments:
- source_prev: float32 [16, 256, 64, 128], P('shot', 'gx'), may hold values from -6 to 6
- source_now: float32 [16, 256, 64, 128], P('shot', 'gx'), may hold values from -6 to 6
- receiver_prev: float32 [16, 256, 64, 128], P('shot', 'gx'), may hold values from -6 to 6
- receiver_now: float32 [16, 256, 64, 128], P('shot', 'gx'), may hold values from -6 to 6
- courant: float32 [256, 64, 128], P('gx'), may hold values from 0.05 to 0.3
- source_cells: int32 [16, 8], P('shot'), may hold values from 0 to 2097151
- wavelet: float32 [16, 2, 8], P('shot'), may hold values from -128 to 128
- receiver_cells: int32 [16, 512], P('shot'), may hold values from 0 to 2097151
- receiver_data: float32 [16, 2, 512], P('shot'), may hold values from -128 to 128
- offsets: int32 [9], replicated, may hold values from -8 to 8, as said below
- conv_weight: float32 [64, 9, 3, 3, 3], replicated, may hold values from -1.25 to 1.25
- conv_bias: float32 [64], replicated, may hold values from -3 to 3
Outputs:
- summary: float32 [64, 64, 512], P(None, 'gx', 'shot')
Inputs may be any that keep to these rules, and one draw needn't show every extreme that they name: The offsets are distinct and include -8 and 8.
All inputs are finite; a program needn't handle non-finite values.
Results may differ from a plain program's by a relative error of at most 0.0003.
Values sent between devices are 32-bit elements; how exact they have to be, the bound alone decides.
No kernel may reach another device: no remote copies, remote signals or barrier semaphores. Data moves between devices by JAX's collectives and lax.ppermute only.
A program may use at most 64 MiB of HBM per device.

v0:
```python
import jax
import jax.numpy as jnp
from jax import lax
from jax.sharding import PartitionSpec as P

HMAX = 8


def padded_2(block, sides, width):
    for axis, dim in sides:
        count = lax.axis_size(axis)
        forward = [(i, i + 1) for i in range(count - 1)]
        backward = [(target, source) for source, target in forward]
        low = lax.ppermute(
            lax.slice_in_dim(block, block.shape[dim] - width, None, axis=dim), axis, forward
        )
        high = lax.ppermute(lax.slice_in_dim(block, 0, width, axis=dim), axis, backward)
        block = jnp.concatenate([low, block, high], axis=dim)
    return block


def inject(cells_here, first_x, cell_index, amplitudes, size_y, size_z):
    plane_size = size_y * size_z
    column = cell_index // plane_size
    within = cell_index % plane_size
    local_x = column - first_x
    inside = (local_x >= 0) & (local_x < cells_here)
    target = jnp.where(inside, local_x * plane_size + within, cells_here * plane_size)
    flat_cells = jnp.zeros((cells_here * plane_size + 1,), jnp.float32).at[target].add(amplitudes)
    return flat_cells[:-1].reshape(cells_here, size_y, size_z)


def laplace_step(previous, extended, courant, sources):
    center = extended[:, 1:-1]
    padded = jnp.pad(center, ((0, 0), (0, 0), (1, 1), (1, 1)))
    laplace = extended[:, 2:] + extended[:, :-2]
    laplace = laplace + padded[:, :, 2:, 1:-1] + padded[:, :, :-2, 1:-1]
    laplace = laplace + padded[:, :, 1:-1, 2:] + padded[:, :, 1:-1, :-2] - 6.0 * center
    return 2.0 * center - previous + courant * laplace + sources


def coarsen(image_block):
    size_x, size_y, size_z = image_block.shape
    return image_block.reshape(size_x // 4, 4, size_y // 4, 4, size_z // 4, 4).mean(axis=(1, 3, 5))


def offset_image(wide, offsets, margin, cells_x):

    def per_offset(offset_value):
        forward_part = lax.dynamic_slice_in_dim(wide, margin + offset_value, cells_x, 1)
        backward_part = lax.dynamic_slice_in_dim(wide, margin - offset_value, cells_x, 1)
        image_block = forward_part[0] * backward_part[1] + forward_part[2] * backward_part[3]
        return coarsen(image_block)

    return lax.map(per_offset, offsets)


def conv_apply(padded, conv_weight, conv_bias):
    channels, span_x, span_y, span_z = padded.shape
    size_x, size_y, size_z = (span_x - 2, span_y - 2, span_z - 2)
    patches = jnp.stack(
        [
            padded[:, step_x : step_x + size_x, step_y : step_y + size_y, step_z : step_z + size_z]
            for step_x in range(3)
            for step_y in range(3)
            for step_z in range(3)
        ],
        axis=1,
    )
    patches = patches.reshape(channels * 27, size_x * size_y * size_z)
    matrix = conv_weight.reshape(conv_weight.shape[0], channels * 27)
    result = jnp.dot(
        matrix, patches, precision=lax.Precision.HIGHEST, preferred_element_type=jnp.float32
    )
    result = result + conv_bias[:, None]
    return result.reshape(conv_weight.shape[0], size_x, size_y * size_z)


def local(
    source_prev,
    source_now,
    receiver_prev,
    receiver_now,
    courant,
    source_cells,
    wavelet,
    receiver_cells,
    receiver_data,
    offsets,
    conv_weight,
    conv_bias,
):
    cells_x, size_y, size_z = courant.shape
    slab_index = lax.axis_index("gx")
    previous = jnp.stack([source_prev[0], receiver_prev[0]])
    current = jnp.stack([source_now[0], receiver_now[0]])
    levels = []
    for step_index in range(2):
        extended = padded_2(current, (("gx", 1),), 1)
        first_x = slab_index * cells_x
        advanced = laplace_step(
            previous,
            extended,
            courant,
            jnp.stack(
                [
                    inject(
                        cells_x, first_x, source_cells[0], wavelet[0, step_index], size_y, size_z
                    ),
                    inject(
                        cells_x,
                        first_x,
                        receiver_cells[0],
                        receiver_data[0, step_index],
                        size_y,
                        size_z,
                    ),
                ]
            ),
        )
        previous, current = (current, advanced)
        levels.append(advanced)
    fields = jnp.concatenate(levels, axis=0)
    wide = padded_2(fields, (("gx", 1),), HMAX)
    coarse = offset_image(wide, offsets, HMAX, cells_x)
    summed = lax.psum(coarse, "shot")
    rimmed = padded_2(summed, (("gx", 1),), 1)
    row_count = summed.shape[2] // lax.axis_size("shot")
    padded = jnp.pad(rimmed, ((0, 0), (0, 0), (1, 1), (1, 1)))
    window = lax.dynamic_slice_in_dim(padded, lax.axis_index("shot") * row_count, row_count + 2, 2)
    return conv_apply(window, conv_weight, conv_bias)


def solution(mesh):
    in_specs = (
        P("shot", "gx", None, None),
        P("shot", "gx", None, None),
        P("shot", "gx", None, None),
        P("shot", "gx", None, None),
        P("gx", None, None),
        P("shot", None),
        P("shot", None, None),
        P("shot", None),
        P("shot", None, None),
        P(),
        P(),
        P(),
    )
    out_specs = P(None, "gx", "shot")
    return jax.shard_map(local, mesh=mesh, in_specs=in_specs, out_specs=out_specs, check_vma=False)
```

profile of v0, /device:TPU:39, one launch (start us, length us, event | category | flops | bytes accessed | tf_op | source)
XLA Modules:
  0.0 508.1 jit_solution(17402110244412481747)
XLA Ops:
  8.8 2.6 collective-permute-start
  11.4 6.6 %collective-permute-start.1 = (f32[2,1,64,128]{3,2,1,0:T(8,128)S(1)}, f32[2,1,64,128]{3,2,1,0:T(8,128)S(1)}, u32[]{:S(2)}, u32[]{:S(2)}) collective-permute-start(f32[2,1,64,128]{3,2,1,0:T(8,128)S(1)} %get-tuple-element.86), channel_id=1, source_target_pairs={{0,1},{1,2},{2,3},{3,4},{4,5},{5,6},{6,7},{7,8},{8,9},{9,10},{10,1... | collective-permute-start | bytes 196616 | tf_op jit(solution)/shard_map/ppermute | solution.py:14
  20.9 4.0 scatter_custom_fusion.1
  25.8 1.9 fusion.10
  29.6 7.3 %collective-permute-start.3 = (f32[2,1,64,128]{3,2,1,0:T(8,128)S(1)}, f32[2,1,64,128]{3,2,1,0:T(8,128)S(1)}, u32[]{:S(2)}, u32[]{:S(2)}) collective-permute-start(f32[2,1,64,128]{3,2,1,0:T(8,128)S(1)} %get-tuple-element.84), channel_id=1, source_target_pairs={{0,1},{1,2},{2,3},{3,4},{4,5},{5,6},{6,7},{7,8},{8,9},{9,10},{10,1... | collective-permute-start | bytes 196616 | tf_op jit(solution)/shard_map/ppermute | solution.py:14
  36.9 4.0 scatter_custom_fusion.3
  45.7 3.5 collective-permute-start.4
  51.2 10.1 %collective-permute-done.4 = f32[4,8,64,128]{3,2,1,0:T(8,128)} collective-permute-done((f32[4,8,64,128]{3,2,1,0:T(8,128)}, f32[4,8,64,128]{3,2,1,0:T(8,128)}, u32[]{:S(2)}, u32[]{:S(2)}) %collective-permute-start.4) | collective-permute-done | bytes 1048608 | tf_op jit(solution)/shard_map/ppermute | solution.py:14
  61.3 7.8 %collective-permute-done.5 = f32[4,8,64,128]{3,2,1,0:T(8,128)} collective-permute-done((f32[4,8,64,128]{3,2,1,0:T(8,128)S(1)}, f32[4,8,64,128]{3,2,1,0:T(8,128)}, u32[]{:S(2)}, u32[]{:S(2)}) %collective-permute-start.5) | collective-permute-done | bytes 1048608 | tf_op jit(solution)/shard_map/ppermute | solution.py:17
  69.1 4.0 pad_maximum_fusion
  73.0 277.4 %while.13 = (s32[]{:T(128)}, f32[9,4,16,32]{3,2,1,0:T(8,128)}, s32[9]{0:T(128)S(1)}, f32[4,32,64,128]{3,2,1,0:T(8,128)}, s32[]{:T(128)}, /*index=5*/s32[]{:T(128...) while((s32[]{:T(128)}, f32[9,4,16,32]{3,2,1,0:T(8,128)}, s32[9]{0:T(128)S(1)}, ...), condition=%wide.region_6.7_spmd, body=%wide.region_4.6_spmd.sunk | while | flops 524301 | bytes 4244249 | solution.py:55
  77.5 18.6 %add.415 = f32[4,4,16,4,32,4]{5,4,3,2,1,0:T(8,128)} reshape(f32[1,16,64,128]{3,2,1,0:T(8,128)S(1)} %fusion.56) | data formatting | bytes 1048576 | tf_op jit(solution)/shard_map/while/body/eval_jaxpr/add | solution.py:52
  96.2 7.1 %reduce_sum.14 = f32[4,16,32]{2,1,0:T(8,128)S(1)} reduce(f32[4,4,16,4,32,4]{5,4,3,2,1,0:T(8,128)} %add.415, f32[]{:T(128)} %constant.122.clone.1..sunk), dimensions={1,3,5}, to_apply=%region_5.5 | reduce | flops 129024 | bytes 532484 | tf_op jit(solution)/shard_map/while/body/eval_jaxpr/reduce_sum | solution.py:44
  108.4 18.6 %add.415 = f32[4,4,16,4,32,4]{5,4,3,2,1,0:T(8,128)} reshape(f32[1,16,64,128]{3,2,1,0:T(8,128)S(1)} %fusion.56) | data formatting | bytes 1048576 | tf_op jit(solution)/shard_map/while/body/eval_jaxpr/add | solution.py:52
  127.0 7.1 %reduce_sum.14 = f32[4,16,32]{2,1,0:T(8,128)S(1)} reduce(f32[4,4,16,4,32,4]{5,4,3,2,1,0:T(8,128)} %add.415, f32[]{:T(128)} %constant.122.clone.1..sunk), dimensions={1,3,5}, to_apply=%region_5.5 | reduce | flops 129024 | bytes 532484 | tf_op jit(solution)/shard_map/while/body/eval_jaxpr/reduce_sum | solution.py:44
  139.2 18.6 %add.415 = f32[4,4,16,4,32,4]{5,4,3,2,1,0:T(8,128)} reshape(f32[1,16,64,128]{3,2,1,0:T(8,128)S(1)} %fusion.56) | data formatting | bytes 1048576 | tf_op jit(solution)/shard_map/while/body/eval_jaxpr/add | solution.py:52
  157.8 7.1 %reduce_sum.14 = f32[4,16,32]{2,1,0:T(8,128)S(1)} reduce(f32[4,4,16,4,32,4]{5,4,3,2,1,0:T(8,128)} %add.415, f32[]{:T(128)} %constant.122.clone.1..sunk), dimensions={1,3,5}, to_apply=%region_5.5 | reduce | flops 129024 | bytes 532484 | tf_op jit(solution)/shard_map/while/body/eval_jaxpr/reduce_sum | solution.py:44
  170.0 18.6 %add.415 = f32[4,4,16,4,32,4]{5,4,3,2,1,0:T(8,128)} reshape(f32[1,16,64,128]{3,2,1,0:T(8,128)S(1)} %fusion.56) | data formatting | bytes 1048576 | tf_op jit(solution)/shard_map/while/body/eval_jaxpr/add | solution.py:52
  188.6 7.1 %reduce_sum.14 = f32[4,16,32]{2,1,0:T(8,128)S(1)} reduce(f32[4,4,16,4,32,4]{5,4,3,2,1,0:T(8,128)} %add.415, f32[]{:T(128)} %constant.122.clone.1..sunk), dimensions={1,3,5}, to_apply=%region_5.5 | reduce | flops 129024 | bytes 532484 | tf_op jit(solution)/shard_map/while/body/eval_jaxpr/reduce_sum | solution.py:44
  200.8 18.6 %add.415 = f32[4,4,16,4,32,4]{5,4,3,2,1,0:T(8,128)} reshape(f32[1,16,64,128]{3,2,1,0:T(8,128)S(1)} %fusion.56) | data formatting | bytes 1048576 | tf_op jit(solution)/shard_map/while/body/eval_jaxpr/add | solution.py:52
  219.5 7.1 %reduce_sum.14 = f32[4,16,32]{2,1,0:T(8,128)S(1)} reduce(f32[4,4,16,4,32,4]{5,4,3,2,1,0:T(8,128)} %add.415, f32[]{:T(128)} %constant.122.clone.1..sunk), dimensions={1,3,5}, to_apply=%region_5.5 | reduce | flops 129024 | bytes 532484 | tf_op jit(solution)/shard_map/while/body/eval_jaxpr/reduce_sum | solution.py:44
  231.6 18.6 %add.415 = f32[4,4,16,4,32,4]{5,4,3,2,1,0:T(8,128)} reshape(f32[1,16,64,128]{3,2,1,0:T(8,128)S(1)} %fusion.56) | data formatting | bytes 1048576 | tf_op jit(solution)/shard_map/while/body/eval_jaxpr/add | solution.py:52
  250.3 7.1 %reduce_sum.14 = f32[4,16,32]{2,1,0:T(8,128)S(1)} reduce(f32[4,4,16,4,32,4]{5,4,3,2,1,0:T(8,128)} %add.415, f32[]{:T(128)} %constant.122.clone.1..sunk), dimensions={1,3,5}, to_apply=%region_5.5 | reduce | flops 129024 | bytes 532484 | tf_op jit(solution)/shard_map/while/body/eval_jaxpr/reduce_sum | solution.py:44
  262.5 18.6 %add.415 = f32[4,4,16,4,32,4]{5,4,3,2,1,0:T(8,128)} reshape(f32[1,16,64,128]{3,2,1,0:T(8,128)S(1)} %fusion.56) | data formatting | bytes 1048576 | tf_op jit(solution)/shard_map/while/body/eval_jaxpr/add | solution.py:52
  281.1 7.1 %reduce_sum.14 = f32[4,16,32]{2,1,0:T(8,128)S(1)} reduce(f32[4,4,16,4,32,4]{5,4,3,2,1,0:T(8,128)} %add.415, f32[]{:T(128)} %constant.122.clone.1..sunk), dimensions={1,3,5}, to_apply=%region_5.5 | reduce | flops 129024 | bytes 532484 | tf_op jit(solution)/shard_map/while/body/eval_jaxpr/reduce_sum | solution.py:44
  293.3 18.6 %add.415 = f32[4,4,16,4,32,4]{5,4,3,2,1,0:T(8,128)} reshape(f32[1,16,64,128]{3,2,1,0:T(8,128)S(1)} %fusion.56) | data formatting | bytes 1048576 | tf_op jit(solution)/shard_map/while/body/eval_jaxpr/add | solution.py:52
  311.9 7.1 %reduce_sum.14 = f32[4,16,32]{2,1,0:T(8,128)S(1)} reduce(f32[4,4,16,4,32,4]{5,4,3,2,1,0:T(8,128)} %add.415, f32[]{:T(128)} %constant.122.clone.1..sunk), dimensions={1,3,5}, to_apply=%region_5.5 | reduce | flops 129024 | bytes 532484 | tf_op jit(solution)/shard_map/while/body/eval_jaxpr/reduce_sum | solution.py:44
  324.1 18.6 %add.415 = f32[4,4,16,4,32,4]{5,4,3,2,1,0:T(8,128)} reshape(f32[1,16,64,128]{3,2,1,0:T(8,128)S(1)} %fusion.56) | data formatting | bytes 1048576 | tf_op jit(solution)/shard_map/while/body/eval_jaxpr/add | solution.py:52
  342.8 7.1 %reduce_sum.14 = f32[4,16,32]{2,1,0:T(8,128)S(1)} reduce(f32[4,4,16,4,32,4]{5,4,3,2,1,0:T(8,128)} %add.415, f32[]{:T(128)} %constant.122.clone.1..sunk), dimensions={1,3,5}, to_apply=%region_5.5 | reduce | flops 129024 | bytes 532484 | tf_op jit(solution)/shard_map/while/body/eval_jaxpr/reduce_sum | solution.py:44
  350.4 121.8 %all-reduce.5.cloned.1.call-done = f32[9,4,16,32]{3,2,1,0:T(8,128)} async-done(((f32[9,4,16,32]{3,2,1,0:T(8,128)}), f32[9,4,16,32]{3,2,1,0:T(8,128)}) %all-reduce.5.cloned.1.call-update) | async-done | bytes 73744 | tf_op jit(solution)/shard_map/psum | solution.py:126
  473.1 14.9 %collective-permute-start.6 = (f32[9,1,16,32]{3,2,1,0:T(8,128)S(1)}, f32[9,1,16,32]{3,2,1,0:T(8,128)S(1)}, u32[]{:S(2)}, u32[]{:S(2)}) collective-permute-start(f32[9,1,16,32]{3,2,1,0:T(8,128)S(1)} %get-tuple-element.88), channel_id=1, source_target_pairs={{0,1},{1,2},{2,3},{3,4},{4,5},{5,6},{6,7},{7,8},{8,9},{9,10},{10,1... | collective-permute-start | bytes 55304 | tf_op jit(solution)/shard_map/ppermute | solution.py:14
  490.2 7.2 %collective-permute-done.7 = f32[9,1,16,32]{3,2,1,0:T(8,128)S(1)} collective-permute-done((f32[9,1,16,32]{3,2,1,0:T(8,128)S(1)}, f32[9,1,16,32]{3,2,1,0:T(8,128)S(1)}, u32[]{:S(2)}, u32[]{:S(2)}) %collective-permute-start.7) | collective-permute-done | bytes 18464 | tf_op jit(solution)/shard_map/ppermute | solution.py:17
  (99 shorter events, 47.0 us)
Async XLA Ops:
  6.5 19.2 %copy-start = (f32[16,64,128]{2,1,0:T(8,128)S(1)}, f32[16,64,128]{2,1,0:T(8,128)}, u32[]{:S(2)}) copy-start(f32[16,64,128]{2,1,0:T(8,128)} %param.18) | copy-start | bytes 1572868
  6.5 465.7 %all-reduce.5.cloned.1.call-start = ((), (), s32[]{:S(2)}) async-start(), calls=%async_computation | async-start | bytes 589824 | tf_op jit(solution)/shard_map/psum | solution.py:126
  8.8 16.9 %collective-permute-start = (f32[2,1,64,128]{3,2,1,0:T(8,128)S(1)}, f32[2,1,64,128]{3,2,1,0:T(8,128)S(1)}, u32[]{:S(2)}, u32[]{:S(2)}) collective-permute-start(f32[2,1,64,128]{3,2,1,0:T(8,128)S(1)} %get-tuple-element.85), channel_id=1, source_target_pairs={{1,0},{2,1},{3,2},{4,3},{5,4},{6,5},{7,6},{8,7},{9,8},{10,9},{11,1... | collective-permute-start | bytes 196616 | tf_op jit(solution)/shard_map/ppermute | solution.py:17
  11.4 14.4 %collective-permute-start.1 = (f32[2,1,64,128]{3,2,1,0:T(8,128)S(1)}, f32[2,1,64,128]{3,2,1,0:T(8,128)S(1)}, u32[]{:S(2)}, u32[]{:S(2)}) collective-permute-start(f32[2,1,64,128]{3,2,1,0:T(8,128)S(1)} %get-tuple-element.86), channel_id=1, source_target_pairs={{0,1},{1,2},{2,3},{3,4},{4,5},{5,6},{6,7},{7,8},{8,9},{9,10},{10,1... | collective-permute-start | bytes 196616 | tf_op jit(solution)/shard_map/ppermute | solution.py:14
  27.7 14.8 %collective-permute-start.2 = (f32[2,1,64,128]{3,2,1,0:T(8,128)S(1)}, f32[2,1,64,128]{3,2,1,0:T(8,128)S(1)}, u32[]{:S(2)}, u32[]{:S(2)}) collective-permute-start(f32[2,1,64,128]{3,2,1,0:T(8,128)S(1)} %get-tuple-element.83), channel_id=1, source_target_pairs={{1,0},{2,1},{3,2},{4,3},{5,4},{6,5},{7,6},{8,7},{9,8},{10,9},{11,1... | collective-permute-start | bytes 196616 | tf_op jit(solution)/shard_map/ppermute | solution.py:17
  29.6 12.9 %collective-permute-start.3 = (f32[2,1,64,128]{3,2,1,0:T(8,128)S(1)}, f32[2,1,64,128]{3,2,1,0:T(8,128)S(1)}, u32[]{:S(2)}, u32[]{:S(2)}) collective-permute-start(f32[2,1,64,128]{3,2,1,0:T(8,128)S(1)} %get-tuple-element.84), channel_id=1, source_target_pairs={{0,1},{1,2},{2,3},{3,4},{4,5},{5,6},{6,7},{7,8},{8,9},{9,10},{10,1... | collective-permute-start | bytes 196616 | tf_op jit(solution)/shard_map/ppermute | solution.py:14
  45.7 15.6 %collective-permute-start.4 = (f32[4,8,64,128]{3,2,1,0:T(8,128)}, f32[4,8,64,128]{3,2,1,0:T(8,128)}, u32[]{:S(2)}, u32[]{:S(2)}) collective-permute-start(f32[4,8,64,128]{3,2,1,0:T(8,128)} %get-tuple-element.81), channel_id=1, source_target_pairs={{0,1},{1,2},{2,3},{3,4},{4,5},{5,6},{6,7},{7,8},{8,9},{9,10},{10,1... | collective-permute-start | bytes 3145736 | tf_op jit(solution)/shard_map/ppermute | solution.py:14
  49.2 19.8 %collective-permute-start.5 = (f32[4,8,64,128]{3,2,1,0:T(8,128)S(1)}, f32[4,8,64,128]{3,2,1,0:T(8,128)}, u32[]{:S(2)}, u32[]{:S(2)}) collective-permute-start(f32[4,8,64,128]{3,2,1,0:T(8,128)S(1)} %get-tuple-element.82), channel_id=1, source_target_pairs={{1,0},{2,1},{3,2},{4,3},{5,4},{6,5},{7,6},{8,7},{9,8},{10,9},{11,1... | collective-permute-start | bytes 3145736 | tf_op jit(solution)/shard_map/ppermute | solution.py:17
  51.2 21.9 %copy-start.3 = (s32[9]{0:T(128)S(1)}, s32[9]{0:T(128)}, u32[]{:S(2)}) copy-start(s32[9]{0:T(128)} %param.23) | copy-start | bytes 112
  73.0 417.1 %copy-start.1 = (f32[64,9,3,3,3]{0,4,3,2,1:T(4,128)S(1)}, f32[64,9,3,3,3]{0,4,3,2,1:T(4,128)}, u32[]{:S(2)}) copy-start(f32[64,9,3,3,3]{0,4,3,2,1:T(4,128)} %param.24) | copy-start | bytes 186628
  350.4 149.7 %copy-start.2 = (f32[64]{0:T(128)S(1)}, f32[64]{0:T(128)}, u32[]{:S(2)}) copy-start(f32[64]{0:T(128)} %param.25) | copy-start | bytes 772
  473.1 17.0 %collective-permute-start.6 = (f32[9,1,16,32]{3,2,1,0:T(8,128)S(1)}, f32[9,1,16,32]{3,2,1,0:T(8,128)S(1)}, u32[]{:S(2)}, u32[]{:S(2)}) collective-permute-start(f32[9,1,16,32]{3,2,1,0:T(8,128)S(1)} %get-tuple-element.88), channel_id=1, source_target_pairs={{0,1},{1,2},{2,3},{3,4},{4,5},{5,6},{6,7},{7,8},{8,9},{9,10},{10,1... | collective-permute-start | bytes 55304 | tf_op jit(solution)/shard_map/ppermute | solution.py:14
  488.1 9.3 %collective-permute-start.7 = (f32[9,1,16,32]{3,2,1,0:T(8,128)S(1)}, f32[9,1,16,32]{3,2,1,0:T(8,128)S(1)}, u32[]{:S(2)}, u32[]{:S(2)}) collective-permute-start(f32[9,1,16,32]{3,2,1,0:T(8,128)S(1)} %get-tuple-element.87), channel_id=1, source_target_pairs={{1,0},{2,1},{3,2},{4,3},{5,4},{6,5},{7,6},{8,7},{9,8},{10,9},{11,1... | collective-permute-start | bytes 55304 | tf_op jit(solution)/shard_map/ppermute | solution.py:17
Sparse Core Ops, SparseCore 0:
  350.6 121.5 all-reduce.4
where the time goes:
time: 512 us; the launch traced here: 508 us
  local copies, waits for them, and re-layouts  181 us (35%)
  waiting for transfers between devices  147 us (29%)
  other arithmetic  105 us (21%)
  starting transfers between devices  40.7 us (8%)
  loops' own time  20.3 us (4%)
  between operations  13.8 us (3%)
    add x9, local copies, waits for them, and re-layouts, per_offset(): forward_part[0] * backward_part[1] + forward_part[2] * backward_part[3]  168 us
    psum x1, waiting for transfers between devices, local(): summed = lax.psum(coarse, 'shot')  122 us
    reduce_sum x9, other arithmetic, coarsen(): image_block.reshape(size_x // 4, 4, size_y // 4, 4, size_z // 4, 4)  63.6 us
    ppermute x4, starting transfers between devices, padded_2(): lax.ppermute(lax.slice_in_dim(block, block.shape[dim] - width, None, axis...  32.3 us
    another operation x1, loops' own time, offset_image(): return lax.map(per_offset, offsets)  20.3 us
    add x9, other arithmetic, per_offset(): forward_part[0] * backward_part[1] + forward_part[2] * backward_part[3]  15.1 us
    ppermute x4, waiting for transfers between devices, padded_2(): lax.ppermute(lax.slice_in_dim(block, 0, width, axis=dim), axis, backward)  15 us
  transfers between devices with their start and end apart: 9, of which 4 were waited for; matrix products, arithmetic and copies ran while one was open for 3% of the time, Pallas kernels for 0%

commit v1 on v0

--- a/solution.py
+++ b/solution.py
@@ -39,20 +39,29 @@
     return 2.0 * center - previous + courant * laplace + sources
 
 
-def coarsen(image_block):
-    size_x, size_y, size_z = image_block.shape
-    return image_block.reshape(size_x // 4, 4, size_y // 4, 4, size_z // 4, 4).mean(axis=(1, 3, 5))
+def pooling(size, group):
+    fine = jnp.arange(size)[:, None] // group
+    coarse = jnp.arange(size // group)[None, :]
+    return (fine == coarse).astype(jnp.float32)
 
 
 def offset_image(wide, offsets, margin, cells_x):
-
-    def per_offset(offset_value):
+    _, _, size_y, size_z = wide.shape
+    parts = []
+    for index in range(offsets.shape[0]):
+        offset_value = offsets[index]
         forward_part = lax.dynamic_slice_in_dim(wide, margin + offset_value, cells_x, 1)
         backward_part = lax.dynamic_slice_in_dim(wide, margin - offset_value, cells_x, 1)
         image_block = forward_part[0] * backward_part[1] + forward_part[2] * backward_part[3]
-        return coarsen(image_block)
-
-    return lax.map(per_offset, offsets)
+        parts.append(image_block.reshape(cells_x // 4, 4, size_y, size_z).sum(axis=1))
+    pooled_x = jnp.stack(parts)
+    pooled_z = jnp.einsum(
+        "ixyz,zc->ixyc", pooled_x, pooling(size_z, 4), precision=lax.Precision.HIGHEST
+    )
+    pooled = jnp.einsum(
+        "yb,ixyc->ixbc", pooling(size_y, 4), pooled_z, precision=lax.Precision.HIGHEST
+    )
+    return pooled * (1.0 / 64.0)
 
 
 def conv_apply(padded, conv_weight, conv_bias):
@@ -74,6 +83,17 @@
     )
     result = result + conv_bias[:, None]
     return result.reshape(conv_weight.shape[0], size_x, size_y * size_z)
+
+
+def group_sum_windows(coarse, axis):
+    count = lax.axis_size(axis)
+    rows = coarse.shape[2] // count
+    rimmed = jnp.pad(coarse, ((0, 0), (0, 0), (1, 1), (0, 0)))
+    windows = jnp.stack(
+        [lax.slice_in_dim(rimmed, member * rows, member * rows + rows + 2, axis=2) for member in range(count)]
+    )
+    received = lax.all_to_all(windows, axis, 0, 0, tiled=True)
+    return received.sum(axis=0)
 
 
 def local(
@@ -123,11 +143,9 @@
     fields = jnp.concatenate(levels, axis=0)
     wide = padded_2(fields, (("gx", 1),), HMAX)
     coarse = offset_image(wide, offsets, HMAX, cells_x)
-    summed = lax.psum(coarse, "shot")
+    summed = group_sum_windows(coarse, "shot")
     rimmed = padded_2(summed, (("gx", 1),), 1)
-    row_count = summed.shape[2] // lax.axis_size("shot")
-    padded = jnp.pad(rimmed, ((0, 0), (0, 0), (1, 1), (1, 1)))
-    window = lax.dynamic_slice_in_dim(padded, lax.axis_index("shot") * row_count, row_count + 2, 2)
+    window = jnp.pad(rimmed, ((0, 0), (0, 0), (0, 0), (1, 1)))
     return conv_apply(window, conv_weight, conv_bias)
 
 

time: 512 us -> 120 us (0.23)
  the two profiles are of different devices: /device:TPU:39 before, /device:TPU:56 now
where the time goes in v1:
time: 120 us; the launch traced here: 119 us
  starting transfers between devices  37 us (31%)
  other arithmetic  28 us (23%)
  between operations  22.4 us (19%)
  waiting for transfers between devices  18.6 us (16%)
  local copies, waits for them, and re-layouts  10.1 us (8%)
  matrix products  3.35 us (3%)
    ppermute x4, starting transfers between devices, padded_2(): lax.ppermute(lax.slice_in_dim(block, 0, width, axis=dim), axis, backward)  19.5 us
    ppermute x4, waiting for transfers between devices, padded_2(): lax.ppermute(lax.slice_in_dim(block, block.shape[dim] - width, None, axis...  10.2 us
    scatter-add x4, other arithmetic, inject(): jnp.zeros((cells_here * plane_size + 1,), jnp.float32).at[target]  9.51 us
    all_to_all x1, starting transfers between devices, group_sum_windows(): received = lax.all_to_all(windows, axis, 0, 0, tiled=True)  9.51 us
    all_to_all x1, waiting for transfers between devices, group_sum_windows(): received = lax.all_to_all(windows, axis, 0, 0, tiled=True)  8.36 us
    ppermute x4, starting transfers between devices, padded_2(): lax.ppermute(lax.slice_in_dim(block, block.shape[dim] - width, None, axis...  8 us
    add x2, other arithmetic, offset_image(): forward_part[0] * backward_part[1] + forward_part[2] * backward_part[3]  6.44 us
    unnamed x80, local copies, waits for them, and re-layouts  6.39 us
  transfers between devices with their start and end apart: 9, of which 4 were waited for; matrix products, arithmetic and copies ran while one was open for 9% of the time, Pallas kernels for 0%

profile of v1, /device:TPU:56, one launch (start us, length us, event | category | flops | bytes accessed | tf_op | source)
XLA Modules:
  0.0 119.4 jit_solution(5052953134817718465)
XLA Ops:
  0.0 1.1 constant_dynamic-update-slice_fusion.1
  1.3 4.8 %collective-permute-start = (f32[2,1,64,128]{3,2,1,0:T(8,128)S(1)}, f32[2,1,64,128]{3,2,1,0:T(8,128)S(1)}, u32[]{:S(2)}, u32[]{:S(2)}) collective-permute-start(f32[2,1,64,128]{3,2,1,0:T(8,128)S(1)} %get-tuple-element.18), channel_id=1, source_target_pairs={{1,0},{2,1},{3,2},{4,3},{5,4},{6,5},{7,6},{8,7},{9,8},{10,9},{11,1... | collective-permute-start | bytes 196616 | tf_op jit(solution)/shard_map/ppermute | solution.py:17
  6.0 1.9 %collective-permute-start.1 = (f32[2,1,64,128]{3,2,1,0:T(8,128)S(1)}, f32[2,1,64,128]{3,2,1,0:T(8,128)S(1)}, u32[]{:S(2)}, u32[]{:S(2)}) collective-permute-start(f32[2,1,64,128]{3,2,1,0:T(8,128)S(1)} %get-tuple-element.19), channel_id=1, source_target_pairs={{0,1},{1,2},{2,3},{3,4},{4,5},{5,6},{6,7},{7,8},{8,9},{9,10},{10,1... | collective-permute-start | bytes 196616 | tf_op jit(solution)/shard_map/ppermute | solution.py:14
  8.1 4.0 %scatter_custom_fusion.1 = f32[131073]{0:T(1024)S(1)} fusion(s32[512]{0:T(512)S(1)} %bitcast.318, f32[512]{0:T(512)S(1)} %bitcast.321, f32[]{:T(128)} %constant.150.clone.1), kind=kCustom, calls=%fused_computation.77 | custom fusion | flops 512 | bytes 524296 | tf_op jit(solution)/shard_map/scatter-add | solution.py:29
  12.2 0.7 scatter_custom_fusion
  13.0 2.3 %collective-permute-done.1 = f32[2,1,64,128]{3,2,1,0:T(8,128)S(1)} collective-permute-done((f32[2,1,64,128]{3,2,1,0:T(8,128)S(1)}, f32[2,1,64,128]{3,2,1,0:T(8,128)S(1)}, u32[]{:S(2)}, u32[]{:S(2)}) %collective-permute-start.1) | collective-permute-done | bytes 65568 | tf_op jit(solution)/shard_map/ppermute | solution.py:14
  15.2 1.9 %fusion.10 = f32[2,16,64,128]{3,2,1,0:T(8,128)S(1)} fusion(f32[2,16,64,128]{3,2,1,0:T(8,128)S(1)} %constant_dynamic-update-slice_fusion, f32[2,1,64,128]{3,2,1,0:T(8,128)S(1)} %collective-permute-done.1, f32[2,1,64,128]{3,2,1,0:T(8,128)S(1)} %collective-permute-done, f32[1,16,64,128]{3,2,1,0:T(8,128)} %param.14, f32[1,16,64,128]{3,2,1,0:T(8,128)} %param.12, ...), kind=kLoop, calls=%fused_computation.27 | loop fusion | flops 4194304 | bytes 4849664 | tf_op jit(solution)/shard_map/add | solution.py:39
  17.2 5.2 %collective-permute-start.2 = (f32[2,1,64,128]{3,2,1,0:T(8,128)S(1)}, f32[2,1,64,128]{3,2,1,0:T(8,128)S(1)}, u32[]{:S(2)}, u32[]{:S(2)}) collective-permute-start(f32[2,1,64,128]{3,2,1,0:T(8,128)S(1)} %get-tuple-element.16), channel_id=1, source_target_pairs={{1,0},{2,1},{3,2},{4,3},{5,4},{6,5},{7,6},{8,7},{9,8},{10,9},{11,1... | collective-permute-start | bytes 196616 | tf_op jit(solution)/shard_map/ppermute | solution.py:17
  22.4 1.9 %collective-permute-start.3 = (f32[2,1,64,128]{3,2,1,0:T(8,128)S(1)}, f32[2,1,64,128]{3,2,1,0:T(8,128)S(1)}, u32[]{:S(2)}, u32[]{:S(2)}) collective-permute-start(f32[2,1,64,128]{3,2,1,0:T(8,128)S(1)} %get-tuple-element.17), channel_id=1, source_target_pairs={{0,1},{1,2},{2,3},{3,4},{4,5},{5,6},{6,7},{7,8},{8,9},{9,10},{10,1... | collective-permute-start | bytes 196616 | tf_op jit(solution)/shard_map/ppermute | solution.py:14
  24.3 4.0 %scatter_custom_fusion.3 = f32[131073]{0:T(1024)S(1)} fusion(s32[512]{0:T(512)S(1)} %bitcast.319, f32[512]{0:T(512)S(1)} %bitcast.320, f32[]{:T(128)} %constant.150.clone.1), kind=kCustom, calls=%fused_computation.73 | custom fusion | flops 512 | bytes 524296 | tf_op jit(solution)/shard_map/scatter-add | solution.py:29
  28.3 0.8 slice.507
  29.2 0.7 scatter_custom_fusion.2
  30.0 1.6 %collective-permute-done.3 = f32[2,1,64,128]{3,2,1,0:T(8,128)S(1)} collective-permute-done((f32[2,1,64,128]{3,2,1,0:T(8,128)S(1)}, f32[2,1,64,128]{3,2,1,0:T(8,128)S(1)}, u32[]{:S(2)}, u32[]{:S(2)}) %collective-permute-start.3) | collective-permute-done | bytes 65568 | tf_op jit(solution)/shard_map/ppermute | solution.py:14
  31.6 1.8 %fusion.18 = f32[2,16,64,128]{3,2,1,0:T(8,128)S(1)} fusion(f32[2,16,64,128]{3,2,1,0:T(8,128)S(1)} %fusion.10, f32[2,1,64,128]{3,2,1,0:T(8,128)S(1)} %collective-permute-done.3, f32[2,1,64,128]{3,2,1,0:T(8,128)S(1)} %collective-permute-done.2, f32[1,16,64,128]{3,2,1,0:T(8,128)S(1)} %bitcast.309, f32[1,16,64,128]{3,2,1,0:T(8,128)S(1)} %bitcast.311, ...), kind=kLoop, calls=%fused_computation.35 | loop fusion | flops 3932160 | bytes 4849664 | tf_op jit(solution)/shard_map/add | solution.py:39
  33.4 1.2 fusion.2
  34.6 1.9 %collective-permute-start.4 = (f32[4,8,64,128]{3,2,1,0:T(8,128)}, f32[4,8,64,128]{3,2,1,0:T(8,128)}, u32[]{:S(2)}, u32[]{:S(2)}) collective-permute-start(f32[4,8,64,128]{3,2,1,0:T(8,128)} %get-tuple-element.14), channel_id=1, source_target_pairs={{0,1},{1,2},{2,3},{3,4},{4,5},{5,6},{6,7},{7,8},{8,9},{9,10},{10,1... | collective-permute-start | bytes 3145736 | tf_op jit(solution)/shard_map/ppermute | solution.py:14
  36.5 7.4 %collective-permute-start.5 = (f32[4,8,64,128]{3,2,1,0:T(8,128)S(1)}, f32[4,8,64,128]{3,2,1,0:T(8,128)}, u32[]{:S(2)}, u32[]{:S(2)}) collective-permute-start(f32[4,8,64,128]{3,2,1,0:T(8,128)S(1)} %get-tuple-element.15), channel_id=1, source_target_pairs={{1,0},{2,1},{3,2},{4,3},{5,4},{6,5},{7,6},{8,7},{9,8},{10,9},{11,1... | collective-permute-start | bytes 3145736 | tf_op jit(solution)/shard_map/ppermute | solution.py:17
  66.3 1.9 %pad_maximum_fusion = f32[4,32,64,128]{3,2,1,0:T(8,128)S(1)} fusion(f32[4,8,64,128]{3,2,1,0:T(8,128)} %collective-permute-done.5, f32[2,16,64,128]{3,2,1,0:T(8,128)S(1)} %fusion.18, f32[2,16,64,128]{3,2,1,0:T(8,128)S(1)} %fusion.10, f32[4,8,64,128]{3,2,1,0:T(8,128)} %collective-permute-done.4), kind=kLoop, calls=%fused_computation.4 | loop fusion | flops 3145728 | bytes 8388608 | tf_op jit(solution)/shard_map/concatenate | solution.py:18
  68.1 2.8 %fusion.21 = (f32[1,16,64,128]{3,2,1,0:T(8,128)S(1)}, f32[1,16,64,128]{3,2,1,0:T(8,128)S(1)}, f32[1,16,64,128]{3,2,1,0:T(8,128)S(1)}, f32[1,16,64,128]{3,2,1,0:T...) fusion(f32[4,32,64,128]{3,2,1,0:T(8,128)S(1)} %pad_maximum_fusion, ...), kind=kLoop, calls=%fused_computation.45 | loop fusion | flops 2752512 | bytes 18350148 | tf_op jit(solution)/shard_map/add | solution.py:55
  70.9 1.1 reduce_sum.91
  72.0 3.6 %fusion.24 = (f32[1,16,64,128]{3,2,1,0:T(8,128)}, f32[1,16,64,128]{3,2,1,0:T(8,128)}) fusion(f32[4,32,64,128]{3,2,1,0:T(8,128)} %copy-done, s32[]{:T(128)S(6)} %add.547, s32[]{:T(128)S(6)} %select_n.196, s32[]{:T(128)S(6)} %add.546, s32[]{:T(128)S(6)} %select_n.195, s32[]{:T(128)S(6)} %add.545, s32[]{:T(128)S(6)} %select_n.186, s32[]{:T(128)S(6)} %select_n.185), kind=kLoop, calls=%fused_computation.54 | loop fusion | flops 786432 | bytes 5242908 | tf_op jit(solution)/shard_map/add | solution.py:55
  75.7 1.1 reduce_sum.90
  79.4 1.1 copy-done.4
  80.6 1.7 %fusion.43 = f32[9,4,64,32]{2,3,1,0:T(8,128)S(1)} fusion(f32[9,4,64,128]{3,2,1,0:T(8,128)S(1)} %bitcast_dynamic-update-slice_fusion, s32[128]{0:T(128)S(1)} %and_select_fusion.4), kind=kOutput, calls=%fused_computation.185 | convolution fusion | flops 113250304 | bytes 1475072 | tf_op jit(solution)/shard_map/ixyz,zc->ixyc/dot_general | solution.py:58
  82.4 1.3 %fusion = f32[9,4,16,32]{3,2,1,0:T(8,128)S(1)} fusion(f32[9,4,64,32]{2,3,1,0:T(8,128)S(1)} %fusion.43, s32[64]{0:T(128)S(1)} %and_select_fusion.3), kind=kOutput, calls=%fused_computation.16 | convolution fusion | flops 14175232 | bytes 368896 | tf_op jit(solution)/shard_map/yb,ixyc->ixbc/dot_general | solution.py:61
  84.4 1.2 %reshape.524 = f32[16,1,3456]{2,1,0:T(1,128)} reshape(f32[16,9,3,4,32]{4,3,2,1,0:T(4,128)S(1)} %bitcast.301) | data formatting | bytes 442368
  85.6 9.5 %all-to-all-start = ((f32[16,1,3456]{2,1,0:T(1,128)}), f32[16,1,3456]{2,1,0:T(1,128)S(1)}, u32[]{:S(2)}, u32[]{:S(2)}) async-start(f32[16,1,3456]{2,1,0:T(1,128)} %reshape.524), calls=%async_computation | async-start | bytes 442368 | tf_op jit(solution)/shard_map/all_to_all | solution.py:95
  95.2 8.4 %all-to-all-done = f32[16,1,3456]{2,1,0:T(1,128)S(1)} async-done(((f32[16,1,3456]{2,1,0:T(1,128)}), f32[16,1,3456]{2,1,0:T(1,128)S(1)}, u32[]{:S(2)}, u32[]{:S(2)}) %all-to-all-start) | async-done | bytes 221216 | tf_op jit(solution)/shard_map/all_to_all | solution.py:95
  104.1 1.2 reduce
  105.9 2.1 %collective-permute-start.7 = (f32[9,1,3,32]{3,1,0,2:T(1,128)S(1)}, f32[9,1,3,32]{3,1,0,2:T(1,128)S(1)}, u32[]{:S(2)}, u32[]{:S(2)}) collective-permute-start(f32[9,1,3,32]{3,1,0,2:T(1,128)S(1)} %get-tuple-element.24), channel_id=1, source_target_pairs={{1,0},{2,1},{3,2},{4,3},{5,4},{6,5},{7,6},{8,7},{9,8},{10,9},{11,1... | collective-permute-start | bytes 10376 | tf_op jit(solution)/shard_map/ppermute | solution.py:17
  108.0 2.3 %collective-permute-start.6 = (f32[9,1,3,32]{3,1,0,2:T(1,128)S(1)}, f32[9,1,3,32]{3,1,0,2:T(1,128)S(1)}, u32[]{:S(2)}, u32[]{:S(2)}) collective-permute-start(f32[9,1,3,32]{3,1,0,2:T(1,128)S(1)} %get-tuple-element.23), channel_id=1, source_target_pairs={{0,1},{1,2},{2,3},{3,4},{4,5},{5,6},{6,7},{7,8},{8,9},{9,10},{10,1... | collective-permute-start | bytes 10376 | tf_op jit(solution)/shard_map/ppermute | solution.py:14
  110.3 6.3 %collective-permute-done.6 = f32[9,1,3,32]{3,1,0,2:T(1,128)S(1)} collective-permute-done((f32[9,1,3,32]{3,1,0,2:T(1,128)S(1)}, f32[9,1,3,32]{3,1,0,2:T(1,128)S(1)}, u32[]{:S(2)}, u32[]{:S(2)}) %collective-permute-start.6) | collective-permute-done | bytes 3488 | tf_op jit(solution)/shard_map/ppermute | solution.py:14
  (120 shorter events, 8.1 us)
Async XLA Ops:
  0.0 1.2 %copy-start.5 = (f32[1,16,64,128]{3,2,1,0:T(8,128)S(1)}, f32[1,16,64,128]{3,2,1,0:T(8,128)}, u32[]{:S(2)}) copy-start(f32[1,16,64,128]{3,2,1,0:T(8,128)} %param.15) | copy-start | bytes 1572868
  0.0 8.0 %copy-start.10 = (f32[1,2,512]{2,1,0:T(2,128)S(1)}, f32[1,2,512]{2,1,0:T(2,128)}, u32[]{:S(2)}) copy-start(f32[1,2,512]{2,1,0:T(2,128)} %param.20) | copy-start | bytes 12292
  0.0 8.0 %copy-start.12 = (f32[1,2,8]{2,1,0:T(2,128)S(1)}, f32[1,2,8]{2,1,0:T(2,128)}, u32[]{:S(2)}) copy-start(f32[1,2,8]{2,1,0:T(2,128)} %param.18) | copy-start | bytes 196
  0.0 8.0 %copy-start.11 = (s32[1,512]{1,0:T(1,128)S(1)}, s32[1,512]{1,0:T(1,128)}, u32[]{:S(2)}) copy-start(s32[1,512]{1,0:T(1,128)} %param.19) | copy-start | bytes 6148
  0.0 8.0 %copy-start.14 = (s32[1,8]{1,0:T(1,128)S(1)}, s32[1,8]{1,0:T(1,128)}, u32[]{:S(2)}) copy-start(s32[1,8]{1,0:T(1,128)} %param.17) | copy-start | bytes 100
  1.3 11.7 %collective-permute-start = (f32[2,1,64,128]{3,2,1,0:T(8,128)S(1)}, f32[2,1,64,128]{3,2,1,0:T(8,128)S(1)}, u32[]{:S(2)}, u32[]{:S(2)}) collective-permute-start(f32[2,1,64,128]{3,2,1,0:T(8,128)S(1)} %get-tuple-element.18), channel_id=1, source_target_pairs={{1,0},{2,1},{3,2},{4,3},{5,4},{6,5},{7,6},{8,7},{9,8},{10,9},{11,1... | collective-permute-start | bytes 196616 | tf_op jit(solution)/shard_map/ppermute | solution.py:17
  6.0 9.2 %collective-permute-start.1 = (f32[2,1,64,128]{3,2,1,0:T(8,128)S(1)}, f32[2,1,64,128]{3,2,1,0:T(8,128)S(1)}, u32[]{:S(2)}, u32[]{:S(2)}) collective-permute-start(f32[2,1,64,128]{3,2,1,0:T(8,128)S(1)} %get-tuple-element.19), channel_id=1, source_target_pairs={{0,1},{1,2},{2,3},{3,4},{4,5},{5,6},{6,7},{7,8},{8,9},{9,10},{10,1... | collective-permute-start | bytes 196616 | tf_op jit(solution)/shard_map/ppermute | solution.py:14
  12.1 3.1 %copy-start.1 = (f32[16,64,128]{2,1,0:T(8,128)S(1)}, f32[16,64,128]{2,1,0:T(8,128)}, u32[]{:S(2)}) copy-start(f32[16,64,128]{2,1,0:T(8,128)} %param.16) | copy-start | bytes 1572868
  17.2 12.8 %collective-permute-start.2 = (f32[2,1,64,128]{3,2,1,0:T(8,128)S(1)}, f32[2,1,64,128]{3,2,1,0:T(8,128)S(1)}, u32[]{:S(2)}, u32[]{:S(2)}) collective-permute-start(f32[2,1,64,128]{3,2,1,0:T(8,128)S(1)} %get-tuple-element.16), channel_id=1, source_target_pairs={{1,0},{2,1},{3,2},{4,3},{5,4},{6,5},{7,6},{8,7},{9,8},{10,9},{11,1... | collective-permute-start | bytes 196616 | tf_op jit(solution)/shard_map/ppermute | solution.py:17
  22.4 9.2 %collective-permute-start.3 = (f32[2,1,64,128]{3,2,1,0:T(8,128)S(1)}, f32[2,1,64,128]{3,2,1,0:T(8,128)S(1)}, u32[]{:S(2)}, u32[]{:S(2)}) collective-permute-start(f32[2,1,64,128]{3,2,1,0:T(8,128)S(1)} %get-tuple-element.17), channel_id=1, source_target_pairs={{0,1},{1,2},{2,3},{3,4},{4,5},{5,6},{6,7},{7,8},{8,9},{9,10},{10,1... | collective-permute-start | bytes 196616 | tf_op jit(solution)/shard_map/ppermute | solution.py:14
  29.9 1.7 %copy-start.2 = (f32[131072]{0:T(1024)S(1)}, f32[131072]{0:T(1024)}, u32[]{:S(2)}) copy-start(f32[131072]{0:T(1024)} %slice.507) | copy-start | bytes 1572868
  33.4 10.6 %copy-start.9 = (s32[9]{0:T(128)S(1)}, s32[9]{0:T(128)}, u32[]{:S(2)}) copy-start(s32[9]{0:T(128)} %param.21) | copy-start | bytes 112
  34.6 31.7 %collective-permute-start.4 = (f32[4,8,64,128]{3,2,1,0:T(8,128)}, f32[4,8,64,128]{3,2,1,0:T(8,128)}, u32[]{:S(2)}, u32[]{:S(2)}) collective-permute-start(f32[4,8,64,128]{3,2,1,0:T(8,128)} %get-tuple-element.14), channel_id=1, source_target_pairs={{0,1},{1,2},{2,3},{3,4},{4,5},{5,6},{6,7},{7,8},{8,9},{9,10},{10,1... | collective-permute-start | bytes 3145736 | tf_op jit(solution)/shard_map/ppermute | solution.py:14
  36.5 29.8 %collective-permute-start.5 = (f32[4,8,64,128]{3,2,1,0:T(8,128)S(1)}, f32[4,8,64,128]{3,2,1,0:T(8,128)}, u32[]{:S(2)}, u32[]{:S(2)}) collective-permute-start(f32[4,8,64,128]{3,2,1,0:T(8,128)S(1)} %get-tuple-element.15), channel_id=1, source_target_pairs={{1,0},{2,1},{3,2},{4,3},{5,4},{6,5},{7,6},{8,7},{9,8},{10,9},{11,1... | collective-permute-start | bytes 3145736 | tf_op jit(solution)/shard_map/ppermute | solution.py:17
  68.1 2.8 %copy-start = (f32[4,32,64,128]{3,2,1,0:T(8,128)}, f32[4,32,64,128]{3,2,1,0:T(8,128)S(1)}, u32[]{:S(2)}) copy-start(f32[4,32,64,128]{3,2,1,0:T(8,128)S(1)} %pad_maximum_fusion) | copy-start | bytes 12582916
  78.1 1.1 copy-start.3
  79.2 1.3 %copy-start.4 = (f32[9,4,64,128]{3,2,1,0:T(8,128)S(1)}, f32[9,4,64,128]{3,2,1,0:T(8,128)}, u32[]{:S(2)}) copy-start(f32[9,4,64,128]{3,2,1,0:T(8,128)} %bitcast_dynamic-update-slice_fusion.8) | copy-start | bytes 3538948
  79.2 1.3 %copy-start.7 = (f32[4,64,128]{2,1,0:T(8,128)S(1)}, f32[4,64,128]{2,1,0:T(8,128)}, u32[]{:S(2)}) copy-start(f32[4,64,128]{2,1,0:T(8,128)} %reduce_sum.92) | copy-start | bytes 393220
  79.2 1.3 %copy-start.6 = (f32[4,64,128]{2,1,0:T(8,128)S(1)}, f32[4,64,128]{2,1,0:T(8,128)}, u32[]{:S(2)}) copy-start(f32[4,64,128]{2,1,0:T(8,128)} %reduce_sum.93) | copy-start | bytes 393220
  84.4 10.8 %copy-start.8 = (f32[64,9,3,3,3]{0,4,3,2,1:T(4,128)S(1)}, f32[64,9,3,3,3]{0,4,3,2,1:T(4,128)}, u32[]{:S(2)}) copy-start(f32[64,9,3,3,3]{0,4,3,2,1:T(4,128)} %param.22) | copy-start | bytes 186628
  85.6 17.9 %all-to-all-start = ((f32[16,1,3456]{2,1,0:T(1,128)}), f32[16,1,3456]{2,1,0:T(1,128)S(1)}, u32[]{:S(2)}, u32[]{:S(2)}) async-start(f32[16,1,3456]{2,1,0:T(1,128)} %reshape.524), calls=%async_computation | async-start | bytes 442368 | tf_op jit(solution)/shard_map/all_to_all | solution.py:95
  105.9 4.4 %collective-permute-start.7 = (f32[9,1,3,32]{3,1,0,2:T(1,128)S(1)}, f32[9,1,3,32]{3,1,0,2:T(1,128)S(1)}, u32[]{:S(2)}, u32[]{:S(2)}) collective-permute-start(f32[9,1,3,32]{3,1,0,2:T(1,128)S(1)} %get-tuple-element.24), channel_id=1, source_target_pairs={{1,0},{2,1},{3,2},{4,3},{5,4},{6,5},{7,6},{8,7},{9,8},{10,9},{11,1... | collective-permute-start | bytes 10376 | tf_op jit(solution)/shard_map/ppermute | solution.py:17
  108.0 8.6 %collective-permute-start.6 = (f32[9,1,3,32]{3,1,0,2:T(1,128)S(1)}, f32[9,1,3,32]{3,1,0,2:T(1,128)S(1)}, u32[]{:S(2)}, u32[]{:S(2)}) collective-permute-start(f32[9,1,3,32]{3,1,0,2:T(1,128)S(1)} %get-tuple-element.23), channel_id=1, source_target_pairs={{0,1},{1,2},{2,3},{3,4},{4,5},{5,6},{6,7},{7,8},{8,9},{9,10},{10,1... | collective-permute-start | bytes 10376 | tf_op jit(solution)/shard_map/ppermute | solution.py:14
  117.1 1.2 copy-start.13

commit v2 on v1

--- a/solution.py
+++ b/solution.py
@@ -17,6 +17,34 @@
         high = lax.ppermute(lax.slice_in_dim(block, 0, width, axis=dim), axis, backward)
         block = jnp.concatenate([low, block, high], axis=dim)
     return block
+
+
+def input_halo(current, previous, courant, axis):
+    count = lax.axis_size(axis)
+    forward = [(i, i + 1) for i in range(count - 1)]
+    backward = [(target, source) for source, target in forward]
+    fields, cells_x, size_y, size_z = current.shape
+
+    def pack(now_planes, prev_planes, courant_planes):
+        return jnp.concatenate(
+            [now_planes.reshape(-1, size_y, size_z), prev_planes.reshape(-1, size_y, size_z), courant_planes]
+        )
+
+    def unpack(planes):
+        now_planes = planes[: 2 * fields].reshape(fields, 2, size_y, size_z)
+        prev_planes = planes[2 * fields : 3 * fields].reshape(fields, 1, size_y, size_z)
+        return now_planes, prev_planes, planes[3 * fields :]
+
+    low = lax.ppermute(
+        pack(current[:, -2:], previous[:, -1:], courant[-1:]), axis, forward
+    )
+    high = lax.ppermute(pack(current[:, :2], previous[:, :1], courant[:1]), axis, backward)
+    low_now, low_prev, low_courant = unpack(low)
+    high_now, high_prev, high_courant = unpack(high)
+    current_wide = jnp.concatenate([low_now, current, high_now], axis=1)
+    previous_wide = jnp.concatenate([low_prev, previous, high_prev], axis=1)
+    courant_wide = jnp.concatenate([low_courant, courant, high_courant], axis=0)
+    return current_wide, previous_wide, courant_wide
 
 
 def inject(cells_here, first_x, cell_index, amplitudes, size_y, size_z):
@@ -112,34 +140,29 @@
 ):
     cells_x, size_y, size_z = courant.shape
     slab_index = lax.axis_index("gx")
+    first_x = slab_index * cells_x
     previous = jnp.stack([source_prev[0], receiver_prev[0]])
     current = jnp.stack([source_now[0], receiver_now[0]])
+    current_wide, previous_wide, courant_wide = input_halo(current, previous, courant, "gx")
     levels = []
     for step_index in range(2):
-        extended = padded_2(current, (("gx", 1),), 1)
-        first_x = slab_index * cells_x
-        advanced = laplace_step(
-            previous,
-            extended,
-            courant,
-            jnp.stack(
-                [
-                    inject(
-                        cells_x, first_x, source_cells[0], wavelet[0, step_index], size_y, size_z
-                    ),
-                    inject(
-                        cells_x,
-                        first_x,
-                        receiver_cells[0],
-                        receiver_data[0, step_index],
-                        size_y,
-                        size_z,
-                    ),
-                ]
-            ),
+        if step_index == 0:
+            cells_here, first_here = cells_x + 2, first_x - 1
+            step_previous, step_extended, step_courant = previous_wide, current_wide, courant_wide
+        else:
+            cells_here, first_here = cells_x, first_x
+            step_previous, step_extended, step_courant = current, levels[0], courant
+        sources = jnp.stack(
+            [
+                inject(cells_here, first_here, source_cells[0], wavelet[0, step_index], size_y, size_z),
+                inject(
+                    cells_here, first_here, receiver_cells[0], receiver_data[0, step_index], size_y, size_z
+                ),
+            ]
         )
-        previous, current = (current, advanced)
+        advanced = laplace_step(step_previous, step_extended, step_courant, sources)
         levels.append(advanced)
+    levels[0] = levels[0][:, 1:-1]
     fields = jnp.concatenate(levels, axis=0)
     wide = padded_2(fields, (("gx", 1),), HMAX)
     coarse = offset_image(wide, offsets, HMAX, cells_x)

time: 120 us -> 119 us (level)
  the two profiles are of different devices: /device:TPU:56 before, /device:TPU:48 now
where the time goes in v2:
time: 119 us; the launch traced here: 118 us
  starting transfers between devices  32.3 us (27%)
  other arithmetic  27.8 us (23%)
  between operations  24 us (20%)
  local copies, waits for them, and re-layouts  16 us (13%)
  waiting for transfers between devices  14.8 us (12%)
  matrix products  3.36 us (3%)
    scatter-add x4, other arithmetic, inject(): jnp.zeros((cells_here * plane_size + 1,), jnp.float32).at[target]  9.42 us
    all_to_all x1, starting transfers between devices, group_sum_windows(): received = lax.all_to_all(windows, axis, 0, 0, tiled=True)  9.41 us
    ppermute x2, starting transfers between devices, padded_2(): lax.ppermute(lax.slice_in_dim(block, 0, width, axis=dim), axis, backward)  9.36 us
    all_to_all x1, waiting for transfers between devices, group_sum_windows(): received = lax.all_to_all(windows, axis, 0, 0, tiled=True)  8.67 us
    unnamed x95, local copies, waits for them, and re-layouts  7.52 us
    ppermute x1, starting transfers between devices, input_halo(): lax.ppermute(pack(current[:, :2], previous[:, :1], courant[:1]), axis, ba...  7.26 us
    add x2, other arithmetic, offset_image(): forward_part[0] * backward_part[1] + forward_part[2] * backward_part[3]  6.45 us
    ppermute x2, waiting for transfers between devices, padded_2(): lax.ppermute(lax.slice_in_dim(block, block.shape[dim] - width, None, axis...  6.15 us
  transfers between devices with their start and end apart: 7, of which 2 were waited for; matrix products, arithmetic and copies ran while one was open for 10% of the time, Pallas kernels for 0%

profile of v2, /device:TPU:48, one launch (start us, length us, event | category | flops | bytes accessed | tf_op | source)
XLA Modules:
  0.0 118.3 jit_solution(3643968766668494738)
XLA Ops:
  0.0 1.1 fusion.37
  1.5 1.9 %collective-permute-start = (f32[7,64,128]{2,1,0:T(8,128)S(1)}, f32[7,64,128]{2,1,0:T(8,128)}, u32[]{:S(2)}, u32[]{:S(2)}) collective-permute-start(f32[7,64,128]{2,1,0:T(8,128)S(1)} %pad_maximum_fusion.7), channel_id=1, source_target_pairs={{0,1},{1,2},{2,3},{3,4},{4,5},{5,6},{6,7},{7,8},{8,9},{9,10},{10,1... | collective-permute-start | bytes 688136 | tf_op jit(solution)/shard_map/ppermute | solution.py:38
  3.5 7.3 %collective-permute-start.1 = (f32[7,64,128]{2,1,0:T(8,128)S(1)}, f32[7,64,128]{2,1,0:T(8,128)}, u32[]{:S(2)}, u32[]{:S(2)}) collective-permute-start(f32[7,64,128]{2,1,0:T(8,128)S(1)} %pad_maximum_fusion.8), channel_id=1, source_target_pairs={{1,0},{2,1},{3,2},{4,3},{5,4},{6,5},{7,6},{8,7},{9,8},{10,9},{11,1... | collective-permute-start | bytes 688136 | tf_op jit(solution)/shard_map/ppermute | solution.py:41
  10.9 4.0 %scatter_custom_fusion.1 = f32[147457]{0:T(1024)S(1)} fusion(s32[512]{0:T(512)S(1)} %bitcast.352, f32[512]{0:T(512)S(1)} %bitcast.354, f32[]{:T(128)} %constant.160.clone.1), kind=kCustom, calls=%fused_computation.79 | custom fusion | flops 512 | bytes 589832 | tf_op jit(solution)/shard_map/scatter-add | solution.py:57
  15.7 4.0 %scatter_custom_fusion.3 = f32[131073]{0:T(1024)S(1)} fusion(s32[512]{0:T(512)S(1)} %bitcast.351, f32[512]{0:T(512)S(1)} %bitcast.353, f32[]{:T(128)} %constant.160.clone.1), kind=kCustom, calls=%fused_computation.83 | custom fusion | flops 512 | bytes 524296 | tf_op jit(solution)/shard_map/scatter-add | solution.py:57
  20.5 1.1 slice.535
  21.6 0.9 slice.538
  22.7 0.9 slice.541
  24.4 0.8 slice_bitcast_fusion.14
  25.2 0.8 slice_bitcast_fusion.15
  26.1 1.5 %fusion.7 = f32[2,18,64,128]{3,2,0,1:T(8,128)S(1)} fusion(f32[2,18,64,128]{3,2,0,1:T(8,128)S(1)} %pad_maximum_fusion.2, f32[2,1,64,128]{3,2,0,1:T(8,128)S(1)} %slice_bitcast_fusion.14, f32[1,16,64,128]{3,2,0,1:T(8,128)S(1)} %bitcast.330, f32[1,16,64,128]{3,2,0,1:T(8,128)S(1)} %bitcast.332, f32[2,1,64,128]{3,2,0,1:T(8,128)S(1)} %slice_bitcast_fusion.15, ...), kind=kLoop, calls=%fused_computation.27 | loop fusion | flops 5898240 | bytes 6619136 | tf_op jit(solution)/shard_map/add | solution.py:67
  27.7 0.9 copy-done.4
  29.0 0.9 fusion.12
  29.9 1.2 fusion.13
  31.0 1.9 %collective-permute-start.2 = (f32[4,8,64,128]{3,2,0,1:T(8,128)}, f32[4,8,64,128]{3,2,0,1:T(8,128)}, u32[]{:S(2)}, u32[]{:S(2)}) collective-permute-start(f32[4,8,64,128]{3,2,0,1:T(8,128)} %get-tuple-element.20), channel_id=1, source_target_pairs={{0,1},{1,2},{2,3},{3,4},{4,5},{5,6},{6,7},{7,8},{8,9},{9,10},{10,1... | collective-permute-start | bytes 3145736 | tf_op jit(solution)/shard_map/ppermute | solution.py:14
  33.0 7.4 %collective-permute-start.3 = (f32[4,8,64,128]{3,2,0,1:T(8,128)S(1)}, f32[4,8,64,128]{3,2,0,1:T(8,128)}, u32[]{:S(2)}, u32[]{:S(2)}) collective-permute-start(f32[4,8,64,128]{3,2,0,1:T(8,128)S(1)} %get-tuple-element.21), channel_id=1, source_target_pairs={{1,0},{2,1},{3,2},{4,3},{5,4},{6,5},{7,6},{8,7},{9,8},{10,9},{11,1... | collective-permute-start | bytes 3145736 | tf_op jit(solution)/shard_map/ppermute | solution.py:17
  64.2 1.9 %pad_maximum_fusion = f32[4,32,64,128]{3,2,0,1:T(8,128)S(1)} fusion(f32[4,8,64,128]{3,2,0,1:T(8,128)} %collective-permute-done.3, f32[2,16,64,128]{3,2,0,1:T(8,128)S(1)} %fusion.12, f32[2,16,64,128]{3,2,0,1:T(8,128)S(1)} %slice.545, f32[4,8,64,128]{3,2,0,1:T(8,128)} %collective-permute-done.2), kind=kLoop, calls=%fused_computation.8 | loop fusion | flops 3145728 | bytes 8388608 | tf_op jit(solution)/shard_map/concatenate | solution.py:18
  66.1 2.8 %fusion.20 = (f32[1,16,64,128]{3,2,0,1:T(8,128)S(1)}, f32[1,16,64,128]{3,2,0,1:T(8,128)S(1)}, f32[1,16,64,128]{3,2,0,1:T(8,128)S(1)}, f32[1,16,64,128]{3,2,0,1:T...) fusion(f32[4,32,64,128]{3,2,0,1:T(8,128)S(1)} %pad_maximum_fusion, ...), kind=kLoop, calls=%fused_computation.51 | loop fusion | flops 2752512 | bytes 18350148 | tf_op jit(solution)/shard_map/add | solution.py:83
  68.9 1.1 reduce_sum.91
  70.0 3.6 %fusion.23 = (f32[1,16,64,128]{3,2,0,1:T(8,128)}, f32[1,16,64,128]{3,2,0,1:T(8,128)}) fusion(f32[4,32,64,128]{3,2,0,1:T(8,128)} %copy-done, s32[]{:T(128)S(6)} %add.612, s32[]{:T(128)S(6)} %select_n.252, s32[]{:T(128)S(6)} %add.611, s32[]{:T(128)S(6)} %select_n.251, s32[]{:T(128)S(6)} %add.610, s32[]{:T(128)S(6)} %select_n.242, s32[]{:T(128)S(6)} %select_n.241), kind=kLoop, calls=%fused_computation.60 | loop fusion | flops 786432 | bytes 5242908 | tf_op jit(solution)/shard_map/add | solution.py:83
  73.6 1.1 reduce_sum.90
  77.3 1.1 copy-done.14
  78.4 0.9 bitcast_dynamic-update-slice_fusion.6
  79.5 1.7 %fusion.45 = f32[9,4,64,32]{2,3,1,0:T(8,128)S(1)} fusion(f32[9,4,64,128]{3,2,1,0:T(8,128)S(1)} %bitcast_dynamic-update-slice_fusion, s32[128]{0:T(128)S(1)} %and_select_fusion.5), kind=kOutput, calls=%fused_computation.198 | convolution fusion | flops 113250304 | bytes 1475072 | tf_op jit(solution)/shard_map/ixyz,zc->ixyc/dot_general | solution.py:86
  81.2 1.3 %fusion.8 = f32[9,4,16,32]{3,2,1,0:T(8,128)S(1)} fusion(f32[9,4,64,32]{2,3,1,0:T(8,128)S(1)} %fusion.45, s32[64]{0:T(128)S(1)} %and_select_fusion.4), kind=kOutput, calls=%fused_computation.34 | convolution fusion | flops 14175232 | bytes 368896 | tf_op jit(solution)/shard_map/yb,ixyc->ixbc/dot_general | solution.py:89
  83.3 1.3 %reshape.649 = f32[16,1,3456]{2,1,0:T(1,128)} reshape(f32[16,9,3,4,32]{4,3,2,1,0:T(4,128)S(1)} %bitcast.324) | data formatting | bytes 442368
  84.5 9.4 %all-to-all-start = ((f32[16,1,3456]{2,1,0:T(1,128)}), f32[16,1,3456]{2,1,0:T(1,128)S(1)}, u32[]{:S(2)}, u32[]{:S(2)}) async-start(f32[16,1,3456]{2,1,0:T(1,128)} %reshape.649), calls=%async_computation | async-start | bytes 442368 | tf_op jit(solution)/shard_map/all_to_all | solution.py:123
  94.0 8.7 %all-to-all-done = f32[16,1,3456]{2,1,0:T(1,128)S(1)} async-done(((f32[16,1,3456]{2,1,0:T(1,128)}), f32[16,1,3456]{2,1,0:T(1,128)S(1)}, u32[]{:S(2)}, u32[]{:S(2)}) %all-to-all-start) | async-done | bytes 221216 | tf_op jit(solution)/shard_map/all_to_all | solution.py:123
  103.2 1.2 reduce
  105.0 1.9 %collective-permute-start.5 = (f32[9,1,3,32]{3,1,0,2:T(1,128)S(1)}, f32[9,1,3,32]{3,1,0,2:T(1,128)S(1)}, u32[]{:S(2)}, u32[]{:S(2)}) collective-permute-start(f32[9,1,3,32]{3,1,0,2:T(1,128)S(1)} %get-tuple-element.32), channel_id=1, source_target_pairs={{1,0},{2,1},{3,2},{4,3},{5,4},{6,5},{7,6},{8,7},{9,8},{10,9},{11,1... | collective-permute-start | bytes 10376 | tf_op jit(solution)/shard_map/ppermute | solution.py:17
  106.9 2.4 %collective-permute-start.4 = (f32[9,1,3,32]{3,1,0,2:T(1,128)S(1)}, f32[9,1,3,32]{3,1,0,2:T(1,128)S(1)}, u32[]{:S(2)}, u32[]{:S(2)}) collective-permute-start(f32[9,1,3,32]{3,1,0,2:T(1,128)S(1)} %get-tuple-element.31), channel_id=1, source_target_pairs={{0,1},{1,2},{2,3},{3,4},{4,5},{5,6},{6,7},{7,8},{8,9},{9,10},{10,1... | collective-permute-start | bytes 10376 | tf_op jit(solution)/shard_map/ppermute | solution.py:14
  109.4 6.2 %collective-permute-done.4 = f32[9,1,3,32]{3,1,0,2:T(1,128)S(1)} collective-permute-done((f32[9,1,3,32]{3,1,0,2:T(1,128)S(1)}, f32[9,1,3,32]{3,1,0,2:T(1,128)S(1)}, u32[]{:S(2)}, u32[]{:S(2)}) %collective-permute-start.4) | collective-permute-done | bytes 3488 | tf_op jit(solution)/shard_map/ppermute | solution.py:14
  (150 shorter events, 11.2 us)
Async XLA Ops:
  0.0 1.2 copy-start.3
  0.0 1.3 %copy-start.11 = (f32[1,16,64,128]{3,2,1,0:T(8,128)S(1)}, f32[1,16,64,128]{3,2,1,0:T(8,128)}, u32[]{:S(2)}) copy-start(f32[1,16,64,128]{3,2,1,0:T(8,128)} %param.12) | copy-start | bytes 1572868
  0.0 1.5 %copy-start.9 = (f32[1,16,64,128]{3,2,1,0:T(8,128)S(1)}, f32[1,16,64,128]{3,2,1,0:T(8,128)}, u32[]{:S(2)}) copy-start(f32[1,16,64,128]{3,2,1,0:T(8,128)} %param.14) | copy-start | bytes 1572868
  1.5 9.3 %copy-start.19 = (s32[1,512]{1,0:T(1,128)S(1)}, s32[1,512]{1,0:T(1,128)}, u32[]{:S(2)}) copy-start(s32[1,512]{1,0:T(1,128)} %param.19) | copy-start | bytes 6148
  1.5 9.3 %copy-start.18 = (f32[1,2,512]{2,1,0:T(2,128)S(1)}, f32[1,2,512]{2,1,0:T(2,128)}, u32[]{:S(2)}) copy-start(f32[1,2,512]{2,1,0:T(2,128)} %param.20) | copy-start | bytes 12292
  1.5 9.4 %copy-start.22 = (s32[1,8]{1,0:T(1,128)S(1)}, s32[1,8]{1,0:T(1,128)}, u32[]{:S(2)}) copy-start(s32[1,8]{1,0:T(1,128)} %param.17) | copy-start | bytes 100
  1.5 19.0 %collective-permute-start = (f32[7,64,128]{2,1,0:T(8,128)S(1)}, f32[7,64,128]{2,1,0:T(8,128)}, u32[]{:S(2)}, u32[]{:S(2)}) collective-permute-start(f32[7,64,128]{2,1,0:T(8,128)S(1)} %pad_maximum_fusion.7), channel_id=1, source_target_pairs={{0,1},{1,2},{2,3},{3,4},{4,5},{5,6},{6,7},{7,8},{8,9},{9,10},{10,1... | collective-permute-start | bytes 688136 | tf_op jit(solution)/shard_map/ppermute | solution.py:38
  3.5 11.4 %copy-start.20 = (f32[1,2,8]{2,1,0:T(2,128)S(1)}, f32[1,2,8]{2,1,0:T(2,128)}, u32[]{:S(2)}) copy-start(f32[1,2,8]{2,1,0:T(2,128)} %param.18) | copy-start | bytes 196
  3.5 18.1 %collective-permute-start.1 = (f32[7,64,128]{2,1,0:T(8,128)S(1)}, f32[7,64,128]{2,1,0:T(8,128)}, u32[]{:S(2)}, u32[]{:S(2)}) collective-permute-start(f32[7,64,128]{2,1,0:T(8,128)S(1)} %pad_maximum_fusion.8), channel_id=1, source_target_pairs={{1,0},{2,1},{3,2},{4,3},{5,4},{6,5},{7,6},{8,7},{9,8},{10,9},{11,1... | collective-permute-start | bytes 688136 | tf_op jit(solution)/shard_map/ppermute | solution.py:41
  15.7 4.0 %copy-start.6 = (f32[147457]{0:T(1024)}, f32[147457]{0:T(1024)S(1)}, u32[]{:S(2)}) copy-start(f32[147457]{0:T(1024)S(1)} %scatter_custom_fusion) | copy-start | bytes 1769488
  19.7 2.8 %copy-start.1 = (f32[1,16,64,128]{3,2,1,0:T(8,128)S(1)}, f32[1,16,64,128]{3,2,1,0:T(8,128)}, u32[]{:S(2)}) copy-start(f32[1,16,64,128]{3,2,1,0:T(8,128)} %param.15) | copy-start | bytes 1572868
  19.7 2.8 %copy-start.2 = (f32[1,16,64,128]{3,2,1,0:T(8,128)S(1)}, f32[1,16,64,128]{3,2,1,0:T(8,128)}, u32[]{:S(2)}) copy-start(f32[1,16,64,128]{3,2,1,0:T(8,128)} %param.13) | copy-start | bytes 1572868
  20.5 2.0 %copy-start.8 = (f32[131073]{0:T(1024)}, f32[131073]{0:T(1024)S(1)}, u32[]{:S(2)}) copy-start(f32[131073]{0:T(1024)S(1)} %scatter_custom_fusion.2) | copy-start | bytes 1572880
  22.5 3.5 %copy-start.10 = (f32[1,16,64,128]{3,2,1,0:T(8,128)S(1)}, f32[1,16,64,128]{3,2,1,0:T(8,128)}, u32[]{:S(2)}) copy-start(f32[1,16,64,128]{3,2,1,0:T(8,128)} %param.14) | copy-start | bytes 1572868
  22.6 3.5 %copy-start.12 = (f32[1,16,64,128]{3,2,1,0:T(8,128)S(1)}, f32[1,16,64,128]{3,2,1,0:T(8,128)}, u32[]{:S(2)}) copy-start(f32[1,16,64,128]{3,2,1,0:T(8,128)} %param.12) | copy-start | bytes 1572868
  22.6 3.4 %slice-start = ((f32[147457]{0:T(1024)}), f32[147456]{0:T(1024)S(1)}, s32[]{:S(2)}) async-start(f32[147457]{0:T(1024)} %copy-done.5), calls=%async_computation.1 | async-start | bytes 1179648 | tf_op jit(solution)/shard_map/slice | solution.py:58
  22.7 3.4 %slice-start.1 = ((f32[147457]{0:T(1024)}), f32[147456]{0:T(1024)S(1)}, s32[]{:S(2)}) async-start(f32[147457]{0:T(1024)} %copy-done.6), calls=%async_computation.2 | async-start | bytes 1179648 | tf_op jit(solution)/shard_map/slice | solution.py:58
  27.6 1.0 copy-start.4
  27.6 1.2 %slice-start.2 = ((f32[131073]{0:T(1024)}), f32[131072]{0:T(1024)S(1)}, s32[]{:S(2)}) async-start(f32[131073]{0:T(1024)} %copy-done.7), calls=%async_computation.3 | async-start | bytes 1048576 | tf_op jit(solution)/shard_map/slice | solution.py:58
  27.7 1.3 %slice-start.3 = ((f32[131073]{0:T(1024)}), f32[131072]{0:T(1024)S(1)}, s32[]{:S(2)}) async-start(f32[131073]{0:T(1024)} %copy-done.8), calls=%async_computation.4 | async-start | bytes 1048576 | tf_op jit(solution)/shard_map/slice | solution.py:58
  29.9 10.5 %copy-start.17 = (s32[9]{0:T(128)S(1)}, s32[9]{0:T(128)}, u32[]{:S(2)}) copy-start(s32[9]{0:T(128)} %param.21) | copy-start | bytes 112
  31.0 33.2 %collective-permute-start.2 = (f32[4,8,64,128]{3,2,0,1:T(8,128)}, f32[4,8,64,128]{3,2,0,1:T(8,128)}, u32[]{:S(2)}, u32[]{:S(2)}) collective-permute-start(f32[4,8,64,128]{3,2,0,1:T(8,128)} %get-tuple-element.20), channel_id=1, source_target_pairs={{0,1},{1,2},{2,3},{3,4},{4,5},{5,6},{6,7},{7,8},{8,9},{9,10},{10,1... | collective-permute-start | bytes 3145736 | tf_op jit(solution)/shard_map/ppermute | solution.py:14
  33.0 31.2 %collective-permute-start.3 = (f32[4,8,64,128]{3,2,0,1:T(8,128)S(1)}, f32[4,8,64,128]{3,2,0,1:T(8,128)}, u32[]{:S(2)}, u32[]{:S(2)}) collective-permute-start(f32[4,8,64,128]{3,2,0,1:T(8,128)S(1)} %get-tuple-element.21), channel_id=1, source_target_pairs={{1,0},{2,1},{3,2},{4,3},{5,4},{6,5},{7,6},{8,7},{9,8},{10,9},{11,1... | collective-permute-start | bytes 3145736 | tf_op jit(solution)/shard_map/ppermute | solution.py:17
  66.1 2.8 %copy-start = (f32[4,32,64,128]{3,2,0,1:T(8,128)}, f32[4,32,64,128]{3,2,0,1:T(8,128)S(1)}, u32[]{:S(2)}) copy-start(f32[4,32,64,128]{3,2,0,1:T(8,128)S(1)} %pad_maximum_fusion) | copy-start | bytes 12582916
  76.0 1.1 copy-start.13
  77.2 1.3 %copy-start.14 = (f32[9,4,64,128]{3,2,1,0:T(8,128)S(1)}, f32[9,4,64,128]{3,2,1,0:T(8,128)}, u32[]{:S(2)}) copy-start(f32[9,4,64,128]{3,2,1,0:T(8,128)} %bitcast_dynamic-update-slice_fusion.8) | copy-start | bytes 3538948
  77.2 2.2 %copy-start.15 = (f32[4,64,128]{2,1,0:T(8,128)S(1)}, f32[4,64,128]{2,1,0:T(8,128)}, u32[]{:S(2)}) copy-start(f32[4,64,128]{2,1,0:T(8,128)} %reduce_sum.93) | copy-start | bytes 393220
  83.2 10.7 %copy-start.16 = (f32[64,9,3,3,3]{0,4,3,2,1:T(4,128)S(1)}, f32[64,9,3,3,3]{0,4,3,2,1:T(4,128)}, u32[]{:S(2)}) copy-start(f32[64,9,3,3,3]{0,4,3,2,1:T(4,128)} %param.22) | copy-start | bytes 186628
  84.5 18.2 %all-to-all-start = ((f32[16,1,3456]{2,1,0:T(1,128)}), f32[16,1,3456]{2,1,0:T(1,128)S(1)}, u32[]{:S(2)}, u32[]{:S(2)}) async-start(f32[16,1,3456]{2,1,0:T(1,128)} %reshape.649), calls=%async_computation | async-start | bytes 442368 | tf_op jit(solution)/shard_map/all_to_all | solution.py:123
  105.0 4.4 %collective-permute-start.5 = (f32[9,1,3,32]{3,1,0,2:T(1,128)S(1)}, f32[9,1,3,32]{3,1,0,2:T(1,128)S(1)}, u32[]{:S(2)}, u32[]{:S(2)}) collective-permute-start(f32[9,1,3,32]{3,1,0,2:T(1,128)S(1)} %get-tuple-element.32), channel_id=1, source_target_pairs={{1,0},{2,1},{3,2},{4,3},{5,4},{6,5},{7,6},{8,7},{9,8},{10,9},{11,1... | collective-permute-start | bytes 10376 | tf_op jit(solution)/shard_map/ppermute | solution.py:17
  106.9 8.6 %collective-permute-start.4 = (f32[9,1,3,32]{3,1,0,2:T(1,128)S(1)}, f32[9,1,3,32]{3,1,0,2:T(1,128)S(1)}, u32[]{:S(2)}, u32[]{:S(2)}) collective-permute-start(f32[9,1,3,32]{3,1,0,2:T(1,128)S(1)} %get-tuple-element.31), channel_id=1, source_target_pairs={{0,1},{1,2},{2,3},{3,4},{4,5},{5,6},{6,7},{7,8},{8,9},{9,10},{10,1... | collective-permute-start | bytes 10376 | tf_op jit(solution)/shard_map/ppermute | solution.py:14
  116.0 1.2 copy-start.21
  (2 other events, 1.6 us)

commit v3 on v1

--- a/solution.py
+++ b/solution.py
@@ -17,6 +17,18 @@
         high = lax.ppermute(lax.slice_in_dim(block, 0, width, axis=dim), axis, backward)
         block = jnp.concatenate([low, block, high], axis=dim)
     return block
+
+
+def input_halo(arrays, width, axis):
+    count = lax.axis_size(axis)
+    forward = [(i, i + 1) for i in range(count - 1)]
+    backward = [(target, source) for source, target in forward]
+    low = lax.ppermute(jnp.concatenate([array[-width:] for array in arrays]), axis, forward)
+    high = lax.ppermute(jnp.concatenate([array[:width] for array in arrays]), axis, backward)
+    return [
+        jnp.concatenate([low[k * width : (k + 1) * width], array, high[k * width : (k + 1) * width]])
+        for k, array in enumerate(arrays)
+    ]
 
 
 def inject(cells_here, first_x, cell_index, amplitudes, size_y, size_z):
@@ -111,37 +123,40 @@
     conv_bias,
 ):
     cells_x, size_y, size_z = courant.shape
-    slab_index = lax.axis_index("gx")
-    previous = jnp.stack([source_prev[0], receiver_prev[0]])
-    current = jnp.stack([source_now[0], receiver_now[0]])
+    margin = HMAX + 2
+    assert margin <= cells_x
+    first_x = lax.axis_index("gx") * cells_x
+    source_prev_w, source_now_w, receiver_prev_w, receiver_now_w, courant_w = input_halo(
+        [source_prev[0], source_now[0], receiver_prev[0], receiver_now[0], courant], margin, "gx"
+    )
+    previous = jnp.stack([source_prev_w, receiver_prev_w])
+    current = jnp.stack([source_now_w, receiver_now_w])
     levels = []
     for step_index in range(2):
-        extended = padded_2(current, (("gx", 1),), 1)
-        first_x = slab_index * cells_x
+        trim = step_index + 1
+        cells_here = cells_x + 2 * (margin - trim)
+        sources = jnp.stack(
+            [
+                inject(cells_here, first_x - margin + trim, source_cells[0], wavelet[0, step_index], size_y, size_z),
+                inject(
+                    cells_here,
+                    first_x - margin + trim,
+                    receiver_cells[0],
+                    receiver_data[0, step_index],
+                    size_y,
+                    size_z,
+                ),
+            ]
+        )
         advanced = laplace_step(
-            previous,
-            extended,
-            courant,
-            jnp.stack(
-                [
-                    inject(
-                        cells_x, first_x, source_cells[0], wavelet[0, step_index], size_y, size_z
-                    ),
-                    inject(
-                        cells_x,
-                        first_x,
-                        receiver_cells[0],
-                        receiver_data[0, step_index],
-                        size_y,
-                        size_z,
-                    ),
-                ]
-            ),
+            previous[:, trim : trim + cells_here],
+            current,
+            courant_w[trim : trim + cells_here],
+            sources,
         )
         previous, current = (current, advanced)
         levels.append(advanced)
-    fields = jnp.concatenate(levels, axis=0)
-    wide = padded_2(fields, (("gx", 1),), HMAX)
+    wide = jnp.concatenate([levels[0][:, 1:-1], levels[1]], axis=0)
     coarse = offset_image(wide, offsets, HMAX, cells_x)
     summed = group_sum_windows(coarse, "shot")
     rimmed = padded_2(summed, (("gx", 1),), 1)

time: 120 us -> 142 us (1.18)
  local copies, waits for them, and re-layouts: 10.1 us -> 30.6 us
  other arithmetic: 28 us -> 44.4 us
  starting transfers between devices: 37 us -> 23.2 us
  waiting for transfers between devices: 18.6 us -> 14.7 us
    ppermute x4 -> x1, starting transfers between devices: 19.5 us -> 2.05 us  [padded_2(): lax.ppermute(lax.slice_in_dim(block, 0, width, axis=dim), axis, backward)]
    concatenate x1 -> x4, other arithmetic: 1.18 us -> 17.4 us  [the longest x3 17.3 us: local(): wide = jnp.concatenate([levels[0][:, 1:-1], levels[1]], axis=0)]
    unnamed x80 -> x101, local copies, waits for them, and re-layouts: 6.39 us -> 19.5 us
    ppermute x0 -> x2, starting transfers between devices: none -> 9.17 us  [the longest x1 7.26 us: input_halo(): lax.ppermute(jnp.concatenate([array[:width] for array in arrays]), axis,...]
    ppermute x4 -> x1, starting transfers between devices: 8 us -> 2.28 us  [padded_2(): lax.ppermute(lax.slice_in_dim(block, block.shape[dim] - width, None, axis...]
    slice x2 -> x7, local copies, waits for them, and re-layouts: 0.02 us -> 5.38 us  [the longest x4 2.01 us: local(): courant_w[trim:trim + cells_here]]
    ppermute x4 -> x1, waiting for transfers between devices: 10.2 us -> 6.28 us  [padded_2(): lax.ppermute(lax.slice_in_dim(block, block.shape[dim] - width, None, axis...]
    add x2 -> x9, other arithmetic: 6.44 us -> 9.99 us  [offset_image(): forward_part[0] * backward_part[1] + forward_part[2] * backward_part[3]]
  transfers between devices with their start and end apart: 9 -> 5, of which waited for: 4 -> 2; matrix products, arithmetic and copies ran while one was open for 9% -> 9% of each run, Pallas kernels for 0% -> 0%
where the time goes in v3:
time: 142 us; the launch traced here: 141 us
  other arithmetic  44.4 us (31%)
  local copies, waits for them, and re-layouts  30.6 us (22%)
  between operations  23.3 us (16%)
  starting transfers between devices  23.2 us (16%)
  waiting for transfers between devices  14.7 us (10%)
  matrix products  4.63 us (3%)
    unnamed x101, local copies, waits for them, and re-layouts  19.5 us
    concatenate x3, other arithmetic, local(): wide = jnp.concatenate([levels[0][:, 1:-1], levels[1]], axis=0)  17.3 us
    add x9, other arithmetic, offset_image(): forward_part[0] * backward_part[1] + forward_part[2] * backward_part[3]  9.99 us
    all_to_all x1, starting transfers between devices, group_sum_windows(): received = lax.all_to_all(windows, axis, 0, 0, tiled=True)  9.68 us
    scatter-add x4, other arithmetic, inject(): jnp.zeros((cells_here * plane_size + 1,), jnp.float32).at[target]  9.6 us
    all_to_all x1, waiting for transfers between devices, group_sum_windows(): received = lax.all_to_all(windows, axis, 0, 0, tiled=True)  8.36 us
    ppermute x1, starting transfers between devices, input_halo(): lax.ppermute(jnp.concatenate([array[:width] for array in arrays]), axis,...  7.26 us
    ppermute x1, waiting for transfers between devices, padded_2(): lax.ppermute(lax.slice_in_dim(block, block.shape[dim] - width, None, axis...  6.28 us
  transfers between devices with their start and end apart: 5, of which 2 were waited for; matrix products, arithmetic and copies ran while one was open for 9% of the time, Pallas kernels for 0%

profile of v3, /device:TPU:56, one launch (start us, length us, event | category | flops | bytes accessed | tf_op | source)
XLA Modules:
  0.0 140.7 jit_solution(11355357121637290242)
XLA Ops:
  0.0 2.1 %bitcast_dynamic-update-slice_fusion.7 = (f32[50,64,128]{2,1,0:T(8,128)}, f32[50,64,128]{2,1,0:T(8,128)}) fusion(f32[1,16,64,128]{3,2,1,0:T(8,128)} %param.12), kind=kLoop, calls=%fused_computation.150 | loop fusion | bytes 1310720
  2.1 2.1 %bitcast_dynamic-update-slice_fusion.6 = (f32[50,64,128]{2,1,0:T(8,128)}, f32[50,64,128]{2,1,0:T(8,128)}) fusion(f32[50,64,128]{2,1,0:T(8,128)} %get-tuple-element.47, f32[1,16,64,128]{3,2,1,0:T(8,128)} %param.13, f32[50,64,128]{2,1,0:T(8,128)} %get-tuple-element.48), kind=kLoop, calls=%fused_computation.149 | loop fusion | bytes 1310720
  7.0 1.9 %collective-permute-start = (f32[50,64,128]{2,1,0:T(8,128)}, f32[50,64,128]{2,1,0:T(8,128)}, u32[]{:S(2)}, u32[]{:S(2)}) collective-permute-start(f32[50,64,128]{2,1,0:T(8,128)} %get-tuple-element.39), channel_id=1, source_target_pairs={{0,1},{1,2},{2,3},{3,4},{4,5},{5,6},{6,7},{7,8},{8,9},{9,10},{10,1... | collective-permute-start | bytes 4915208 | tf_op jit(solution)/shard_map/ppermute | solution.py:26
  8.9 7.3 %collective-permute-start.1 = (f32[50,64,128]{2,1,0:T(8,128)}, f32[50,64,128]{2,1,0:T(8,128)}, u32[]{:S(2)}, u32[]{:S(2)}) collective-permute-start(f32[50,64,128]{2,1,0:T(8,128)} %get-tuple-element.40), channel_id=1, source_target_pairs={{1,0},{2,1},{3,2},{4,3},{5,4},{6,5},{7,6},{8,7},{9,8},{10,9},{11,1... | collective-permute-start | bytes 4915208 | tf_op jit(solution)/shard_map/ppermute | solution.py:27
  39.2 3.8 %scatter_custom_fusion.3 = f32[262145]{0:T(1024)S(1)} fusion(s32[512]{0:T(512)S(1)} %bitcast.349, f32[512]{0:T(512)S(1)} %bitcast.352, f32[]{:T(128)} %constant.164.clone.1), kind=kCustom, calls=%fused_computation.110 | custom fusion | flops 512 | bytes 1048584 | tf_op jit(solution)/shard_map/scatter-add | solution.py:41
  45.0 3.8 %scatter_custom_fusion.1 = f32[278529]{0:T(1024)S(1)} fusion(s32[512]{0:T(512)S(1)} %bitcast.350, f32[512]{0:T(512)S(1)} %bitcast.351, f32[]{:T(128)} %constant.164.clone.1), kind=kCustom, calls=%fused_computation.106 | custom fusion | flops 512 | bytes 1114120 | tf_op jit(solution)/shard_map/scatter-add | solution.py:41
  48.8 1.1 scatter_custom_fusion
  50.1 1.7 %fusion.72 = (f32[10,64,128]{2,1,0:T(8,128)S(1)}, f32[10,64,128]{2,1,0:T(8,128)S(1)}, f32[10,64,128]{2,1,0:T(8,128)S(1)}, f32[10,64,128]{2,1,0:T(8,128)S(1)}, f32[10,64,128]{2,1,0:T(8,128)S(1)}) fusion(f32[50,64,128]{2,1,0:T(8,128)} %collective-permute-done), kind=kLoop, calls=%fused_computation.292 | loop fusion | bytes 3276800 | tf_op jit(solution)/shard_map/slice | solution.py:29
  51.8 1.5 %fusion.73 = (f32[10,64,128]{2,1,0:T(8,128)S(1)}, f32[10,64,128]{2,1,0:T(8,128)S(1)}, f32[10,64,128]{2,1,0:T(8,128)S(1)}, f32[10,64,128]{2,1,0:T(8,128)S(1)}, f32[10,64,128]{2,1,0:T(8,128)S(1)}) fusion(f32[50,64,128]{2,1,0:T(8,128)} %collective-permute-done.1), kind=kLoop, calls=%fused_computation.293 | loop fusion | bytes 3276800 | tf_op jit(solution)/shard_map/slice | solution.py:29
  53.5 1.0 copy-done.1
  58.6 2.5 %fusion.9 = f32[2,34,64,128]{3,2,1,0:T(8,128)S(1)} fusion(f32[1,36,64,128]{3,2,1,0:T(8,128)S(1)} %get-tuple-element.67, f32[1,36,64,128]{3,2,1,0:T(8,128)S(1)} %get-tuple-element.68, f32[2,34,64,128]{3,2,1,0:T(8,128)S(1)} %fusion.10, f32[1,36,64,128]{3,2,1,0:T(8,128)S(1)} %get-tuple-element.70, f32[1,36,64,128]{3,2,1,0:T(8,128)S(1)} %get-tuple-element.69, ...), kind=kLoop, calls=%fused_computation.63 | loop fusion | flops 8912896 | bytes 12517376 | tf_op jit(solution)/shard_map/add | solution.py:51
  61.2 1.0 slice-done
  62.9 2.2 %fusion.20 = f32[2,32,64,128]{3,2,1,0:T(8,128)S(1)} fusion(f32[2,32,64,128]{3,2,1,0:T(8,128)S(1)} %slice.628, f32[2,34,64,128]{3,2,1,0:T(8,128)S(1)} %fusion.9, f32[1,36,64,128]{3,2,1,0:T(8,128)S(1)} %get-tuple-element.68, f32[1,36,64,128]{3,2,1,0:T(8,128)S(1)} %get-tuple-element.67, f32[1,32,64,128]{3,2,1,0:T(8,128)S(1)} %bitcast.330, ...), kind=kLoop, calls=%fused_computation.75 | loop fusion | flops 7340032 | bytes 13893632 | tf_op jit(solution)/shard_map/add | solution.py:51
  65.1 4.2 %fusion.36 = (f32[4,16,64,128]{3,2,1,0:T(8,128)S(1)}, f32[4,16,64,128]{3,2,1,0:T(8,128)}, f32[4,16,64,128]{3,2,1,0:T(8,128)}, f32[4,16,64,128]{3,2,1,0:T(8,128)S...) fusion(s32[]{:T(128)S(6)} %select_n.255, f32[2,32,64,128]{3,2,1,0:T(8,128)S(1)} %slice.628, ...), kind=kLoop, calls=%fused_computation.91 | loop fusion | flops 3145728 | bytes 16777240 | tf_op jit(solution)/shard_map/concatenate | solution.py:159
  69.5 1.7 %fusion.52 = f32[1,16,64,128]{3,2,1,0:T(8,128)S(1)} fusion(f32[4,16,64,128]{3,2,1,0:T(8,128)} %get-tuple-element.25, f32[4,16,64,128]{3,2,1,0:T(8,128)} %get-tuple-element.24), kind=kLoop, calls=%fused_computation.121 | loop fusion | flops 393216 | bytes 2621440 | tf_op jit(solution)/shard_map/add | solution.py:67
  71.2 1.7 %fusion.58 = f32[1,16,64,128]{3,2,1,0:T(8,128)S(1)} fusion(f32[4,16,64,128]{3,2,1,0:T(8,128)} %get-tuple-element.28, f32[4,16,64,128]{3,2,1,0:T(8,128)} %get-tuple-element.27), kind=kLoop, calls=%fused_computation.139 | loop fusion | flops 393216 | bytes 2621440 | tf_op jit(solution)/shard_map/add | solution.py:67
  73.6 6.2 %fusion.38 = (f32[4,16,64,128]{3,2,1,0:T(8,128)}, f32[4,16,64,128]{3,2,1,0:T(8,128)S(1)}, f32[4,16,64,128]{3,2,1,0:T(8,128)S(1)}, f32[4,16,64,128]{3,2,1,0:T(8,1...) fusion(s32[]{:T(128)S(6)} %select_n.257, f32[2,32,64,128]{3,2,1,0:T(8,128)S(1)} %slice.628, ...), kind=kLoop, calls=%fused_computation.93 | loop fusion | flops 3145728 | bytes 16777240 | tf_op jit(solution)/shard_map/concatenate | solution.py:159
  79.9 1.7 %fusion.56 = f32[1,16,64,128]{3,2,1,0:T(8,128)S(1)} fusion(f32[4,16,64,128]{3,2,1,0:T(8,128)} %get-tuple-element.15, f32[4,16,64,128]{3,2,1,0:T(8,128)} %get-tuple-element.14), kind=kLoop, calls=%fused_computation.133 | loop fusion | flops 393216 | bytes 2621440 | tf_op jit(solution)/shard_map/add | solution.py:67
  81.7 7.0 %fusion.21 = (f32[4,16,64,128]{3,2,1,0:T(8,128)S(1)}, f32[4,16,64,128]{3,2,1,0:T(8,128)}, f32[4,16,64,128]{3,2,1,0:T(8,128)}, f32[4,16,64,128]{3,2,1,0:T(8,128)}...) fusion(s32[]{:T(128)S(6)} %select_n.258, f32[2,32,64,128]{3,2,1,0:T(8,128)S(1)} %slice.628, ...), kind=kLoop, calls=%fused_computation.76 | loop fusion | flops 3145728 | bytes 16777240 | tf_op jit(solution)/shard_map/concatenate | solution.py:159
  88.8 1.4 copy-done.2
  90.2 1.4 fusion.55
  91.6 1.8 %fusion.54 = f32[1,16,64,128]{3,2,1,0:T(8,128)S(1)} fusion(f32[4,16,64,128]{3,2,1,0:T(8,128)} %get-tuple-element.20, f32[4,16,64,128]{3,2,1,0:T(8,128)} %get-tuple-element.19), kind=kLoop, calls=%fused_computation.127 | loop fusion | flops 393216 | bytes 2621440 | tf_op jit(solution)/shard_map/add | solution.py:67
  93.8 1.4 fusion.53
  100.5 3.0 %fusion.64 = f32[9,4,64,32]{2,3,1,0:T(8,128)S(1)} fusion(f32[9,4,64,128]{3,2,1,0:T(8,128)} %constant_dynamic-update-slice_fusion, s32[128]{0:T(128)S(1)} %and_select_fusion.5), kind=kOutput, calls=%fused_computation.255 | convolution fusion | flops 113250304 | bytes 1475072 | tf_op jit(solution)/shard_map/ixyz,zc->ixyc/dot_general | solution.py:70
  103.5 1.3 fusion.40
  105.6 1.3 reshape.625
  106.8 9.7 %all-to-all-start = ((f32[16,1,3456]{2,1,0:T(1,128)}), f32[16,1,3456]{2,1,0:T(1,128)S(1)}, u32[]{:S(2)}, u32[]{:S(2)}) async-start(f32[16,1,3456]{2,1,0:T(1,128)} %reshape.625), calls=%async_computation | async-start | bytes 442368 | tf_op jit(solution)/shard_map/all_to_all | solution.py:107
  116.6 8.4 %all-to-all-done = f32[16,1,3456]{2,1,0:T(1,128)S(1)} async-done(((f32[16,1,3456]{2,1,0:T(1,128)}), f32[16,1,3456]{2,1,0:T(1,128)S(1)}, u32[]{:S(2)}, u32[]{:S(2)}) %all-to-all-start) | async-done | bytes 221216 | tf_op jit(solution)/shard_map/all_to_all | solution.py:107
  125.5 1.2 reduce
  127.2 2.1 %collective-permute-start.3 = (f32[9,1,3,32]{3,1,0,2:T(1,128)S(1)}, f32[9,1,3,32]{3,1,0,2:T(1,128)S(1)}, u32[]{:S(2)}, u32[]{:S(2)}) collective-permute-start(f32[9,1,3,32]{3,1,0,2:T(1,128)S(1)} %get-tuple-element.53), channel_id=1, source_target_pairs={{1,0},{2,1},{3,2},{4,3},{5,4},{6,5},{7,6},{8,7},{9,8},{10,9},{11,1... | collective-permute-start | bytes 10376 | tf_op jit(solution)/shard_map/ppermute | solution.py:17
  129.3 2.3 %collective-permute-start.2 = (f32[9,1,3,32]{3,1,0,2:T(1,128)S(1)}, f32[9,1,3,32]{3,1,0,2:T(1,128)S(1)}, u32[]{:S(2)}, u32[]{:S(2)}) collective-permute-start(f32[9,1,3,32]{3,1,0,2:T(1,128)S(1)} %get-tuple-element.52), channel_id=1, source_target_pairs={{0,1},{1,2},{2,3},{3,4},{4,5},{5,6},{6,7},{7,8},{8,9},{9,10},{10,1... | collective-permute-start | bytes 10376 | tf_op jit(solution)/shard_map/ppermute | solution.py:14
  131.7 6.3 %collective-permute-done.2 = f32[9,1,3,32]{3,1,0,2:T(1,128)S(1)} collective-permute-done((f32[9,1,3,32]{3,1,0,2:T(1,128)S(1)}, f32[9,1,3,32]{3,1,0,2:T(1,128)S(1)}, u32[]{:S(2)}, u32[]{:S(2)}) %collective-permute-start.2) | collective-permute-done | bytes 3488 | tf_op jit(solution)/shard_map/ppermute | solution.py:14
  (156 shorter events, 21.9 us)
Async XLA Ops:
  0.0 4.1 %copy-start.13 = (f32[1,16,64,128]{3,2,1,0:T(8,128)S(1)}, f32[1,16,64,128]{3,2,1,0:T(8,128)}, u32[]{:S(2)}) copy-start(f32[1,16,64,128]{3,2,1,0:T(8,128)} %param.14) | copy-start | bytes 1572868
  0.0 5.1 %copy-start.10 = (f32[1,16,64,128]{3,2,1,0:T(8,128)S(1)}, f32[1,16,64,128]{3,2,1,0:T(8,128)}, u32[]{:S(2)}) copy-start(f32[1,16,64,128]{3,2,1,0:T(8,128)} %param.15) | copy-start | bytes 1572868
  2.1 3.9 %copy-start.15 = (f32[16,64,128]{2,1,0:T(8,128)S(1)}, f32[16,64,128]{2,1,0:T(8,128)}, u32[]{:S(2)}) copy-start(f32[16,64,128]{2,1,0:T(8,128)} %param.16) | copy-start | bytes 1572868
  4.1 12.0 %copy-start.19 = (f32[1,2,512]{2,1,0:T(2,128)S(1)}, f32[1,2,512]{2,1,0:T(2,128)}, u32[]{:S(2)}) copy-start(f32[1,2,512]{2,1,0:T(2,128)} %param.20) | copy-start | bytes 12292
  4.1 12.0 %copy-start.18 = (s32[9]{0:T(128)S(1)}, s32[9]{0:T(128)}, u32[]{:S(2)}) copy-start(s32[9]{0:T(128)} %param.21) | copy-start | bytes 112
  4.1 35.0 %copy-start.20 = (s32[1,512]{1,0:T(1,128)S(1)}, s32[1,512]{1,0:T(1,128)}, u32[]{:S(2)}) copy-start(s32[1,512]{1,0:T(1,128)} %param.19) | copy-start | bytes 6148
  6.0 37.1 %copy-start.23 = (s32[1,8]{1,0:T(1,128)S(1)}, s32[1,8]{1,0:T(1,128)}, u32[]{:S(2)}) copy-start(s32[1,8]{1,0:T(1,128)} %param.17) | copy-start | bytes 100
  6.0 37.1 %copy-start.21 = (f32[1,2,8]{2,1,0:T(2,128)S(1)}, f32[1,2,8]{2,1,0:T(2,128)}, u32[]{:S(2)}) copy-start(f32[1,2,8]{2,1,0:T(2,128)} %param.18) | copy-start | bytes 196
  7.0 43.1 %collective-permute-start = (f32[50,64,128]{2,1,0:T(8,128)}, f32[50,64,128]{2,1,0:T(8,128)}, u32[]{:S(2)}, u32[]{:S(2)}) collective-permute-start(f32[50,64,128]{2,1,0:T(8,128)} %get-tuple-element.39), channel_id=1, source_target_pairs={{0,1},{1,2},{2,3},{3,4},{4,5},{5,6},{6,7},{7,8},{8,9},{9,10},{10,1... | collective-permute-start | bytes 4915208 | tf_op jit(solution)/shard_map/ppermute | solution.py:26
  8.9 43.0 %collective-permute-start.1 = (f32[50,64,128]{2,1,0:T(8,128)}, f32[50,64,128]{2,1,0:T(8,128)}, u32[]{:S(2)}, u32[]{:S(2)}) collective-permute-start(f32[50,64,128]{2,1,0:T(8,128)} %get-tuple-element.40), channel_id=1, source_target_pairs={{1,0},{2,1},{3,2},{4,3},{5,4},{6,5},{7,6},{8,7},{9,8},{10,9},{11,1... | collective-permute-start | bytes 4915208 | tf_op jit(solution)/shard_map/ppermute | solution.py:27
  48.8 1.1 copy-start.5
  49.9 1.9 %copy-start.6 = (f32[278529]{0:T(1024)}, f32[278529]{0:T(1024)S(1)}, u32[]{:S(2)}) copy-start(f32[278529]{0:T(1024)S(1)} %scatter_custom_fusion) | copy-start | bytes 3342352
  51.8 1.6 %copy-start.16 = (f32[16,64,128]{2,1,0:T(8,128)S(1)}, f32[16,64,128]{2,1,0:T(8,128)}, u32[]{:S(2)}) copy-start(f32[16,64,128]{2,1,0:T(8,128)} %param.16) | copy-start | bytes 1572868
  53.5 1.4 copy-start.9
  53.5 1.6 %copy-start.11 = (f32[1,16,64,128]{3,2,1,0:T(8,128)S(1)}, f32[1,16,64,128]{3,2,1,0:T(8,128)}, u32[]{:S(2)}) copy-start(f32[1,16,64,128]{3,2,1,0:T(8,128)} %param.15) | copy-start | bytes 1572868
  55.4 1.0 copy-start.12
  55.4 1.2 copy-start.14
  56.6 1.2 slice-start.1
  56.6 1.6 %slice-start.2 = ((f32[278529]{0:T(1024)}), f32[278528]{0:T(1024)S(1)}, s32[]{:S(2)}) async-start(f32[278529]{0:T(1024)} %copy-done.5), calls=%async_computation.3 | async-start | bytes 2228224 | tf_op jit(solution)/shard_map/slice | solution.py:42
  56.6 1.9 %slice-start.3 = ((f32[278529]{0:T(1024)}), f32[278528]{0:T(1024)S(1)}, s32[]{:S(2)}) async-start(f32[278529]{0:T(1024)} %copy-done.6), calls=%async_computation.4 | async-start | bytes 2228224 | tf_op jit(solution)/shard_map/slice | solution.py:42
  61.1 1.2 slice-start
  61.1 1.5 %slice-start.4 = ((f32[262145]{0:T(1024)}), f32[262144]{0:T(1024)S(1)}, s32[]{:S(2)}) async-start(f32[262145]{0:T(1024)} %copy-done.7), calls=%async_computation.5 | async-start | bytes 2097152 | tf_op jit(solution)/shard_map/slice | solution.py:42
  61.1 1.8 %slice-start.5 = ((f32[262145]{0:T(1024)}), f32[262144]{0:T(1024)S(1)}, s32[]{:S(2)}) async-start(f32[262145]{0:T(1024)} %copy-done.8), calls=%async_computation.6 | async-start | bytes 2097152 | tf_op jit(solution)/shard_map/slice | solution.py:42
  65.1 4.2 %copy-start = (f32[2,32,64,128]{3,2,1,0:T(8,128)}, f32[2,32,64,128]{3,2,1,0:T(8,128)S(1)}, u32[]{:S(2)}) copy-start(f32[2,32,64,128]{3,2,1,0:T(8,128)S(1)} %fusion.20) | copy-start | bytes 6291460
  81.7 7.0 %copy-start.3 = (f32[4,16,64,128]{3,2,1,0:T(8,128)S(1)}, f32[4,16,64,128]{3,2,1,0:T(8,128)}, u32[]{:S(2)}) copy-start(f32[4,16,64,128]{3,2,1,0:T(8,128)} %get-tuple-element.11) | copy-start | bytes 6291460
  88.6 1.6 %copy-start.2 = (f32[4,16,64,128]{3,2,1,0:T(8,128)S(1)}, f32[4,16,64,128]{3,2,1,0:T(8,128)}, u32[]{:S(2)}) copy-start(f32[4,16,64,128]{3,2,1,0:T(8,128)} %get-tuple-element.16) | copy-start | bytes 6291460
  91.6 2.2 %copy-start.4 = (f32[4,16,64,128]{3,2,1,0:T(8,128)S(1)}, f32[4,16,64,128]{3,2,1,0:T(8,128)}, u32[]{:S(2)}) copy-start(f32[4,16,64,128]{3,2,1,0:T(8,128)} %get-tuple-element.21) | copy-start | bytes 6291460
  105.2 11.3 %copy-start.17 = (f32[64,9,3,3,3]{0,4,3,2,1:T(4,128)S(1)}, f32[64,9,3,3,3]{0,4,3,2,1:T(4,128)}, u32[]{:S(2)}) copy-start(f32[64,9,3,3,3]{0,4,3,2,1:T(4,128)} %param.22) | copy-start | bytes 186628
  106.8 18.1 %all-to-all-start = ((f32[16,1,3456]{2,1,0:T(1,128)}), f32[16,1,3456]{2,1,0:T(1,128)S(1)}, u32[]{:S(2)}, u32[]{:S(2)}) async-start(f32[16,1,3456]{2,1,0:T(1,128)} %reshape.625), calls=%async_computation | async-start | bytes 442368 | tf_op jit(solution)/shard_map/all_to_all | solution.py:107
  127.1 12.5 %copy-start.22 = (f32[64]{0:T(128)S(1)}, f32[64]{0:T(128)}, u32[]{:S(2)}) copy-start(f32[64]{0:T(128)} %param.23) | copy-start | bytes 772
  127.2 4.4 %collective-permute-start.3 = (f32[9,1,3,32]{3,1,0,2:T(1,128)S(1)}, f32[9,1,3,32]{3,1,0,2:T(1,128)S(1)}, u32[]{:S(2)}, u32[]{:S(2)}) collective-permute-start(f32[9,1,3,32]{3,1,0,2:T(1,128)S(1)} %get-tuple-element.53), channel_id=1, source_target_pairs={{1,0},{2,1},{3,2},{4,3},{5,4},{6,5},{7,6},{8,7},{9,8},{10,9},{11,1... | collective-permute-start | bytes 10376 | tf_op jit(solution)/shard_map/ppermute | solution.py:17
  129.3 8.6 %collective-permute-start.2 = (f32[9,1,3,32]{3,1,0,2:T(1,128)S(1)}, f32[9,1,3,32]{3,1,0,2:T(1,128)S(1)}, u32[]{:S(2)}, u32[]{:S(2)}) collective-permute-start(f32[9,1,3,32]{3,1,0,2:T(1,128)S(1)} %get-tuple-element.52), channel_id=1, source_target_pairs={{0,1},{1,2},{2,3},{3,4},{4,5},{5,6},{6,7},{7,8},{8,9},{9,10},{10,1... | collective-permute-start | bytes 10376 | tf_op jit(solution)/shard_map/ppermute | solution.py:14
  (3 other events, 3.0 us)

commit v4 on v2

--- a/solution.py
+++ b/solution.py
@@ -1,6 +1,8 @@
 import jax
 import jax.numpy as jnp
 from jax import lax
+from jax.experimental import pallas as pl
+from jax.experimental.pallas import tpu as pltpu
 from jax.sharding import PartitionSpec as P
 
 HMAX = 8
@@ -73,23 +75,68 @@
     return (fine == coarse).astype(jnp.float32)
 
 
+def split_dot(left, right, split_left):
+    def parts(value):
+        high = value.astype(jnp.bfloat16)
+        rest = value - high.astype(jnp.float32)
+        middle = rest.astype(jnp.bfloat16)
+        low = (rest - middle.astype(jnp.float32)).astype(jnp.bfloat16)
+        return (high, middle, low)
+
+    total = None
+    if split_left:
+        pieces = [(piece, right.astype(jnp.bfloat16)) for piece in parts(left)]
+    else:
+        pieces = [(left.astype(jnp.bfloat16), piece) for piece in parts(right)]
+    for a, b in pieces:
+        term = jnp.dot(a, b, preferred_element_type=jnp.float32)
+        total = term if total is None else total + term
+    return total
+
+
 def offset_image(wide, offsets, margin, cells_x):
-    _, _, size_y, size_z = wide.shape
-    parts = []
-    for index in range(offsets.shape[0]):
-        offset_value = offsets[index]
-        forward_part = lax.dynamic_slice_in_dim(wide, margin + offset_value, cells_x, 1)
-        backward_part = lax.dynamic_slice_in_dim(wide, margin - offset_value, cells_x, 1)
-        image_block = forward_part[0] * backward_part[1] + forward_part[2] * backward_part[3]
-        parts.append(image_block.reshape(cells_x // 4, 4, size_y, size_z).sum(axis=1))
-    pooled_x = jnp.stack(parts)
-    pooled_z = jnp.einsum(
-        "ixyz,zc->ixyc", pooled_x, pooling(size_z, 4), precision=lax.Precision.HIGHEST
-    )
-    pooled = jnp.einsum(
-        "yb,ixyc->ixbc", pooling(size_y, 4), pooled_z, precision=lax.Precision.HIGHEST
-    )
-    return pooled * (1.0 / 64.0)
+    fields, span_x, size_y, size_z = wide.shape
+    count = offsets.shape[0]
+    blocks_x, blocks_y, blocks_z = cells_x // 4, size_y // 4, size_z // 4
+    pool_z = pooling(size_z, 4)
+    pool_y = (
+        (jnp.arange(blocks_x * size_y)[None, :] // 4) == jnp.arange(blocks_x * blocks_y)[:, None]
+    ).astype(jnp.float32)
+
+    def kernel(offsets_ref, wide_ref, pool_z_ref, pool_y_ref, out_ref):
+        offset_value = offsets_ref[pl.program_id(0)]
+        forward = margin + offset_value
+        backward = margin - offset_value
+        rows = []
+        for block in range(blocks_x):
+            total = None
+            for step in range(4):
+                x = block * 4 + step
+                term = (
+                    wide_ref[0, forward + x] * wide_ref[1, backward + x]
+                    + wide_ref[2, forward + x] * wide_ref[3, backward + x]
+                )
+                total = term if total is None else total + term
+            rows.append(total)
+        pooled_x = jnp.concatenate(rows, axis=0)
+        pooled_z = split_dot(pooled_x, pool_z_ref[...], True)
+        pooled = split_dot(pool_y_ref[...], pooled_z, False)
+        out_ref[0] = (pooled * (1.0 / 64.0)).reshape(blocks_x, blocks_y, blocks_z)
+
+    return pl.pallas_call(
+        kernel,
+        grid_spec=pltpu.PrefetchScalarGridSpec(
+            num_scalar_prefetch=1,
+            grid=(count,),
+            in_specs=[
+                pl.BlockSpec((fields, span_x, size_y, size_z), lambda i, offsets_ref: (0, 0, 0, 0)),
+                pl.BlockSpec((size_z, blocks_z), lambda i, offsets_ref: (0, 0)),
+                pl.BlockSpec((blocks_x * blocks_y, blocks_x * size_y), lambda i, offsets_ref: (0, 0)),
+            ],
+            out_specs=pl.BlockSpec((1, blocks_x, blocks_y, blocks_z), lambda i, offsets_ref: (i, 0, 0, 0)),
+        ),
+        out_shape=jax.ShapeDtypeStruct((count, blocks_x, blocks_y, blocks_z), jnp.float32),
+    )(offsets, wide, pool_z, pool_y)
 
 
 def conv_apply(padded, conv_weight, conv_bias):

time: 119 us -> 110 us (0.924)
  the two profiles are of different devices: /device:TPU:48 before, /device:TPU:56 now
where the time goes in v4:
time: 110 us; the launch traced here: 109 us
  starting transfers between devices  35.8 us (33%)
  waiting for transfers between devices  25.9 us (24%)
  local copies, waits for them, and re-layouts  19.7 us (18%)
  other arithmetic  18.4 us (17%)
  Pallas kernels  8.23 us (7%)
    ppermute x2, waiting for transfers between devices, padded_2(): lax.ppermute(lax.slice_in_dim(block, block.shape[dim] - width, None, axis...  15.8 us
    ppermute x2, starting transfers between devices, padded_2(): lax.ppermute(lax.slice_in_dim(block, 0, width, axis=dim), axis, backward)  13.3 us
    unnamed x76, local copies, waits for them, and re-layouts  11 us
    all_to_all x1, starting transfers between devices, group_sum_windows(): received = lax.all_to_all(windows, axis, 0, 0, tiled=True)  9.52 us
    scatter-add x4, other arithmetic, inject(): jnp.zeros((cells_here * plane_size + 1,), jnp.float32).at[target]  9.44 us
    all_to_all x1, waiting for transfers between devices, group_sum_windows(): received = lax.all_to_all(windows, axis, 0, 0, tiled=True)  8.36 us
    pallas_call x1, Pallas kernels, offset_image(): pl.pallas_call(kernel, grid_spec=pltpu.PrefetchScalarGridSpec(num_scalar_...  8.23 us
    ppermute x1, starting transfers between devices, input_halo(): lax.ppermute(pack(current[:, :2], previous[:, :1], courant[:1]), axis, ba...  7.24 us
  transfers between devices with their start and end apart: 7, of which 4 were waited for; matrix products, arithmetic and copies ran while one was open for 12% of the time, Pallas kernels for 0%

profile of v4, /device:TPU:56, one launch (start us, length us, event | category | flops | bytes accessed | tf_op | source)
XLA Modules:
  0.0 109.1 jit_solution(6179640550977664692)
XLA Ops:
  0.0 1.2 %constant_dynamic-update-slice_fusion.1 = f32[2,16,64,128]{3,2,1,0:T(8,128)S(1)} fusion(f32[1,16,64,128]{3,2,1,0:T(8,128)} %param.13), kind=kLoop, calls=%fused_computation.64 | loop fusion | bytes 1048576
  1.7 1.9 %collective-permute-start = (f32[7,64,128]{2,1,0:T(8,128)S(1)}, f32[7,64,128]{2,1,0:T(8,128)}, u32[]{:S(2)}, u32[]{:S(2)}) collective-permute-start(f32[7,64,128]{2,1,0:T(8,128)S(1)} %pad_maximum_fusion.6), channel_id=1, source_target_pairs={{0,1},{1,2},{2,3},{3,4},{4,5},{5,6},{6,7},{7,8},{8,9},{9,10},{10,1... | collective-permute-start | bytes 688136 | tf_op jit(solution)/shard_map/ppermute | solution.py:40
  4.4 7.2 %collective-permute-start.1 = (f32[7,64,128]{2,1,0:T(8,128)}, f32[7,64,128]{2,1,0:T(8,128)}, u32[]{:S(2)}, u32[]{:S(2)}) collective-permute-start(f32[7,64,128]{2,1,0:T(8,128)} %pad_maximum_fusion.7), channel_id=1, source_target_pairs={{1,0},{2,1},{3,2},{4,3},{5,4},{6,5},{7,6},{8,7},{9,8},{10,9},{11,1... | collective-permute-start | bytes 688136 | tf_op jit(solution)/shard_map/ppermute | solution.py:43
  11.8 4.0 %scatter_custom_fusion.1 = f32[147457]{0:T(1024)S(1)} fusion(s32[512]{0:T(512)S(1)} %bitcast.256, f32[512]{0:T(512)S(1)} %bitcast.258, f32[]{:T(128)} %constant.103.clone.1), kind=kCustom, calls=%fused_computation.48 | custom fusion | flops 512 | bytes 589832 | tf_op jit(solution)/shard_map/scatter-add | solution.py:59
  16.6 4.0 %scatter_custom_fusion.3 = f32[131073]{0:T(1024)S(1)} fusion(s32[512]{0:T(512)S(1)} %bitcast.255, f32[512]{0:T(512)S(1)} %bitcast.257, f32[]{:T(128)} %constant.103.clone.1), kind=kCustom, calls=%fused_computation.52 | custom fusion | flops 512 | bytes 524296 | tf_op jit(solution)/shard_map/scatter-add | solution.py:59
  21.4 1.1 slice.356
  22.5 0.9 slice.360
  23.6 0.9 slice.363
  25.3 0.8 slice_bitcast_fusion.14
  27.0 1.5 %fusion.7 = f32[2,18,64,128]{3,2,1,0:T(8,128)S(1)} fusion(f32[2,18,64,128]{3,2,1,0:T(8,128)S(1)} %pad_maximum_fusion.2, f32[2,1,64,128]{3,2,1,0:T(8,128)S(1)} %slice_bitcast_fusion.14, f32[2,1,64,128]{3,2,1,0:T(8,128)S(1)} %slice_bitcast_fusion.15, f32[2,2,64,128]{3,2,1,0:T(8,128)S(1)} %bitcast.249, ...), kind=kLoop, calls=%fused_computation.27 | loop fusion | flops 5275648 | bytes 6619136 | tf_op jit(solution)/shard_map/add | solution.py:69
  28.6 0.9 slice-done.2
  29.7 0.9 fusion.17
  30.8 1.9 %collective-permute-start.2 = (f32[4,8,64,128]{3,2,1,0:T(8,128)S(1)}, f32[4,8,64,128]{3,2,1,0:T(8,128)S(1)}, u32[]{:S(2)}, u32[]{:S(2)}) collective-permute-start(f32[4,8,64,128]{3,2,1,0:T(8,128)S(1)} %get-tuple-element.11), channel_id=1, source_target_pairs={{0,1},{1,2},{2,3},{3,4},{4,5},{5,6},{6,7},{7,8},{8,9},{9,10},{10,1... | collective-permute-start | bytes 3145736 | tf_op jit(solution)/shard_map/ppermute | solution.py:16
  32.7 7.3 %collective-permute-start.3 = (f32[4,8,64,128]{3,2,1,0:T(8,128)S(1)}, f32[4,8,64,128]{3,2,1,0:T(8,128)S(1)}, u32[]{:S(2)}, u32[]{:S(2)}) collective-permute-start(f32[4,8,64,128]{3,2,1,0:T(8,128)S(1)} %get-tuple-element.12), channel_id=1, source_target_pairs={{1,0},{2,1},{3,2},{4,3},{5,4},{6,5},{7,6},{8,7},{9,8},{10,9},{11,1... | collective-permute-start | bytes 3145736 | tf_op jit(solution)/shard_map/ppermute | solution.py:19
  41.4 9.2 %collective-permute-done.2 = f32[4,8,64,128]{3,2,1,0:T(8,128)S(1)} collective-permute-done((f32[4,8,64,128]{3,2,1,0:T(8,128)S(1)}, f32[4,8,64,128]{3,2,1,0:T(8,128)S(1)}, u32[]{:S(2)}, u32[]{:S(2)}) %collective-permute-start.2) | collective-permute-done | bytes 1048608 | tf_op jit(solution)/shard_map/ppermute | solution.py:16
  50.5 1.8 %collective-permute-done.3 = f32[4,8,64,128]{3,2,1,0:T(8,128)S(1)} collective-permute-done((f32[4,8,64,128]{3,2,1,0:T(8,128)S(1)}, f32[4,8,64,128]{3,2,1,0:T(8,128)S(1)}, u32[]{:S(2)}, u32[]{:S(2)}) %collective-permute-start.3) | collective-permute-done | bytes 1048608 | tf_op jit(solution)/shard_map/ppermute | solution.py:19
  52.3 2.5 %pad_maximum_fusion.wide_ref = f32[4,32,64,128]{3,2,1,0:T(8,128)} fusion(f32[4,8,64,128]{3,2,1,0:T(8,128)S(1)} %collective-permute-done.3, f32[2,16,64,128]{3,2,1,0:T(8,128)S(1)} %fusion.17, f32[2,16,64,128]{3,2,1,0:T(8,128)S(1)} %slice.367, f32[4,8,64,128]{3,2,1,0:T(8,128)S(1)} %collective-permute-done.2), kind=kLoop, calls=%fused_computation.8 | loop fusion | flops 3145728 | bytes 8388608 | tf_op jit(solution)/shard_map/concatenate | solution.py:20
  54.8 8.2 %shard_map.118 = f32[9,4,16,32]{3,2,1,0:T(8,128)} custom-call(s32[9]{0:T(128)} %offsets_ref.1, f32[4,32,64,128]{3,2,1,0:T(8,128)} %pad_maximum_fusion.wide_ref, f32[128,32]{1,0:T(8,128)} %fusion.33.pool_z_ref, f32[64,256]{1,0:T(8,128)} %fusion.34.pool_y_ref), custom_call_target="tpu_custom_call" | custom-call | tf_op jit(solution)/shard_map/pallas_call | solution.py:126
  63.0 1.0 constant_dynamic-update-slice_fusion.17
  64.0 0.9 constant_dynamic-update-slice_fusion.16
  64.9 0.9 constant_dynamic-update-slice_fusion.15
  65.9 0.9 constant_dynamic-update-slice_fusion.14
  66.8 0.9 constant_dynamic-update-slice_fusion.13
  67.7 0.9 constant_dynamic-update-slice_fusion.12
  68.7 0.9 constant_dynamic-update-slice_fusion.11
  70.2 1.3 %reshape.503 = f32[16,1,3456]{2,1,0:T(1,128)} reshape(f32[16,9,3,4,32]{4,3,2,1,0:T(4,128)S(1)} %bitcast.237) | data formatting | bytes 442368
  71.4 9.5 %all-to-all-start = ((f32[16,1,3456]{2,1,0:T(1,128)}), f32[16,1,3456]{2,1,0:T(1,128)S(1)}, u32[]{:S(2)}, u32[]{:S(2)}) async-start(f32[16,1,3456]{2,1,0:T(1,128)} %reshape.503), calls=%async_computation | async-start | bytes 442368 | tf_op jit(solution)/shard_map/all_to_all | solution.py:170
  81.0 8.4 %all-to-all-done = f32[16,1,3456]{2,1,0:T(1,128)S(1)} async-done(((f32[16,1,3456]{2,1,0:T(1,128)}), f32[16,1,3456]{2,1,0:T(1,128)S(1)}, u32[]{:S(2)}, u32[]{:S(2)}) %all-to-all-start) | async-done | bytes 221216 | tf_op jit(solution)/shard_map/all_to_all | solution.py:170
  89.9 1.2 %reduce = f32[16,3456]{1,0:T(8,128)S(1)} reduce(f32[16,1,3456]{2,1,0:T(1,128)S(1)} %all-to-all-done, f32[]{:T(128)} %broadcast.620), dimensions={1}, to_apply=%all_to_all.3.reduce_sub_computation | reduce | bytes 442372 | tf_op jit(solution)/shard_map/all_to_all | solution.py:170
  91.7 6.0 %collective-permute-start.5 = (f32[9,1,3,32]{3,1,0,2:T(1,128)S(1)}, f32[9,1,3,32]{3,1,0,2:T(1,128)S(1)}, u32[]{:S(2)}, u32[]{:S(2)}) collective-permute-start(f32[9,1,3,32]{3,1,0,2:T(1,128)S(1)} %get-tuple-element.23), channel_id=1, source_target_pairs={{1,0},{2,1},{3,2},{4,3},{5,4},{6,5},{7,6},{8,7},{9,8},{10,9},{11,1... | collective-permute-start | bytes 10376 | tf_op jit(solution)/shard_map/ppermute | solution.py:19
  97.7 1.9 %collective-permute-start.4 = (f32[9,1,3,32]{3,1,0,2:T(1,128)S(1)}, f32[9,1,3,32]{3,1,0,2:T(1,128)S(1)}, u32[]{:S(2)}, u32[]{:S(2)}) collective-permute-start(f32[9,1,3,32]{3,1,0,2:T(1,128)S(1)} %get-tuple-element.22), channel_id=1, source_target_pairs={{0,1},{1,2},{2,3},{3,4},{4,5},{5,6},{6,7},{7,8},{8,9},{9,10},{10,1... | collective-permute-start | bytes 10376 | tf_op jit(solution)/shard_map/ppermute | solution.py:16
  99.7 6.6 %collective-permute-done.4 = f32[9,1,3,32]{3,1,0,2:T(1,128)S(1)} collective-permute-done((f32[9,1,3,32]{3,1,0,2:T(1,128)S(1)}, f32[9,1,3,32]{3,1,0,2:T(1,128)S(1)}, u32[]{:S(2)}, u32[]{:S(2)}) %collective-permute-start.4) | collective-permute-done | bytes 3488 | tf_op jit(solution)/shard_map/ppermute | solution.py:16
  (118 shorter events, 10.6 us)
Async XLA Ops:
  0.0 1.3 %copy-start.10 = (f32[1,16,64,128]{3,2,1,0:T(8,128)S(1)}, f32[1,16,64,128]{3,2,1,0:T(8,128)}, u32[]{:S(2)}) copy-start(f32[1,16,64,128]{3,2,1,0:T(8,128)} %param.15) | copy-start | bytes 1572868
  0.0 1.4 %copy-start.1 = (f32[16,64,128]{2,1,0:T(8,128)S(1)}, f32[16,64,128]{2,1,0:T(8,128)}, u32[]{:S(2)}) copy-start(f32[16,64,128]{2,1,0:T(8,128)} %param.16) | copy-start | bytes 1572868
  0.0 1.5 %copy-start.8 = (f32[1,16,64,128]{3,2,1,0:T(8,128)S(1)}, f32[1,16,64,128]{3,2,1,0:T(8,128)}, u32[]{:S(2)}) copy-start(f32[1,16,64,128]{3,2,1,0:T(8,128)} %param.12) | copy-start | bytes 1572868
  0.0 1.7 %copy-start.6 = (f32[1,16,64,128]{3,2,1,0:T(8,128)S(1)}, f32[1,16,64,128]{3,2,1,0:T(8,128)}, u32[]{:S(2)}) copy-start(f32[1,16,64,128]{3,2,1,0:T(8,128)} %param.14) | copy-start | bytes 1572868
  1.4 10.3 %copy-start.13 = (s32[1,512]{1,0:T(1,128)S(1)}, s32[1,512]{1,0:T(1,128)}, u32[]{:S(2)}) copy-start(s32[1,512]{1,0:T(1,128)} %param.19) | copy-start | bytes 6148
  1.4 10.3 %copy-start.12 = (f32[1,2,512]{2,1,0:T(2,128)S(1)}, f32[1,2,512]{2,1,0:T(2,128)}, u32[]{:S(2)}) copy-start(f32[1,2,512]{2,1,0:T(2,128)} %param.20) | copy-start | bytes 12292
  1.4 10.3 %copy-start.16 = (s32[1,8]{1,0:T(1,128)S(1)}, s32[1,8]{1,0:T(1,128)}, u32[]{:S(2)}) copy-start(s32[1,8]{1,0:T(1,128)} %param.17) | copy-start | bytes 100
  1.7 14.1 %copy-start.14 = (f32[1,2,8]{2,1,0:T(2,128)S(1)}, f32[1,2,8]{2,1,0:T(2,128)}, u32[]{:S(2)}) copy-start(f32[1,2,8]{2,1,0:T(2,128)} %param.18) | copy-start | bytes 196
  1.7 19.7 %collective-permute-start = (f32[7,64,128]{2,1,0:T(8,128)S(1)}, f32[7,64,128]{2,1,0:T(8,128)}, u32[]{:S(2)}, u32[]{:S(2)}) collective-permute-start(f32[7,64,128]{2,1,0:T(8,128)S(1)} %pad_maximum_fusion.6), channel_id=1, source_target_pairs={{0,1},{1,2},{2,3},{3,4},{4,5},{5,6},{6,7},{7,8},{8,9},{9,10},{10,1... | collective-permute-start | bytes 688136 | tf_op jit(solution)/shard_map/ppermute | solution.py:40
  4.4 18.1 %collective-permute-start.1 = (f32[7,64,128]{2,1,0:T(8,128)}, f32[7,64,128]{2,1,0:T(8,128)}, u32[]{:S(2)}, u32[]{:S(2)}) collective-permute-start(f32[7,64,128]{2,1,0:T(8,128)} %pad_maximum_fusion.7), channel_id=1, source_target_pairs={{1,0},{2,1},{3,2},{4,3},{5,4},{6,5},{7,6},{8,7},{9,8},{10,9},{11,1... | collective-permute-start | bytes 688136 | tf_op jit(solution)/shard_map/ppermute | solution.py:43
  15.8 0.8 copy-start.2
  16.5 4.1 %copy-start.3 = (f32[147457]{0:T(1024)}, f32[147457]{0:T(1024)S(1)}, u32[]{:S(2)}) copy-start(f32[147457]{0:T(1024)S(1)} %scatter_custom_fusion) | copy-start | bytes 1769488
  20.6 0.8 copy-start.5
  21.4 2.2 %copy-start.4 = (f32[131073]{0:T(1024)}, f32[131073]{0:T(1024)S(1)}, u32[]{:S(2)}) copy-start(f32[131073]{0:T(1024)S(1)} %scatter_custom_fusion.2) | copy-start | bytes 1572880
  23.4 3.6 %copy-start.7 = (f32[1,16,64,128]{3,2,1,0:T(8,128)S(1)}, f32[1,16,64,128]{3,2,1,0:T(8,128)}, u32[]{:S(2)}) copy-start(f32[1,16,64,128]{3,2,1,0:T(8,128)} %param.14) | copy-start | bytes 1572868
  23.4 3.6 %copy-start.9 = (f32[1,16,64,128]{3,2,1,0:T(8,128)S(1)}, f32[1,16,64,128]{3,2,1,0:T(8,128)}, u32[]{:S(2)}) copy-start(f32[1,16,64,128]{3,2,1,0:T(8,128)} %param.12) | copy-start | bytes 1572868
  23.5 3.4 %slice-start = ((f32[147457]{0:T(1024)}), f32[147456]{0:T(1024)S(1)}, s32[]{:S(2)}) async-start(f32[147457]{0:T(1024)} %copy-done.2), calls=%async_computation.1 | async-start | bytes 1179648 | tf_op jit(solution)/shard_map/slice | solution.py:60
  23.6 3.4 %slice-start.1 = ((f32[147457]{0:T(1024)}), f32[147456]{0:T(1024)S(1)}, s32[]{:S(2)}) async-start(f32[147457]{0:T(1024)} %copy-done.3), calls=%async_computation.2 | async-start | bytes 1179648 | tf_op jit(solution)/shard_map/slice | solution.py:60
  28.5 1.0 slice-start.2
  28.5 1.2 %slice-start.3 = ((f32[131073]{0:T(1024)}), f32[131072]{0:T(1024)S(1)}, s32[]{:S(2)}) async-start(f32[131073]{0:T(1024)} %copy-done.5), calls=%async_computation.4 | async-start | bytes 1048576 | tf_op jit(solution)/shard_map/slice | solution.py:60
  30.8 19.7 %collective-permute-start.2 = (f32[4,8,64,128]{3,2,1,0:T(8,128)S(1)}, f32[4,8,64,128]{3,2,1,0:T(8,128)S(1)}, u32[]{:S(2)}, u32[]{:S(2)}) collective-permute-start(f32[4,8,64,128]{3,2,1,0:T(8,128)S(1)} %get-tuple-element.11), channel_id=1, source_target_pairs={{0,1},{1,2},{2,3},{3,4},{4,5},{5,6},{6,7},{7,8},{8,9},{9,10},{10,1... | collective-permute-start | bytes 3145736 | tf_op jit(solution)/shard_map/ppermute | solution.py:16
  32.7 19.6 %collective-permute-start.3 = (f32[4,8,64,128]{3,2,1,0:T(8,128)S(1)}, f32[4,8,64,128]{3,2,1,0:T(8,128)S(1)}, u32[]{:S(2)}, u32[]{:S(2)}) collective-permute-start(f32[4,8,64,128]{3,2,1,0:T(8,128)S(1)} %get-tuple-element.12), channel_id=1, source_target_pairs={{1,0},{2,1},{3,2},{4,3},{5,4},{6,5},{7,6},{8,7},{9,8},{10,9},{11,1... | collective-permute-start | bytes 3145736 | tf_op jit(solution)/shard_map/ppermute | solution.py:19
  63.0 6.6 %copy-start = (f32[9,4,16,32]{3,2,1,0:T(8,128)S(1)}, f32[9,4,16,32]{3,2,1,0:T(8,128)}, u32[]{:S(2)}) copy-start(f32[9,4,16,32]{3,2,1,0:T(8,128)} %shard_map.118) | copy-start | bytes 221188
  70.2 10.8 %copy-start.11 = (f32[64,9,3,3,3]{0,4,3,2,1:T(4,128)S(1)}, f32[64,9,3,3,3]{0,4,3,2,1:T(4,128)}, u32[]{:S(2)}) copy-start(f32[64,9,3,3,3]{0,4,3,2,1:T(4,128)} %param.22) | copy-start | bytes 186628
  71.4 18.0 %all-to-all-start = ((f32[16,1,3456]{2,1,0:T(1,128)}), f32[16,1,3456]{2,1,0:T(1,128)S(1)}, u32[]{:S(2)}, u32[]{:S(2)}) async-start(f32[16,1,3456]{2,1,0:T(1,128)} %reshape.503), calls=%async_computation | async-start | bytes 442368 | tf_op jit(solution)/shard_map/all_to_all | solution.py:170
  91.7 8.0 %collective-permute-start.5 = (f32[9,1,3,32]{3,1,0,2:T(1,128)S(1)}, f32[9,1,3,32]{3,1,0,2:T(1,128)S(1)}, u32[]{:S(2)}, u32[]{:S(2)}) collective-permute-start(f32[9,1,3,32]{3,1,0,2:T(1,128)S(1)} %get-tuple-element.23), channel_id=1, source_target_pairs={{1,0},{2,1},{3,2},{4,3},{5,4},{6,5},{7,6},{8,7},{9,8},{10,9},{11,1... | collective-permute-start | bytes 10376 | tf_op jit(solution)/shard_map/ppermute | solution.py:19
  97.7 8.6 %collective-permute-start.4 = (f32[9,1,3,32]{3,1,0,2:T(1,128)S(1)}, f32[9,1,3,32]{3,1,0,2:T(1,128)S(1)}, u32[]{:S(2)}, u32[]{:S(2)}) collective-permute-start(f32[9,1,3,32]{3,1,0,2:T(1,128)S(1)} %get-tuple-element.22), channel_id=1, source_target_pairs={{0,1},{1,2},{2,3},{3,4},{4,5},{5,6},{6,7},{7,8},{8,9},{9,10},{10,1... | collective-permute-start | bytes 10376 | tf_op jit(solution)/shard_map/ppermute | solution.py:16
  106.8 1.2 %copy-start.15 = (f32[64]{0:T(128)S(1)}, f32[64]{0:T(128)}, u32[]{:S(2)}) copy-start(f32[64]{0:T(128)} %param.23) | copy-start | bytes 772

commit v5 on v4

--- a/solution.py
+++ b/solution.py
@@ -165,10 +165,11 @@
     rows = coarse.shape[2] // count
     rimmed = jnp.pad(coarse, ((0, 0), (0, 0), (1, 1), (0, 0)))
     windows = jnp.stack(
-        [lax.slice_in_dim(rimmed, member * rows, member * rows + rows + 2, axis=2) for member in range(count)]
-    )
+        [lax.slice_in_dim(rimmed, k, k + (count - 1) * rows + 1, stride=rows, axis=2) for k in range(rows + 2)]
+    )
+    windows = jnp.moveaxis(windows, 3, 0)
     received = lax.all_to_all(windows, axis, 0, 0, tiled=True)
-    return received.sum(axis=0)
+    return jnp.moveaxis(received.sum(axis=0), 0, 2)
 
 
 def local(
@@ -211,11 +212,10 @@
         levels.append(advanced)
     levels[0] = levels[0][:, 1:-1]
     fields = jnp.concatenate(levels, axis=0)
-    wide = padded_2(fields, (("gx", 1),), HMAX)
-    coarse = offset_image(wide, offsets, HMAX, cells_x)
+    wide = padded_2(fields, (("gx", 1),), HMAX + 4)
+    coarse = offset_image(wide, offsets, HMAX, cells_x + 8)
     summed = group_sum_windows(coarse, "shot")
-    rimmed = padded_2(summed, (("gx", 1),), 1)
-    window = jnp.pad(rimmed, ((0, 0), (0, 0), (0, 0), (1, 1)))
+    window = jnp.pad(summed, ((0, 0), (0, 0), (0, 0), (1, 1)))
     return conv_apply(window, conv_weight, conv_bias)
 
 

time: 110 us -> 100 us (0.909)
  the two profiles are of different devices: /device:TPU:56 before, /device:TPU:39 now
where the time goes in v5:
time: 100 us; the launch traced here: 99.8 us
  waiting for transfers between devices  30.6 us (31%)
  starting transfers between devices  24.5 us (24%)
  other arithmetic  18.9 us (19%)
  local copies, waits for them, and re-layouts  15.3 us (15%)
  Pallas kernels  9.58 us (10%)
    ppermute x1, waiting for transfers between devices, padded_2(): lax.ppermute(lax.slice_in_dim(block, block.shape[dim] - width, None, axis...  14 us
    pallas_call x1, Pallas kernels, offset_image(): pl.pallas_call(kernel, grid_spec=pltpu.PrefetchScalarGridSpec(num_scalar_...  9.58 us
    scatter-add x4, other arithmetic, inject(): jnp.zeros((cells_here * plane_size + 1,), jnp.float32).at[target]  9.54 us
    all_to_all x1, waiting for transfers between devices, group_sum_windows(): received = lax.all_to_all(windows, axis, 0, 0, tiled=True)  8.57 us
    all_to_all x1, starting transfers between devices, group_sum_windows(): received = lax.all_to_all(windows, axis, 0, 0, tiled=True)  8.28 us
    ppermute x1, waiting for transfers between devices, padded_2(): lax.ppermute(lax.slice_in_dim(block, 0, width, axis=dim), axis, backward)  8.01 us
    ppermute x1, starting transfers between devices, padded_2(): lax.ppermute(lax.slice_in_dim(block, block.shape[dim] - width, None, axis...  7.11 us
    unnamed x61, local copies, waits for them, and re-layouts  5.3 us
  transfers between devices with their start and end apart: 5, of which 3 were waited for; matrix products, arithmetic and copies ran while one was open for 13% of the time, Pallas kernels for 0%

profile of v5, /device:TPU:39, one launch (start us, length us, event | category | flops | bytes accessed | tf_op | source)
XLA Modules:
  0.0 99.8 jit_solution(4450365590441423573)
XLA Ops:
  0.0 1.2 %constant_dynamic-update-slice_fusion.1 = f32[2,16,64,128]{3,2,1,0:T(8,128)S(1)} fusion(f32[1,16,64,128]{3,2,1,0:T(8,128)} %param.13), kind=kLoop, calls=%fused_computation.72 | loop fusion | bytes 1048576
  1.7 5.3 %collective-permute-start = (f32[7,64,128]{2,1,0:T(8,128)S(1)}, f32[7,64,128]{2,1,0:T(8,128)}, u32[]{:S(2)}, u32[]{:S(2)}) collective-permute-start(f32[7,64,128]{2,1,0:T(8,128)S(1)} %pad_maximum_fusion.6), channel_id=1, source_target_pairs={{0,1},{1,2},{2,3},{3,4},{4,5},{5,6},{6,7},{7,8},{8,9},{9,10},{10,1... | collective-permute-start | bytes 688136 | tf_op jit(solution)/shard_map/ppermute | solution.py:40
  7.0 0.7 pad_maximum_fusion.7
  7.7 1.9 %collective-permute-start.1 = (f32[7,64,128]{2,1,0:T(8,128)}, f32[7,64,128]{2,1,0:T(8,128)}, u32[]{:S(2)}, u32[]{:S(2)}) collective-permute-start(f32[7,64,128]{2,1,0:T(8,128)} %pad_maximum_fusion.7), channel_id=1, source_target_pairs={{1,0},{2,1},{3,2},{4,3},{5,4},{6,5},{7,6},{8,7},{9,8},{10,9},{11,1... | collective-permute-start | bytes 688136 | tf_op jit(solution)/shard_map/ppermute | solution.py:43
  9.8 4.0 %scatter_custom_fusion.1 = f32[147457]{0:T(1024)S(1)} fusion(s32[512]{0:T(512)S(1)} %bitcast.240, f32[512]{0:T(512)S(1)} %bitcast.242, f32[]{:T(128)} %constant.103.clone.1), kind=kCustom, calls=%fused_computation.51 | custom fusion | flops 512 | bytes 589832 | tf_op jit(solution)/shard_map/scatter-add | solution.py:59
  13.9 0.8 scatter_custom_fusion
  14.7 4.0 %scatter_custom_fusion.3 = f32[131073]{0:T(1024)S(1)} fusion(s32[512]{0:T(512)S(1)} %bitcast.239, f32[512]{0:T(512)S(1)} %bitcast.241, f32[]{:T(128)} %constant.103.clone.1), kind=kCustom, calls=%fused_computation.55 | custom fusion | flops 512 | bytes 524296 | tf_op jit(solution)/shard_map/scatter-add | solution.py:59
  18.7 0.7 scatter_custom_fusion.2
  19.5 1.1 %slice.270 = f32[4,64,128]{2,1,0:T(8,128)S(1)} slice(f32[7,64,128]{2,1,0:T(8,128)} %collective-permute-done), slice={[0:4], [0:64], [0:128]} | slice | bytes 262144 | tf_op jit(solution)/shard_map/slice | solution.py:36
  20.6 0.9 slice.274
  21.7 0.9 slice.277
  22.5 0.8 slice.278
  23.3 0.8 slice_bitcast_fusion
  24.2 0.8 slice_bitcast_fusion.1
  25.0 1.5 %fusion.8 = f32[2,18,64,128]{3,2,1,0:T(8,128)S(1)} fusion(f32[2,18,64,128]{3,2,1,0:T(8,128)S(1)} %pad_maximum_fusion.3, f32[2,1,64,128]{3,2,1,0:T(8,128)S(1)} %slice_bitcast_fusion, f32[2,1,64,128]{3,2,1,0:T(8,128)S(1)} %slice_bitcast_fusion.1, f32[2,2,64,128]{3,2,1,0:T(8,128)S(1)} %bitcast.236, f32[2,16,64,128]{3,2,1,0:T(8,128)S(1)} %constant_dynamic-update-slice_fusion, ...), kind=kLoop, calls=%fused_computation.30 | loop fusion | flops 5275648 | bytes 6619136 | tf_op jit(solution)/shard_map/add | solution.py:69
  26.6 0.9 slice-done.2
  27.7 0.9 fusion.17
  28.9 7.1 %collective-permute-start.2 = (f32[4,12,64,128]{3,2,1,0:T(8,128)S(1)}, f32[4,12,64,128]{3,2,1,0:T(8,128)S(1)}, u32[]{:S(2)}, u32[]{:S(2)}) collective-permute-start(f32[4,12,64,128]{3,2,1,0:T(8,128)S(1)} %get-tuple-element.11), channel_id=1, source_target_pairs={{0,1},{1,2},{2,3},{3,4},{4,5},{5,6},{6,7},{7,8},{8,9},{9,10},{10,1... | collective-permute-start | bytes 4718600 | tf_op jit(solution)/shard_map/ppermute | solution.py:16
  36.0 1.9 %collective-permute-start.3 = (f32[4,12,64,128]{3,2,1,0:T(8,128)S(1)}, f32[4,12,64,128]{3,2,1,0:T(8,128)S(1)}, u32[]{:S(2)}, u32[]{:S(2)}) collective-permute-start(f32[4,12,64,128]{3,2,1,0:T(8,128)S(1)} %get-tuple-element.12), channel_id=1, source_target_pairs={{1,0},{2,1},{3,2},{4,3},{5,4},{6,5},{7,6},{8,7},{9,8},{10,9},{11,1... | collective-permute-start | bytes 4718600 | tf_op jit(solution)/shard_map/ppermute | solution.py:19
  38.0 0.7 fusion.33.pool_z_ref
  38.7 0.7 fusion.28.pool_y_ref
  39.4 14.0 %collective-permute-done.2 = f32[4,12,64,128]{3,2,1,0:T(8,128)S(1)} collective-permute-done((f32[4,12,64,128]{3,2,1,0:T(8,128)S(1)}, f32[4,12,64,128]{3,2,1,0:T(8,128)S(1)}, u32[]{:S(2)}, u32[]{:S(2)}) %collective-permute-start.2) | collective-permute-done | bytes 1572896 | tf_op jit(solution)/shard_map/ppermute | solution.py:16
  53.3 8.0 %collective-permute-done.3 = f32[4,12,64,128]{3,2,1,0:T(8,128)S(1)} collective-permute-done((f32[4,12,64,128]{3,2,1,0:T(8,128)S(1)}, f32[4,12,64,128]{3,2,1,0:T(8,128)S(1)}, u32[]{:S(2)}, u32[]{:S(2)}) %collective-permute-start.3) | collective-permute-done | bytes 1572896 | tf_op jit(solution)/shard_map/ppermute | solution.py:19
  61.4 2.6 %pad_maximum_fusion.wide_ref = f32[4,40,64,128]{3,2,1,0:T(8,128)} fusion(f32[4,12,64,128]{3,2,1,0:T(8,128)S(1)} %collective-permute-done.3, f32[2,16,64,128]{3,2,1,0:T(8,128)S(1)} %fusion.17, f32[2,16,64,128]{3,2,1,0:T(8,128)S(1)} %slice.281, f32[4,12,64,128]{3,2,1,0:T(8,128)S(1)} %collective-permute-done.2), kind=kLoop, calls=%fused_computation.4 | loop fusion | flops 3932160 | bytes 10485760 | tf_op jit(solution)/shard_map/concatenate | solution.py:20
  64.0 9.6 %shard_map.118 = f32[9,6,16,32]{3,2,1,0:T(8,128)} custom-call(s32[9]{0:T(128)} %offsets_ref.1, f32[4,40,64,128]{3,2,1,0:T(8,128)} %pad_maximum_fusion.wide_ref, f32[128,32]{1,0:T(8,128)} %fusion.33.pool_z_ref, f32[96,384]{1,0:T(8,128)} %fusion.28.pool_y_ref), custom_call_target="tpu_custom_call" | custom-call | tf_op jit(solution)/shard_map/pallas_call | solution.py:126
  73.6 1.3 %fusion.18 = (f32[1,9,6,16,32]{4,3,2,1,0:T(8,128)S(1)}, f32[1,9,6,16,32]{4,3,2,1,0:T(8,128)S(1)}) fusion(f32[9,6,16,32]{3,2,1,0:T(8,128)} %shard_map.118), kind=kLoop, calls=%fused_computation.49 | loop fusion | bytes 331776 | tf_op jit(solution)/shard_map/stack | solution.py:167
  75.5 1.5 %reshape.503 = f32[16,1,5184]{2,1,0:T(1,128)} reshape(f32[16,3,9,6,32]{4,3,2,1,0:T(8,128)S(1)} %copy.50) | data formatting | bytes 663552
  77.0 8.3 %all-to-all-start = ((f32[16,1,5184]{2,1,0:T(1,128)}), f32[16,1,5184]{2,1,0:T(1,128)S(1)}, u32[]{:S(2)}, u32[]{:S(2)}) async-start(f32[16,1,5184]{2,1,0:T(1,128)} %reshape.503), calls=%async_computation | async-start | bytes 671744 | tf_op jit(solution)/shard_map/all_to_all | solution.py:171
  85.4 8.6 %all-to-all-done = f32[16,1,5184]{2,1,0:T(1,128)S(1)} async-done(((f32[16,1,5184]{2,1,0:T(1,128)}), f32[16,1,5184]{2,1,0:T(1,128)S(1)}, u32[]{:S(2)}, u32[]{:S(2)}) %all-to-all-start) | async-done | bytes 331808 | tf_op jit(solution)/shard_map/all_to_all | solution.py:171
  94.5 1.4 %reduce = f32[16,5184]{1,0:T(8,128)S(1)} reduce(f32[16,1,5184]{2,1,0:T(1,128)S(1)} %all-to-all-done, f32[]{:T(128)} %broadcast.608), dimensions={1}, to_apply=%all_to_all.3.reduce_sub_computation | reduce | bytes 663556 | tf_op jit(solution)/shard_map/all_to_all | solution.py:171
  95.9 0.5 reshape.504
  99.1 0.7 copy.77
  (92 shorter events, 4.9 us)
Async XLA Ops:
  0.0 1.2 %copy-start.9 = (f32[1,16,64,128]{3,2,1,0:T(8,128)S(1)}, f32[1,16,64,128]{3,2,1,0:T(8,128)}, u32[]{:S(2)}) copy-start(f32[1,16,64,128]{3,2,1,0:T(8,128)} %param.15) | copy-start | bytes 1572868
  0.0 1.4 %copy-start.1 = (f32[16,64,128]{2,1,0:T(8,128)S(1)}, f32[16,64,128]{2,1,0:T(8,128)}, u32[]{:S(2)}) copy-start(f32[16,64,128]{2,1,0:T(8,128)} %param.16) | copy-start | bytes 1572868
  0.0 1.5 %copy-start.7 = (f32[1,16,64,128]{3,2,1,0:T(8,128)S(1)}, f32[1,16,64,128]{3,2,1,0:T(8,128)}, u32[]{:S(2)}) copy-start(f32[1,16,64,128]{3,2,1,0:T(8,128)} %param.12) | copy-start | bytes 1572868
  0.0 1.7 %copy-start.6 = (f32[1,16,64,128]{3,2,1,0:T(8,128)S(1)}, f32[1,16,64,128]{3,2,1,0:T(8,128)}, u32[]{:S(2)}) copy-start(f32[1,16,64,128]{3,2,1,0:T(8,128)} %param.14) | copy-start | bytes 1572868
  1.4 8.3 %copy-start.12 = (s32[1,512]{1,0:T(1,128)S(1)}, s32[1,512]{1,0:T(1,128)}, u32[]{:S(2)}) copy-start(s32[1,512]{1,0:T(1,128)} %param.19) | copy-start | bytes 6148
  1.4 8.4 %copy-start.11 = (f32[1,2,512]{2,1,0:T(2,128)S(1)}, f32[1,2,512]{2,1,0:T(2,128)}, u32[]{:S(2)}) copy-start(f32[1,2,512]{2,1,0:T(2,128)} %param.20) | copy-start | bytes 12292
  1.4 8.4 %copy-start.15 = (s32[1,8]{1,0:T(1,128)S(1)}, s32[1,8]{1,0:T(1,128)}, u32[]{:S(2)}) copy-start(s32[1,8]{1,0:T(1,128)} %param.17) | copy-start | bytes 100
  1.7 12.1 %copy-start.13 = (f32[1,2,8]{2,1,0:T(2,128)S(1)}, f32[1,2,8]{2,1,0:T(2,128)}, u32[]{:S(2)}) copy-start(f32[1,2,8]{2,1,0:T(2,128)} %param.18) | copy-start | bytes 196
  1.7 17.8 %collective-permute-start = (f32[7,64,128]{2,1,0:T(8,128)S(1)}, f32[7,64,128]{2,1,0:T(8,128)}, u32[]{:S(2)}, u32[]{:S(2)}) collective-permute-start(f32[7,64,128]{2,1,0:T(8,128)S(1)} %pad_maximum_fusion.6), channel_id=1, source_target_pairs={{0,1},{1,2},{2,3},{3,4},{4,5},{5,6},{6,7},{7,8},{8,9},{9,10},{10,1... | collective-permute-start | bytes 688136 | tf_op jit(solution)/shard_map/ppermute | solution.py:40
  7.7 12.9 %collective-permute-start.1 = (f32[7,64,128]{2,1,0:T(8,128)}, f32[7,64,128]{2,1,0:T(8,128)}, u32[]{:S(2)}, u32[]{:S(2)}) collective-permute-start(f32[7,64,128]{2,1,0:T(8,128)} %pad_maximum_fusion.7), channel_id=1, source_target_pairs={{1,0},{2,1},{3,2},{4,3},{5,4},{6,5},{7,6},{8,7},{9,8},{10,9},{11,1... | collective-permute-start | bytes 688136 | tf_op jit(solution)/shard_map/ppermute | solution.py:43
  13.8 0.8 copy-start.2
  14.6 4.1 %copy-start.3 = (f32[147457]{0:T(1024)}, f32[147457]{0:T(1024)S(1)}, u32[]{:S(2)}) copy-start(f32[147457]{0:T(1024)S(1)} %scatter_custom_fusion) | copy-start | bytes 1769488
  18.7 0.8 copy-start.4
  19.5 2.2 %copy-start.5 = (f32[131073]{0:T(1024)}, f32[131073]{0:T(1024)S(1)}, u32[]{:S(2)}) copy-start(f32[131073]{0:T(1024)S(1)} %scatter_custom_fusion.2) | copy-start | bytes 1572880
  21.5 3.5 %copy-start.8 = (f32[1,16,64,128]{3,2,1,0:T(8,128)S(1)}, f32[1,16,64,128]{3,2,1,0:T(8,128)}, u32[]{:S(2)}) copy-start(f32[1,16,64,128]{3,2,1,0:T(8,128)} %param.12) | copy-start | bytes 1572868
  21.6 3.4 %slice-start = ((f32[147457]{0:T(1024)}), f32[147456]{0:T(1024)S(1)}, s32[]{:S(2)}) async-start(f32[147457]{0:T(1024)} %copy-done.2), calls=%async_computation.1 | async-start | bytes 1179648 | tf_op jit(solution)/shard_map/slice | solution.py:60
  21.6 3.4 %slice-start.1 = ((f32[147457]{0:T(1024)}), f32[147456]{0:T(1024)S(1)}, s32[]{:S(2)}) async-start(f32[147457]{0:T(1024)} %copy-done.3), calls=%async_computation.2 | async-start | bytes 1179648 | tf_op jit(solution)/shard_map/slice | solution.py:60
  26.5 1.0 %slice-start.2 = ((f32[131073]{0:T(1024)}), f32[131072]{0:T(1024)S(1)}, s32[]{:S(2)}) async-start(f32[131073]{0:T(1024)} %copy-done.4), calls=%async_computation.3 | async-start | bytes 1048576 | tf_op jit(solution)/shard_map/slice | solution.py:60
  26.5 1.2 %slice-start.3 = ((f32[131073]{0:T(1024)}), f32[131072]{0:T(1024)S(1)}, s32[]{:S(2)}) async-start(f32[131073]{0:T(1024)} %copy-done.5), calls=%async_computation.4 | async-start | bytes 1048576 | tf_op jit(solution)/shard_map/slice | solution.py:60
  28.9 24.5 %collective-permute-start.2 = (f32[4,12,64,128]{3,2,1,0:T(8,128)S(1)}, f32[4,12,64,128]{3,2,1,0:T(8,128)S(1)}, u32[]{:S(2)}, u32[]{:S(2)}) collective-permute-start(f32[4,12,64,128]{3,2,1,0:T(8,128)S(1)} %get-tuple-element.11), channel_id=1, source_target_pairs={{0,1},{1,2},{2,3},{3,4},{4,5},{5,6},{6,7},{7,8},{8,9},{9,10},{10,1... | collective-permute-start | bytes 4718600 | tf_op jit(solution)/shard_map/ppermute | solution.py:16
  36.0 25.3 %collective-permute-start.3 = (f32[4,12,64,128]{3,2,1,0:T(8,128)S(1)}, f32[4,12,64,128]{3,2,1,0:T(8,128)S(1)}, u32[]{:S(2)}, u32[]{:S(2)}) collective-permute-start(f32[4,12,64,128]{3,2,1,0:T(8,128)S(1)} %get-tuple-element.12), channel_id=1, source_target_pairs={{1,0},{2,1},{3,2},{4,3},{5,4},{6,5},{7,6},{8,7},{9,8},{10,9},{11,1... | collective-permute-start | bytes 4718600 | tf_op jit(solution)/shard_map/ppermute | solution.py:19
  73.6 1.3 %copy-start = (f32[9,6,16,32]{3,2,1,0:T(8,128)S(1)}, f32[9,6,16,32]{3,2,1,0:T(8,128)}, u32[]{:S(2)}) copy-start(f32[9,6,16,32]{3,2,1,0:T(8,128)} %shard_map.118) | copy-start | bytes 331780
  75.5 9.8 %copy-start.10 = (f32[64,9,3,3,3]{0,4,3,2,1:T(4,128)S(1)}, f32[64,9,3,3,3]{0,4,3,2,1:T(4,128)}, u32[]{:S(2)}) copy-start(f32[64,9,3,3,3]{0,4,3,2,1:T(4,128)} %param.22) | copy-start | bytes 186628
  77.0 16.9 %all-to-all-start = ((f32[16,1,5184]{2,1,0:T(1,128)}), f32[16,1,5184]{2,1,0:T(1,128)S(1)}, u32[]{:S(2)}, u32[]{:S(2)}) async-start(f32[16,1,5184]{2,1,0:T(1,128)} %reshape.503), calls=%async_computation | async-start | bytes 671744 | tf_op jit(solution)/shard_map/all_to_all | solution.py:171
  97.2 1.5 %copy-start.14 = (f32[64]{0:T(128)S(1)}, f32[64]{0:T(128)}, u32[]{:S(2)}) copy-start(f32[64]{0:T(128)} %param.23) | copy-start | bytes 772

commit v6 on v5

--- a/solution.py
+++ b/solution.py
@@ -49,15 +49,37 @@
     return current_wide, previous_wide, courant_wide
 
 
+def bf16_parts(value):
+    high = value.astype(jnp.bfloat16)
+    rest = value - high.astype(jnp.float32)
+    middle = rest.astype(jnp.bfloat16)
+    low = (rest - middle.astype(jnp.float32)).astype(jnp.bfloat16)
+    return (high, middle, low)
+
+
+def rounded_parts(value):
+    high = lax.reduce_precision(value, exponent_bits=8, mantissa_bits=7)
+    rest = value - high
+    middle = lax.reduce_precision(rest, exponent_bits=8, mantissa_bits=7)
+    low = rest - middle
+    return (high.astype(jnp.bfloat16), middle.astype(jnp.bfloat16), low.astype(jnp.bfloat16))
+
+
 def inject(cells_here, first_x, cell_index, amplitudes, size_y, size_z):
     plane_size = size_y * size_z
     column = cell_index // plane_size
     within = cell_index % plane_size
-    local_x = column - first_x
-    inside = (local_x >= 0) & (local_x < cells_here)
-    target = jnp.where(inside, local_x * plane_size + within, cells_here * plane_size)
-    flat_cells = jnp.zeros((cells_here * plane_size + 1,), jnp.float32).at[target].add(amplitudes)
-    return flat_cells[:-1].reshape(cells_here, size_y, size_z)
+    row = (column - first_x) * size_y + within // size_z
+    rows = (jnp.arange(cells_here * size_y)[:, None] == row[None, :]).astype(jnp.bfloat16)
+    at_z = jnp.arange(size_z)[None, :] == (within % size_z)[:, None]
+    fields = []
+    for amplitude in amplitudes:
+        placed = jnp.where(at_z, amplitude[:, None], 0.0)
+        parts = jnp.concatenate(rounded_parts(placed), axis=1)
+        sums = jnp.dot(rows, parts, preferred_element_type=jnp.float32)
+        total = sums[:, :size_z] + sums[:, size_z : 2 * size_z] + sums[:, 2 * size_z :]
+        fields.append(total.reshape(cells_here, size_y, size_z))
+    return fields
 
 
 def laplace_step(previous, extended, courant, sources):
@@ -76,18 +98,11 @@
 
 
 def split_dot(left, right, split_left):
-    def parts(value):
-        high = value.astype(jnp.bfloat16)
-        rest = value - high.astype(jnp.float32)
-        middle = rest.astype(jnp.bfloat16)
-        low = (rest - middle.astype(jnp.float32)).astype(jnp.bfloat16)
-        return (high, middle, low)
-
     total = None
     if split_left:
-        pieces = [(piece, right.astype(jnp.bfloat16)) for piece in parts(left)]
+        pieces = [(piece, right.astype(jnp.bfloat16)) for piece in bf16_parts(left)]
     else:
-        pieces = [(left.astype(jnp.bfloat16), piece) for piece in parts(right)]
+        pieces = [(left.astype(jnp.bfloat16), piece) for piece in bf16_parts(right)]
     for a, b in pieces:
         term = jnp.dot(a, b, preferred_element_type=jnp.float32)
         total = term if total is None else total + term
@@ -104,36 +119,40 @@
     ).astype(jnp.float32)
 
     def kernel(offsets_ref, wide_ref, pool_z_ref, pool_y_ref, out_ref):
-        offset_value = offsets_ref[pl.program_id(0)]
-        forward = margin + offset_value
-        backward = margin - offset_value
-        rows = []
-        for block in range(blocks_x):
-            total = None
-            for step in range(4):
-                x = block * 4 + step
-                term = (
-                    wide_ref[0, forward + x] * wide_ref[1, backward + x]
-                    + wide_ref[2, forward + x] * wide_ref[3, backward + x]
-                )
-                total = term if total is None else total + term
-            rows.append(total)
-        pooled_x = jnp.concatenate(rows, axis=0)
-        pooled_z = split_dot(pooled_x, pool_z_ref[...], True)
-        pooled = split_dot(pool_y_ref[...], pooled_z, False)
-        out_ref[0] = (pooled * (1.0 / 64.0)).reshape(blocks_x, blocks_y, blocks_z)
+        def per_offset(index, carry):
+            offset_value = offsets_ref[index]
+            forward = margin + offset_value
+            backward = margin - offset_value
+            rows = []
+            for block in range(blocks_x):
+                total = None
+                for step in range(4):
+                    x = block * 4 + step
+                    term = (
+                        wide_ref[0, forward + x] * wide_ref[1, backward + x]
+                        + wide_ref[2, forward + x] * wide_ref[3, backward + x]
+                    )
+                    total = term if total is None else total + term
+                rows.append(total)
+            pooled_x = jnp.concatenate(rows, axis=0)
+            pooled_z = split_dot(pooled_x, pool_z_ref[...], True)
+            pooled = split_dot(pool_y_ref[...], pooled_z, False)
+            out_ref[index] = (pooled * (1.0 / 64.0)).reshape(blocks_x, blocks_y, blocks_z)
+            return carry
+
+        lax.fori_loop(0, count, per_offset, 0)
 
     return pl.pallas_call(
         kernel,
         grid_spec=pltpu.PrefetchScalarGridSpec(
             num_scalar_prefetch=1,
-            grid=(count,),
+            grid=(1,),
             in_specs=[
                 pl.BlockSpec((fields, span_x, size_y, size_z), lambda i, offsets_ref: (0, 0, 0, 0)),
                 pl.BlockSpec((size_z, blocks_z), lambda i, offsets_ref: (0, 0)),
                 pl.BlockSpec((blocks_x * blocks_y, blocks_x * size_y), lambda i, offsets_ref: (0, 0)),
             ],
-            out_specs=pl.BlockSpec((1, blocks_x, blocks_y, blocks_z), lambda i, offsets_ref: (i, 0, 0, 0)),
+            out_specs=pl.BlockSpec((count, blocks_x, blocks_y, blocks_z), lambda i, offsets_ref: (0, 0, 0, 0)),
         ),
         out_shape=jax.ShapeDtypeStruct((count, blocks_x, blocks_y, blocks_z), jnp.float32),
     )(offsets, wide, pool_z, pool_y)
@@ -192,22 +211,16 @@
     previous = jnp.stack([source_prev[0], receiver_prev[0]])
     current = jnp.stack([source_now[0], receiver_now[0]])
     current_wide, previous_wide, courant_wide = input_halo(current, previous, courant, "gx")
+    source_fields = inject(cells_x + 2, first_x - 1, source_cells[0], wavelet[0], size_y, size_z)
+    receiver_fields = inject(cells_x + 2, first_x - 1, receiver_cells[0], receiver_data[0], size_y, size_z)
     levels = []
     for step_index in range(2):
+        sources = jnp.stack([source_fields[step_index], receiver_fields[step_index]])
         if step_index == 0:
-            cells_here, first_here = cells_x + 2, first_x - 1
             step_previous, step_extended, step_courant = previous_wide, current_wide, courant_wide
         else:
-            cells_here, first_here = cells_x, first_x
+            sources = sources[:, 1:-1]
             step_previous, step_extended, step_courant = current, levels[0], courant
-        sources = jnp.stack(
-            [
-                inject(cells_here, first_here, source_cells[0], wavelet[0, step_index], size_y, size_z),
-                inject(
-                    cells_here, first_here, receiver_cells[0], receiver_data[0, step_index], size_y, size_z
-                ),
-            ]
-        )
         advanced = laplace_step(step_previous, step_extended, step_courant, sources)
         levels.append(advanced)
     levels[0] = levels[0][:, 1:-1]

time: 100 us -> 88.6 us (0.89)
  other arithmetic: 18.9 us -> 10.8 us
  local copies, waits for them, and re-layouts: 15.3 us -> 9.37 us
  waiting for transfers between devices: 30.6 us -> 34.6 us
  starting transfers between devices: 24.5 us -> 20.6 us
  matrix products: 0.37 us -> 2.66 us
    scatter-add x4 -> x0, other arithmetic: 9.54 us -> none  [inject(): jnp.zeros((cells_here * plane_size + 1,), jnp.float32).at[target]]
    ppermute x1, waiting for transfers between devices: 0.01 us -> 3.91 us  [input_halo(): lax.ppermute(pack(current[:, :2], previous[:, :1], courant[:1]), axis, ba...]
    ppermute x1, starting transfers between devices: 7.11 us -> 3.37 us  [padded_2(): lax.ppermute(lax.slice_in_dim(block, block.shape[dim] - width, None, axis...]
    dot_general x0 -> x4, matrix products: none -> 2.29 us  [inject(): sums = jnp.dot(rows, parts, preferred_element_type=jnp.float32)]
    slice x2, local copies, waits for them, and re-layouts: 1.99 us -> 0.02 us  [unpack(): now_planes = planes[:2 * fields].reshape(fields, 2, size_y, size_z)]
    reshape x2, local copies, waits for them, and re-layouts: 1.69 us -> 0.01 us  [unpack(): planes[2 * fields:3 * fields].reshape(fields, 1, size_y, size_z)]
    slice x2, local copies, waits for them, and re-layouts: 1.62 us -> 0.01 us  [unpack(): return (now_planes, prev_planes, planes[3 * fields:])]
    slice x9 -> x0, local copies, waits for them, and re-layouts: 1.12 us -> none  [the longest x8 1.12 us: inject(): return flat_cells[:-1].reshape(cells_here, size_y, size_z)]
  transfers between devices with their start and end apart: 5 -> 5, of which waited for: 3 -> 4; matrix products, arithmetic and copies ran while one was open for 13% -> 7% of each run, Pallas kernels for 0% -> 0%
where the time goes in v6:
time: 88.6 us; the launch traced here: 88.2 us
  waiting for transfers between devices  34.6 us (39%)
  starting transfers between devices  20.6 us (23%)
  other arithmetic  10.8 us (12%)
  Pallas kernels  9.59 us (11%)
  local copies, waits for them, and re-layouts  9.37 us (11%)
  matrix products  2.66 us (3%)
    ppermute x1, waiting for transfers between devices, padded_2(): lax.ppermute(lax.slice_in_dim(block, block.shape[dim] - width, None, axis...  14 us
    pallas_call x1, Pallas kernels, offset_image(): pl.pallas_call(kernel, grid_spec=pltpu.PrefetchScalarGridSpec(num_scalar_...  9.59 us
    all_to_all x1, waiting for transfers between devices, group_sum_windows(): received = lax.all_to_all(windows, axis, 0, 0, tiled=True)  8.65 us
    all_to_all x1, starting transfers between devices, group_sum_windows(): received = lax.all_to_all(windows, axis, 0, 0, tiled=True)  8.14 us
    ppermute x1, waiting for transfers between devices, padded_2(): lax.ppermute(lax.slice_in_dim(block, 0, width, axis=dim), axis, backward)  8.01 us
    unnamed x49, local copies, waits for them, and re-layouts  5.79 us
    ppermute x1, starting transfers between devices, input_halo(): lax.ppermute(pack(current[:, -2:], previous[:, -1:], courant[-1:]), axis,...  5.3 us
    ppermute x1, waiting for transfers between devices, input_halo(): lax.ppermute(pack(current[:, :2], previous[:, :1], courant[:1]), axis, ba...  3.91 us
  transfers between devices with their start and end apart: 5, of which 4 were waited for; matrix products, arithmetic and copies ran while one was open for 7% of the time, Pallas kernels for 0%

profile of v6, /device:TPU:39, one launch (start us, length us, event | category | flops | bytes accessed | tf_op | source)
XLA Modules:
  0.0 88.2 jit_solution(17099088895833539174)
XLA Ops:
  0.0 1.2 %constant_dynamic-update-slice_fusion.1 = f32[2,16,64,128]{3,2,1,0:T(8,128)S(1)} fusion(f32[1,16,64,128]{3,2,1,0:T(8,128)} %param.13), kind=kLoop, calls=%fused_computation.100 | loop fusion | bytes 1048576
  1.7 5.3 %collective-permute-start = (f32[7,64,128]{2,1,0:T(8,128)S(1)}, f32[7,64,128]{2,1,0:T(8,128)S(1)}, u32[]{:S(2)}, u32[]{:S(2)}) collective-permute-start(f32[7,64,128]{2,1,0:T(8,128)S(1)} %pad_maximum_fusion.7), channel_id=1, source_target_pairs={{0,1},{1,2},{2,3},{3,4},{4,5},{5,6},{6,7},{7,8},{8,9},{9,10},{10,1... | collective-permute-start | bytes 688136 | tf_op jit(solution)/shard_map/ppermute | solution.py:40
  7.0 1.9 %collective-permute-start.1 = (f32[7,64,128]{2,1,0:T(8,128)S(1)}, f32[7,64,128]{2,1,0:T(8,128)S(1)}, u32[]{:S(2)}, u32[]{:S(2)}) collective-permute-start(f32[7,64,128]{2,1,0:T(8,128)S(1)} %pad_maximum_fusion.8), channel_id=1, source_target_pairs={{1,0},{2,1},{3,2},{4,3},{5,4},{6,5},{7,6},{8,7},{9,8},{10,9},{11,1... | collective-permute-start | bytes 688136 | tf_op jit(solution)/shard_map/ppermute | solution.py:43
  9.0 0.7 and_select_fusion.4
  9.7 0.7 add_bitcast_fusion
  10.7 0.8 fusion.1
  11.6 0.6 copy-done.8
  12.3 0.4 fusion.23
  12.7 0.8 fusion
  13.6 0.4 fusion.22
  14.1 3.9 %collective-permute-done.1 = f32[7,64,128]{2,1,0:T(8,128)S(1)} collective-permute-done((f32[7,64,128]{2,1,0:T(8,128)S(1)}, f32[7,64,128]{2,1,0:T(8,128)S(1)}, u32[]{:S(2)}, u32[]{:S(2)}) %collective-permute-start.1) | collective-permute-done | bytes 229408 | tf_op jit(solution)/shard_map/ppermute | solution.py:43
  18.2 1.5 %fusion.10 = f32[2,18,64,128]{3,2,1,0:T(8,128)S(1)} fusion(f32[2,18,64,128]{3,2,1,0:T(8,128)S(1)} %pad_maximum_fusion.3, f32[2,1,64,128]{3,2,1,0:T(8,128)S(1)} %slice_bitcast_fusion, f32[2,1,64,128]{3,2,1,0:T(8,128)S(1)} %slice_bitcast_fusion.1, f32[2,2,64,128]{3,2,1,0:T(8,128)S(1)} %bitcast.210, ...), kind=kLoop, calls=%fused_computation.29 | loop fusion | flops 5275648 | bytes 6619136 | tf_op jit(solution)/shard_map/add | solution.py:91
  19.8 0.9 fusion.21
  20.6 0.4 fusion.2
  21.1 3.4 %collective-permute-start.2 = (f32[4,12,64,128]{3,2,1,0:T(8,128)S(1)}, f32[4,12,64,128]{3,2,1,0:T(8,128)S(1)}, u32[]{:S(2)}, u32[]{:S(2)}) collective-permute-start(f32[4,12,64,128]{3,2,1,0:T(8,128)S(1)} %get-tuple-element.5), channel_id=1, source_target_pairs={{0,1},{1,2},{2,3},{3,4},{4,5},{5,6},{6,7},{7,8},{8,9},{9,10},{10,1... | collective-permute-start | bytes 4718600 | tf_op jit(solution)/shard_map/ppermute | solution.py:16
  24.5 1.9 %collective-permute-start.3 = (f32[4,12,64,128]{3,2,1,0:T(8,128)S(1)}, f32[4,12,64,128]{3,2,1,0:T(8,128)S(1)}, u32[]{:S(2)}, u32[]{:S(2)}) collective-permute-start(f32[4,12,64,128]{3,2,1,0:T(8,128)S(1)} %get-tuple-element.6), channel_id=1, source_target_pairs={{1,0},{2,1},{3,2},{4,3},{5,4},{6,5},{7,6},{8,7},{9,8},{10,9},{11,1... | collective-permute-start | bytes 4718600 | tf_op jit(solution)/shard_map/ppermute | solution.py:19
  26.4 0.7 fusion.45.pool_z_ref
  27.1 0.7 fusion.40.pool_y_ref
  27.8 14.0 %collective-permute-done.2 = f32[4,12,64,128]{3,2,1,0:T(8,128)S(1)} collective-permute-done((f32[4,12,64,128]{3,2,1,0:T(8,128)S(1)}, f32[4,12,64,128]{3,2,1,0:T(8,128)S(1)}, u32[]{:S(2)}, u32[]{:S(2)}) %collective-permute-start.2) | collective-permute-done | bytes 1572896 | tf_op jit(solution)/shard_map/ppermute | solution.py:16
  41.8 8.0 %collective-permute-done.3 = f32[4,12,64,128]{3,2,1,0:T(8,128)S(1)} collective-permute-done((f32[4,12,64,128]{3,2,1,0:T(8,128)S(1)}, f32[4,12,64,128]{3,2,1,0:T(8,128)S(1)}, u32[]{:S(2)}, u32[]{:S(2)}) %collective-permute-start.3) | collective-permute-done | bytes 1572896 | tf_op jit(solution)/shard_map/ppermute | solution.py:19
  49.8 2.7 %pad_maximum_fusion.wide_ref = f32[4,40,64,128]{3,2,1,0:T(8,128)} fusion(f32[4,12,64,128]{3,2,1,0:T(8,128)S(1)} %collective-permute-done.3, f32[2,16,64,128]{3,2,1,0:T(8,128)S(1)} %fusion.21, f32[2,16,64,128]{3,2,1,0:T(8,128)S(1)} %slice.309, f32[4,12,64,128]{3,2,1,0:T(8,128)S(1)} %collective-permute-done.2), kind=kLoop, calls=%fused_computation | loop fusion | flops 3932160 | bytes 10485760 | tf_op jit(solution)/shard_map/concatenate | solution.py:20
  52.5 9.6 %shard_map.118 = f32[9,6,16,32]{3,2,1,0:T(8,128)} custom-call(s32[9]{0:T(128)} %offsets_ref.1, f32[4,40,64,128]{3,2,1,0:T(8,128)} %pad_maximum_fusion.wide_ref, f32[128,32]{1,0:T(8,128)} %fusion.45.pool_z_ref, f32[96,384]{1,0:T(8,128)} %fusion.40.pool_y_ref), custom_call_target="tpu_custom_call" | custom-call | tf_op jit(solution)/shard_map/pallas_call | solution.py:145
  62.1 1.3 %fusion.24 = (f32[1,9,6,16,32]{4,3,2,1,0:T(8,128)S(1)}, f32[1,9,6,16,32]{4,3,2,1,0:T(8,128)S(1)}) fusion(f32[9,6,16,32]{3,2,1,0:T(8,128)} %shard_map.118), kind=kLoop, calls=%fused_computation.62 | loop fusion | bytes 331776 | tf_op jit(solution)/shard_map/stack | solution.py:186
  63.5 0.4 copy.50
  64.0 1.5 %reshape.197 = f32[16,1,5184]{2,1,0:T(1,128)} reshape(f32[16,3,9,6,32]{4,3,2,1,0:T(8,128)S(1)} %copy.50) | data formatting | bytes 663552
  65.5 8.1 %all-to-all-start = ((f32[16,1,5184]{2,1,0:T(1,128)}), f32[16,1,5184]{2,1,0:T(1,128)S(1)}, u32[]{:S(2)}, u32[]{:S(2)}) async-start(f32[16,1,5184]{2,1,0:T(1,128)} %reshape.197), calls=%async_computation | async-start | bytes 671744 | tf_op jit(solution)/shard_map/all_to_all | solution.py:190
  73.7 8.6 %all-to-all-done = f32[16,1,5184]{2,1,0:T(1,128)S(1)} async-done(((f32[16,1,5184]{2,1,0:T(1,128)}), f32[16,1,5184]{2,1,0:T(1,128)S(1)}, u32[]{:S(2)}, u32[]{:S(2)}) %all-to-all-start) | async-done | bytes 331808 | tf_op jit(solution)/shard_map/all_to_all | solution.py:190
  82.4 0.5 broadcast.281
  82.9 1.4 %reduce = f32[16,5184]{1,0:T(8,128)S(1)} reduce(f32[16,1,5184]{2,1,0:T(1,128)S(1)} %all-to-all-done, f32[]{:T(128)} %broadcast.281), dimensions={1}, to_apply=%all_to_all.3.reduce_sub_computation | reduce | bytes 663556 | tf_op jit(solution)/shard_map/all_to_all | solution.py:190
  84.3 0.5 reshape.198
  87.1 0.4 fusion.13
  87.5 0.7 copy.77
  (78 shorter events, 3.7 us)
Async XLA Ops:
  0.0 1.3 %copy-start.4 = (f32[1,16,64,128]{3,2,1,0:T(8,128)S(1)}, f32[1,16,64,128]{3,2,1,0:T(8,128)}, u32[]{:S(2)}) copy-start(f32[1,16,64,128]{3,2,1,0:T(8,128)} %param.15) | copy-start | bytes 1572868
  0.0 1.4 %copy-start.1 = (f32[16,64,128]{2,1,0:T(8,128)S(1)}, f32[16,64,128]{2,1,0:T(8,128)}, u32[]{:S(2)}) copy-start(f32[16,64,128]{2,1,0:T(8,128)} %param.16) | copy-start | bytes 1572868
  0.0 1.5 %copy-start.3 = (f32[1,16,64,128]{3,2,1,0:T(8,128)S(1)}, f32[1,16,64,128]{3,2,1,0:T(8,128)}, u32[]{:S(2)}) copy-start(f32[1,16,64,128]{3,2,1,0:T(8,128)} %param.12) | copy-start | bytes 1572868
  0.0 1.7 %copy-start.2 = (f32[1,16,64,128]{3,2,1,0:T(8,128)S(1)}, f32[1,16,64,128]{3,2,1,0:T(8,128)}, u32[]{:S(2)}) copy-start(f32[1,16,64,128]{3,2,1,0:T(8,128)} %param.14) | copy-start | bytes 1572868
  1.3 7.7 %copy-start.7 = (f32[1,2,512]{2,1,0:T(2,128)S(1)}, f32[1,2,512]{2,1,0:T(2,128)}, u32[]{:S(2)}) copy-start(f32[1,2,512]{2,1,0:T(2,128)} %param.20) | copy-start | bytes 12292
  1.3 9.0 %copy-start.6 = (s32[1,512]{1,0:T(1,128)S(1)}, s32[1,512]{1,0:T(1,128)}, u32[]{:S(2)}) copy-start(s32[1,512]{1,0:T(1,128)} %param.19) | copy-start | bytes 6148
  1.7 12.3 %collective-permute-start = (f32[7,64,128]{2,1,0:T(8,128)S(1)}, f32[7,64,128]{2,1,0:T(8,128)S(1)}, u32[]{:S(2)}, u32[]{:S(2)}) collective-permute-start(f32[7,64,128]{2,1,0:T(8,128)S(1)} %pad_maximum_fusion.7), channel_id=1, source_target_pairs={{0,1},{1,2},{2,3},{3,4},{4,5},{5,6},{6,7},{7,8},{8,9},{9,10},{10,1... | collective-permute-start | bytes 688136 | tf_op jit(solution)/shard_map/ppermute | solution.py:40
  7.0 11.0 %collective-permute-start.1 = (f32[7,64,128]{2,1,0:T(8,128)S(1)}, f32[7,64,128]{2,1,0:T(8,128)S(1)}, u32[]{:S(2)}, u32[]{:S(2)}) collective-permute-start(f32[7,64,128]{2,1,0:T(8,128)S(1)} %pad_maximum_fusion.8), channel_id=1, source_target_pairs={{1,0},{2,1},{3,2},{4,3},{5,4},{6,5},{7,6},{8,7},{9,8},{10,9},{11,1... | collective-permute-start | bytes 688136 | tf_op jit(solution)/shard_map/ppermute | solution.py:43
  11.5 0.7 copy-start.8
  21.1 20.7 %collective-permute-start.2 = (f32[4,12,64,128]{3,2,1,0:T(8,128)S(1)}, f32[4,12,64,128]{3,2,1,0:T(8,128)S(1)}, u32[]{:S(2)}, u32[]{:S(2)}) collective-permute-start(f32[4,12,64,128]{3,2,1,0:T(8,128)S(1)} %get-tuple-element.5), channel_id=1, source_target_pairs={{0,1},{1,2},{2,3},{3,4},{4,5},{5,6},{6,7},{7,8},{8,9},{9,10},{10,1... | collective-permute-start | bytes 4718600 | tf_op jit(solution)/shard_map/ppermute | solution.py:16
  24.5 25.3 %collective-permute-start.3 = (f32[4,12,64,128]{3,2,1,0:T(8,128)S(1)}, f32[4,12,64,128]{3,2,1,0:T(8,128)S(1)}, u32[]{:S(2)}, u32[]{:S(2)}) collective-permute-start(f32[4,12,64,128]{3,2,1,0:T(8,128)S(1)} %get-tuple-element.6), channel_id=1, source_target_pairs={{1,0},{2,1},{3,2},{4,3},{5,4},{6,5},{7,6},{8,7},{9,8},{10,9},{11,1... | collective-permute-start | bytes 4718600 | tf_op jit(solution)/shard_map/ppermute | solution.py:19
  62.1 1.3 %copy-start = (f32[9,6,16,32]{3,2,1,0:T(8,128)S(1)}, f32[9,6,16,32]{3,2,1,0:T(8,128)}, u32[]{:S(2)}) copy-start(f32[9,6,16,32]{3,2,1,0:T(8,128)} %shard_map.118) | copy-start | bytes 331780
  64.0 9.7 %copy-start.5 = (f32[64,9,3,3,3]{0,4,3,2,1:T(4,128)S(1)}, f32[64,9,3,3,3]{0,4,3,2,1:T(4,128)}, u32[]{:S(2)}) copy-start(f32[64,9,3,3,3]{0,4,3,2,1:T(4,128)} %param.22) | copy-start | bytes 186628
  65.5 16.9 %all-to-all-start = ((f32[16,1,5184]{2,1,0:T(1,128)}), f32[16,1,5184]{2,1,0:T(1,128)S(1)}, u32[]{:S(2)}, u32[]{:S(2)}) async-start(f32[16,1,5184]{2,1,0:T(1,128)} %reshape.197), calls=%async_computation | async-start | bytes 671744 | tf_op jit(solution)/shard_map/all_to_all | solution.py:190
  85.4 1.7 %copy-start.9 = (f32[64]{0:T(128)S(1)}, f32[64]{0:T(128)}, u32[]{:S(2)}) copy-start(f32[64]{0:T(128)} %param.23) | copy-start | bytes 772

commit v7 on v6

--- a/solution.py
+++ b/solution.py
@@ -19,6 +19,15 @@
         high = lax.ppermute(lax.slice_in_dim(block, 0, width, axis=dim), axis, backward)
         block = jnp.concatenate([low, block, high], axis=dim)
     return block
+
+
+def halo_pieces(block, axis, width):
+    count = lax.axis_size(axis)
+    forward = [(i, i + 1) for i in range(count - 1)]
+    backward = [(target, source) for source, target in forward]
+    low = lax.ppermute(block[:, block.shape[1] - width :], axis, forward)
+    high = lax.ppermute(block[:, :width], axis, backward)
+    return [low, block, high]
 
 
 def input_halo(current, previous, courant, axis):
@@ -109,21 +118,31 @@
     return total
 
 
-def offset_image(wide, offsets, margin, cells_x):
-    fields, span_x, size_y, size_z = wide.shape
+def offset_image(pieces, offsets, margin, cells_x):
+    fields, _, size_y, size_z = pieces[0].shape
+    spans = [piece.shape[1] for piece in pieces]
+    starts = [sum(spans[:k]) for k in range(len(spans))]
+    span_x = sum(spans)
     count = offsets.shape[0]
     blocks_x, blocks_y, blocks_z = cells_x // 4, size_y // 4, size_z // 4
     pool_z = pooling(size_z, 4)
-    pool_y = (
-        (jnp.arange(blocks_x * size_y)[None, :] // 4) == jnp.arange(blocks_x * blocks_y)[:, None]
-    ).astype(jnp.float32)
-
-    def kernel(offsets_ref, wide_ref, pool_z_ref, pool_y_ref, out_ref):
+
+    def kernel(offsets_ref, *refs):
+        piece_refs = refs[: len(pieces)]
+        pool_z_ref, out_ref, wide_ref, sum_ref, semaphores = refs[len(pieces) :]
+        copies = [
+            pltpu.make_async_copy(piece_ref, wide_ref.at[:, start : start + span], semaphores.at[k])
+            for k, (piece_ref, start, span) in enumerate(zip(piece_refs, starts, spans))
+        ]
+        for copy in copies:
+            copy.start()
+        for copy in copies:
+            copy.wait()
+
         def per_offset(index, carry):
             offset_value = offsets_ref[index]
             forward = margin + offset_value
             backward = margin - offset_value
-            rows = []
             for block in range(blocks_x):
                 total = None
                 for step in range(4):
@@ -133,10 +152,12 @@
                         + wide_ref[2, forward + x] * wide_ref[3, backward + x]
                     )
                     total = term if total is None else total + term
-                rows.append(total)
-            pooled_x = jnp.concatenate(rows, axis=0)
-            pooled_z = split_dot(pooled_x, pool_z_ref[...], True)
-            pooled = split_dot(pool_y_ref[...], pooled_z, False)
+                sum_ref[block * size_y : (block + 1) * size_y, :] = total
+            pooled_y = None
+            for step in range(4):
+                rows = sum_ref[pl.ds(step, blocks_x * blocks_y, stride=4), :]
+                pooled_y = rows if pooled_y is None else pooled_y + rows
+            pooled = split_dot(pooled_y, pool_z_ref[...], True)
             out_ref[index] = (pooled * (1.0 / 64.0)).reshape(blocks_x, blocks_y, blocks_z)
             return carry
 
@@ -147,15 +168,17 @@
         grid_spec=pltpu.PrefetchScalarGridSpec(
             num_scalar_prefetch=1,
             grid=(1,),
-            in_specs=[
-                pl.BlockSpec((fields, span_x, size_y, size_z), lambda i, offsets_ref: (0, 0, 0, 0)),
-                pl.BlockSpec((size_z, blocks_z), lambda i, offsets_ref: (0, 0)),
-                pl.BlockSpec((blocks_x * blocks_y, blocks_x * size_y), lambda i, offsets_ref: (0, 0)),
+            in_specs=[pl.BlockSpec(memory_space=pl.ANY) for _ in pieces]
+            + [pl.BlockSpec((size_z, blocks_z), lambda i, offsets_ref: (0, 0))],
+            out_specs=pl.BlockSpec((count, blocks_x, blocks_y, blocks_z), lambda i, offsets_ref: (0, 0, 0, 0)),
+            scratch_shapes=[
+                pltpu.VMEM((fields, span_x, size_y, size_z), jnp.float32),
+                pltpu.VMEM((blocks_x * size_y, size_z), jnp.float32),
+                pltpu.SemaphoreType.DMA((len(pieces),)),
             ],
-            out_specs=pl.BlockSpec((count, blocks_x, blocks_y, blocks_z), lambda i, offsets_ref: (0, 0, 0, 0)),
         ),
         out_shape=jax.ShapeDtypeStruct((count, blocks_x, blocks_y, blocks_z), jnp.float32),
-    )(offsets, wide, pool_z, pool_y)
+    )(offsets, *pieces, pool_z)
 
 
 def conv_apply(padded, conv_weight, conv_bias):
@@ -225,8 +248,7 @@
         levels.append(advanced)
     levels[0] = levels[0][:, 1:-1]
     fields = jnp.concatenate(levels, axis=0)
-    wide = padded_2(fields, (("gx", 1),), HMAX + 4)
-    coarse = offset_image(wide, offsets, HMAX, cells_x + 8)
+    coarse = offset_image(halo_pieces(fields, "gx", HMAX + 4), offsets, HMAX, cells_x + 8)
     summed = group_sum_windows(coarse, "shot")
     window = jnp.pad(summed, ((0, 0), (0, 0), (0, 0), (1, 1)))
     return conv_apply(window, conv_weight, conv_bias)

time: 88.6 us -> 85.7 us (0.967)
  Pallas kernels: 9.59 us -> 7.56 us
  other arithmetic: 10.8 us -> 8.95 us
  starting transfers between devices: 20.6 us -> 22 us
    concatenate x1 -> x0, other arithmetic: 2.67 us -> none  [padded_2(): block = jnp.concatenate([low, block, high], axis=dim)]
    pallas_call x1, Pallas kernels: 9.59 us -> 7.56 us  [offset_image(): pl.pallas_call(kernel, grid_spec=pltpu.PrefetchScalarGridSpec(num_scalar_...]
    concatenate x1 -> x2, other arithmetic: 0.44 us -> 1.85 us  [local(): fields = jnp.concatenate(levels, axis=0)]
    all_to_all x1, starting transfers between devices: 8.14 us -> 9.49 us  [group_sum_windows(): received = lax.all_to_all(windows, axis, 0, 0, tiled=True)]
    unnamed x49 -> x51, local copies, waits for them, and re-layouts: 5.79 us -> 5.8 us
  transfers between devices with their start and end apart: 5 -> 5, of which waited for: 4 -> 4; matrix products, arithmetic and copies ran while one was open for 7% -> 8% of each run, Pallas kernels for 0% -> 0%
where the time goes in v7:
time: 85.7 us; the launch traced here: 85.2 us
  waiting for transfers between devices  34.1 us (40%)
  starting transfers between devices  22 us (26%)
  local copies, waits for them, and re-layouts  9.38 us (11%)
  other arithmetic  8.95 us (10%)
  Pallas kernels  7.56 us (9%)
  matrix products  2.66 us (3%)
    ppermute x1, waiting for transfers between devices, halo_pieces(): low = lax.ppermute(block[:, block.shape[1] - width:], axis, forward)  13.2 us
    all_to_all x1, starting transfers between devices, group_sum_windows(): received = lax.all_to_all(windows, axis, 0, 0, tiled=True)  9.49 us
    all_to_all x1, waiting for transfers between devices, group_sum_windows(): received = lax.all_to_all(windows, axis, 0, 0, tiled=True)  8.57 us
    ppermute x1, waiting for transfers between devices, halo_pieces(): high = lax.ppermute(block[:, :width], axis, backward)  8.44 us
    pallas_call x1, Pallas kernels, offset_image(): pl.pallas_call(kernel, grid_spec=pltpu.PrefetchScalarGridSpec(num_scalar_...  7.56 us
    unnamed x51, local copies, waits for them, and re-layouts  5.8 us
    ppermute x1, starting transfers between devices, input_halo(): lax.ppermute(pack(current[:, -2:], previous[:, -1:], courant[-1:]), axis,...  5.3 us
    ppermute x1, waiting for transfers between devices, input_halo(): lax.ppermute(pack(current[:, :2], previous[:, :1], courant[:1]), axis, ba...  3.91 us
  transfers between devices with their start and end apart: 5, of which 4 were waited for; matrix products, arithmetic and copies ran while one was open for 8% of the time, Pallas kernels for 0%

profile of v7, /device:TPU:39, one launch (start us, length us, event | category | flops | bytes accessed | tf_op | source)
XLA Modules:
  0.0 85.2 jit_solution(13796484650931065685)
XLA Ops:
  0.0 1.2 %constant_dynamic-update-slice_fusion.1 = f32[2,16,64,128]{3,2,1,0:T(8,128)S(1)} fusion(f32[1,16,64,128]{3,2,1,0:T(8,128)} %param.13), kind=kLoop, calls=%fused_computation.100 | loop fusion | bytes 1048576
  1.7 5.3 %collective-permute-start = (f32[7,64,128]{2,1,0:T(8,128)S(1)}, f32[7,64,128]{2,1,0:T(8,128)S(1)}, u32[]{:S(2)}, u32[]{:S(2)}) collective-permute-start(f32[7,64,128]{2,1,0:T(8,128)S(1)} %pad_maximum_fusion.6), channel_id=1, source_target_pairs={{0,1},{1,2},{2,3},{3,4},{4,5},{5,6},{6,7},{7,8},{8,9},{9,10},{10,1... | collective-permute-start | bytes 688136 | tf_op jit(solution)/shard_map/ppermute | solution.py:49
  7.0 1.9 %collective-permute-start.1 = (f32[7,64,128]{2,1,0:T(8,128)S(1)}, f32[7,64,128]{2,1,0:T(8,128)S(1)}, u32[]{:S(2)}, u32[]{:S(2)}) collective-permute-start(f32[7,64,128]{2,1,0:T(8,128)S(1)} %pad_maximum_fusion.7), channel_id=1, source_target_pairs={{1,0},{2,1},{3,2},{4,3},{5,4},{6,5},{7,6},{8,7},{9,8},{10,9},{11,1... | collective-permute-start | bytes 688136 | tf_op jit(solution)/shard_map/ppermute | solution.py:52
  9.0 0.7 and_select_fusion.4
  9.7 0.7 add_bitcast_fusion
  10.4 0.3 reduce-precision_convert_fusion.1
  10.7 0.8 fusion.1
  11.6 0.6 copy-done.9
  12.3 0.4 fusion.24
  12.7 0.8 fusion
  13.6 0.4 fusion.23
  14.1 3.9 %collective-permute-done.1 = f32[7,64,128]{2,1,0:T(8,128)S(1)} collective-permute-done((f32[7,64,128]{2,1,0:T(8,128)S(1)}, f32[7,64,128]{2,1,0:T(8,128)S(1)}, u32[]{:S(2)}, u32[]{:S(2)}) %collective-permute-start.1) | collective-permute-done | bytes 229408 | tf_op jit(solution)/shard_map/ppermute | solution.py:52
  18.2 1.5 %fusion.11 = f32[2,18,64,128]{3,2,1,0:T(8,128)S(1)} fusion(f32[2,18,64,128]{3,2,1,0:T(8,128)S(1)} %pad_maximum_fusion.2, f32[2,1,64,128]{3,2,1,0:T(8,128)S(1)} %slice_bitcast_fusion, f32[2,1,64,128]{3,2,1,0:T(8,128)S(1)} %slice_bitcast_fusion.1, f32[2,2,64,128]{3,2,1,0:T(8,128)S(1)} %bitcast.210, ...), kind=kLoop, calls=%fused_computation.31 | loop fusion | flops 5275648 | bytes 6619136 | tf_op jit(solution)/shard_map/add | solution.py:100
  19.8 0.9 %fusion.22 = f32[2,16,64,128]{3,2,1,0:T(8,128)S(1)} fusion(f32[2,16,64,128]{3,2,1,0:T(8,128)S(1)} %slice.309, f32[1,18,64,128]{3,2,1,0:T(8,128)S(1)} %bitcast.201, f32[1,18,64,128]{3,2,1,0:T(8,128)S(1)} %bitcast.202, f32[2,18,64,128]{3,2,1,0:T(8,128)S(1)} %fusion.11, f32[2,16,64,128]{3,2,1,0:T(8,128)S(1)} %constant_dynamic-update-slice_fusion, ...), kind=kLoop, calls=%fused_computation.47 | loop fusion | flops 3407872 | bytes 6946816 | tf_op jit(solution)/shard_map/add | solution.py:100
  20.7 0.4 fusion.3
  21.1 3.4 %collective-permute-start.2 = (f32[4,12,64,128]{3,2,1,0:T(8,128)S(1)}, f32[4,12,64,128]{3,2,1,0:T(8,128)S(1)}, u32[]{:S(2)}, u32[]{:S(2)}) collective-permute-start(f32[4,12,64,128]{3,2,1,0:T(8,128)S(1)} %get-tuple-element.6), channel_id=1, source_target_pairs={{0,1},{1,2},{2,3},{3,4},{4,5},{5,6},{6,7},{7,8},{8,9},{9,10},{10,1... | collective-permute-start | bytes 4718600 | tf_op jit(solution)/shard_map/ppermute | solution.py:28
  24.5 1.9 %collective-permute-start.3 = (f32[4,12,64,128]{3,2,1,0:T(8,128)S(1)}, f32[4,12,64,128]{3,2,1,0:T(8,128)}, u32[]{:S(2)}, u32[]{:S(2)}) collective-permute-start(f32[4,12,64,128]{3,2,1,0:T(8,128)S(1)} %get-tuple-element.5), channel_id=1, source_target_pairs={{1,0},{2,1},{3,2},{4,3},{5,4},{6,5},{7,6},{8,7},{9,8},{10,9},{11,1... | collective-permute-start | bytes 4718600 | tf_op jit(solution)/shard_map/ppermute | solution.py:29
  26.4 0.7 fusion.45.refs_3_
  27.1 1.5 %pad_maximum_fusion.refs_1_ = f32[4,16,64,128]{3,2,1,0:T(8,128)} fusion(f32[2,16,64,128]{3,2,1,0:T(8,128)S(1)} %fusion.22, f32[2,16,64,128]{3,2,1,0:T(8,128)S(1)} %slice.309), kind=kLoop, calls=%fused_computation.10 | loop fusion | flops 524288 | bytes 4194304 | tf_op jit(solution)/shard_map/concatenate | solution.py:250
  28.6 13.2 %collective-permute-done.2.refs_0_ = f32[4,12,64,128]{3,2,1,0:T(8,128)S(1)} collective-permute-done((f32[4,12,64,128]{3,2,1,0:T(8,128)S(1)}, f32[4,12,64,128]{3,2,1,0:T(8,128)S(1)}, u32[]{:S(2)}, u32[]{:S(2)}) %collective-permute-start.2) | collective-permute-done | bytes 1572896 | tf_op jit(solution)/shard_map/ppermute | solution.py:28
  41.8 8.4 %collective-permute-done.3.refs_2_ = f32[4,12,64,128]{3,2,1,0:T(8,128)} collective-permute-done((f32[4,12,64,128]{3,2,1,0:T(8,128)S(1)}, f32[4,12,64,128]{3,2,1,0:T(8,128)}, u32[]{:S(2)}, u32[]{:S(2)}) %collective-permute-start.3) | collective-permute-done | bytes 1572896 | tf_op jit(solution)/shard_map/ppermute | solution.py:29
  50.2 7.6 %shard_map.118 = f32[9,6,16,32]{3,2,1,0:T(8,128)} custom-call(s32[9]{0:T(128)} %offsets_ref.1, f32[4,12,64,128]{3,2,1,0:T(8,128)} %copy-done.4, f32[4,16,64,128]{3,2,1,0:T(8,128)} %pad_maximum_fusion.refs_1_, f32[4,12,64,128]{3,2,1,0:T(8,128)} %collective-permute-done.3.refs_2_, f32[128,32]{1,0:T(8,128)} %fusion.45.refs_3_), custom_call_target="tpu_custom_call" | custom-call | tf_op jit(solution)/shard_map/pallas_call | solution.py:166
  57.8 1.3 %fusion.25 = (f32[1,9,6,16,32]{4,3,2,1,0:T(8,128)S(1)}, f32[1,9,6,16,32]{4,3,2,1,0:T(8,128)S(1)}) fusion(f32[9,6,16,32]{3,2,1,0:T(8,128)} %shard_map.118), kind=kLoop, calls=%fused_computation.64 | loop fusion | bytes 331776 | tf_op jit(solution)/shard_map/stack | solution.py:209
  59.3 0.4 copy.50
  59.7 1.5 %reshape.160 = f32[16,1,5184]{2,1,0:T(1,128)} reshape(f32[16,3,9,6,32]{4,3,2,1,0:T(8,128)S(1)} %copy.50) | data formatting | bytes 663552
  61.3 9.5 %all-to-all-start = ((f32[16,1,5184]{2,1,0:T(1,128)}), f32[16,1,5184]{2,1,0:T(1,128)S(1)}, u32[]{:S(2)}, u32[]{:S(2)}) async-start(f32[16,1,5184]{2,1,0:T(1,128)} %reshape.160), calls=%async_computation | async-start | bytes 671744 | tf_op jit(solution)/shard_map/all_to_all | solution.py:213
  70.8 8.6 %all-to-all-done = f32[16,1,5184]{2,1,0:T(1,128)S(1)} async-done(((f32[16,1,5184]{2,1,0:T(1,128)}), f32[16,1,5184]{2,1,0:T(1,128)S(1)}, u32[]{:S(2)}, u32[]{:S(2)}) %all-to-all-start) | async-done | bytes 331808 | tf_op jit(solution)/shard_map/all_to_all | solution.py:213
  79.4 0.5 broadcast.241
  79.9 1.4 %reduce = f32[16,5184]{1,0:T(8,128)S(1)} reduce(f32[16,1,5184]{2,1,0:T(1,128)S(1)} %all-to-all-done, f32[]{:T(128)} %broadcast.241), dimensions={1}, to_apply=%all_to_all.3.reduce_sub_computation | reduce | bytes 663556 | tf_op jit(solution)/shard_map/all_to_all | solution.py:213
  81.3 0.5 reshape.161
  84.1 0.4 fusion.14
  84.5 0.7 copy.77
  (78 shorter events, 3.5 us)
Async XLA Ops:
  0.0 1.3 %copy-start.5 = (f32[1,16,64,128]{3,2,1,0:T(8,128)S(1)}, f32[1,16,64,128]{3,2,1,0:T(8,128)}, u32[]{:S(2)}) copy-start(f32[1,16,64,128]{3,2,1,0:T(8,128)} %param.15) | copy-start | bytes 1572868
  0.0 1.4 %copy-start.1 = (f32[16,64,128]{2,1,0:T(8,128)S(1)}, f32[16,64,128]{2,1,0:T(8,128)}, u32[]{:S(2)}) copy-start(f32[16,64,128]{2,1,0:T(8,128)} %param.16) | copy-start | bytes 1572868
  0.0 1.5 %copy-start.3 = (f32[1,16,64,128]{3,2,1,0:T(8,128)S(1)}, f32[1,16,64,128]{3,2,1,0:T(8,128)}, u32[]{:S(2)}) copy-start(f32[1,16,64,128]{3,2,1,0:T(8,128)} %param.12) | copy-start | bytes 1572868
  0.0 1.7 %copy-start.2 = (f32[1,16,64,128]{3,2,1,0:T(8,128)S(1)}, f32[1,16,64,128]{3,2,1,0:T(8,128)}, u32[]{:S(2)}) copy-start(f32[1,16,64,128]{3,2,1,0:T(8,128)} %param.14) | copy-start | bytes 1572868
  1.3 7.7 %copy-start.8 = (f32[1,2,512]{2,1,0:T(2,128)S(1)}, f32[1,2,512]{2,1,0:T(2,128)}, u32[]{:S(2)}) copy-start(f32[1,2,512]{2,1,0:T(2,128)} %param.20) | copy-start | bytes 12292
  1.3 9.0 %copy-start.7 = (s32[1,512]{1,0:T(1,128)S(1)}, s32[1,512]{1,0:T(1,128)}, u32[]{:S(2)}) copy-start(s32[1,512]{1,0:T(1,128)} %param.19) | copy-start | bytes 6148
  1.7 12.3 %collective-permute-start = (f32[7,64,128]{2,1,0:T(8,128)S(1)}, f32[7,64,128]{2,1,0:T(8,128)S(1)}, u32[]{:S(2)}, u32[]{:S(2)}) collective-permute-start(f32[7,64,128]{2,1,0:T(8,128)S(1)} %pad_maximum_fusion.6), channel_id=1, source_target_pairs={{0,1},{1,2},{2,3},{3,4},{4,5},{5,6},{6,7},{7,8},{8,9},{9,10},{10,1... | collective-permute-start | bytes 688136 | tf_op jit(solution)/shard_map/ppermute | solution.py:49
  7.0 11.0 %collective-permute-start.1 = (f32[7,64,128]{2,1,0:T(8,128)S(1)}, f32[7,64,128]{2,1,0:T(8,128)S(1)}, u32[]{:S(2)}, u32[]{:S(2)}) collective-permute-start(f32[7,64,128]{2,1,0:T(8,128)S(1)} %pad_maximum_fusion.7), channel_id=1, source_target_pairs={{1,0},{2,1},{3,2},{4,3},{5,4},{6,5},{7,6},{8,7},{9,8},{10,9},{11,1... | collective-permute-start | bytes 688136 | tf_op jit(solution)/shard_map/ppermute | solution.py:52
  11.5 0.7 copy-start.9
  21.1 20.7 %collective-permute-start.2 = (f32[4,12,64,128]{3,2,1,0:T(8,128)S(1)}, f32[4,12,64,128]{3,2,1,0:T(8,128)S(1)}, u32[]{:S(2)}, u32[]{:S(2)}) collective-permute-start(f32[4,12,64,128]{3,2,1,0:T(8,128)S(1)} %get-tuple-element.6), channel_id=1, source_target_pairs={{0,1},{1,2},{2,3},{3,4},{4,5},{5,6},{6,7},{7,8},{8,9},{9,10},{10,1... | collective-permute-start | bytes 4718600 | tf_op jit(solution)/shard_map/ppermute | solution.py:28
  24.5 25.8 %collective-permute-start.3 = (f32[4,12,64,128]{3,2,1,0:T(8,128)S(1)}, f32[4,12,64,128]{3,2,1,0:T(8,128)}, u32[]{:S(2)}, u32[]{:S(2)}) collective-permute-start(f32[4,12,64,128]{3,2,1,0:T(8,128)S(1)} %get-tuple-element.5), channel_id=1, source_target_pairs={{1,0},{2,1},{3,2},{4,3},{5,4},{6,5},{7,6},{8,7},{9,8},{10,9},{11,1... | collective-permute-start | bytes 4718600 | tf_op jit(solution)/shard_map/ppermute | solution.py:29
  41.8 8.4 %copy-start.4 = (f32[4,12,64,128]{3,2,1,0:T(8,128)}, f32[4,12,64,128]{3,2,1,0:T(8,128)S(1)}, u32[]{:S(2)}) copy-start(f32[4,12,64,128]{3,2,1,0:T(8,128)S(1)} %collective-permute-done.2.refs_0_) | copy-start | bytes 4718596
  57.8 1.3 %copy-start = (f32[9,6,16,32]{3,2,1,0:T(8,128)S(1)}, f32[9,6,16,32]{3,2,1,0:T(8,128)}, u32[]{:S(2)}) copy-start(f32[9,6,16,32]{3,2,1,0:T(8,128)} %shard_map.118) | copy-start | bytes 331780
  59.7 11.0 %copy-start.6 = (f32[64,9,3,3,3]{0,4,3,2,1:T(4,128)S(1)}, f32[64,9,3,3,3]{0,4,3,2,1:T(4,128)}, u32[]{:S(2)}) copy-start(f32[64,9,3,3,3]{0,4,3,2,1:T(4,128)} %param.22) | copy-start | bytes 186628
  61.3 18.1 %all-to-all-start = ((f32[16,1,5184]{2,1,0:T(1,128)}), f32[16,1,5184]{2,1,0:T(1,128)S(1)}, u32[]{:S(2)}, u32[]{:S(2)}) async-start(f32[16,1,5184]{2,1,0:T(1,128)} %reshape.160), calls=%async_computation | async-start | bytes 671744 | tf_op jit(solution)/shard_map/all_to_all | solution.py:213
  82.4 1.7 %copy-start.10 = (f32[64]{0:T(128)S(1)}, f32[64]{0:T(128)}, u32[]{:S(2)}) copy-start(f32[64]{0:T(128)} %param.23) | copy-start | bytes 772

commit v8 on v7

--- a/solution.py
+++ b/solution.py
@@ -27,7 +27,7 @@
     backward = [(target, source) for source, target in forward]
     low = lax.ppermute(block[:, block.shape[1] - width :], axis, forward)
     high = lax.ppermute(block[:, :width], axis, backward)
-    return [low, block, high]
+    return low, high
 
 
 def input_halo(current, previous, courant, axis):
@@ -119,10 +119,9 @@
 
 
 def offset_image(pieces, offsets, margin, cells_x):
-    fields, _, size_y, size_z = pieces[0].shape
-    spans = [piece.shape[1] for piece in pieces]
-    starts = [sum(spans[:k]) for k in range(len(spans))]
-    span_x = sum(spans)
+    size_y, size_z = pieces[0][0].shape[2:]
+    fields = max(first + array.shape[0] for array, first, _, _, _ in pieces)
+    span_x = max(at + span for _, _, at, _, span in pieces)
     count = offsets.shape[0]
     blocks_x, blocks_y, blocks_z = cells_x // 4, size_y // 4, size_z // 4
     pool_z = pooling(size_z, 4)
@@ -130,10 +129,11 @@
     def kernel(offsets_ref, *refs):
         piece_refs = refs[: len(pieces)]
         pool_z_ref, out_ref, wide_ref, sum_ref, semaphores = refs[len(pieces) :]
-        copies = [
-            pltpu.make_async_copy(piece_ref, wide_ref.at[:, start : start + span], semaphores.at[k])
-            for k, (piece_ref, start, span) in enumerate(zip(piece_refs, starts, spans))
-        ]
+        copies = []
+        for k, (piece_ref, (array, first, at, taken, span)) in enumerate(zip(piece_refs, pieces)):
+            source = piece_ref.at[:, taken : taken + span] if span != array.shape[1] else piece_ref
+            target = wide_ref.at[first : first + array.shape[0], at : at + span]
+            copies.append(pltpu.make_async_copy(source, target, semaphores.at[k]))
         for copy in copies:
             copy.start()
         for copy in copies:
@@ -178,7 +178,7 @@
             ],
         ),
         out_shape=jax.ShapeDtypeStruct((count, blocks_x, blocks_y, blocks_z), jnp.float32),
-    )(offsets, *pieces, pool_z)
+    )(offsets, *[piece[0] for piece in pieces], pool_z)
 
 
 def conv_apply(padded, conv_weight, conv_bias):
@@ -210,8 +210,9 @@
         [lax.slice_in_dim(rimmed, k, k + (count - 1) * rows + 1, stride=rows, axis=2) for k in range(rows + 2)]
     )
     windows = jnp.moveaxis(windows, 3, 0)
-    received = lax.all_to_all(windows, axis, 0, 0, tiled=True)
-    return jnp.moveaxis(received.sum(axis=0), 0, 2)
+    shape = windows.shape[1:]
+    received = lax.all_to_all(windows.reshape(count, -1), axis, 0, 0, tiled=True)
+    return jnp.moveaxis(received.sum(axis=0).reshape(shape), 0, 2)
 
 
 def local(
@@ -246,9 +247,18 @@
             step_previous, step_extended, step_courant = current, levels[0], courant
         advanced = laplace_step(step_previous, step_extended, step_courant, sources)
         levels.append(advanced)
+    levels_full = list(levels)
     levels[0] = levels[0][:, 1:-1]
     fields = jnp.concatenate(levels, axis=0)
-    coarse = offset_image(halo_pieces(fields, "gx", HMAX + 4), offsets, HMAX, cells_x + 8)
+    width = HMAX + 4
+    low, high = halo_pieces(fields, "gx", width)
+    pieces = [
+        (low, 0, 0, 0, width),
+        (levels_full[0], 0, width, 1, cells_x),
+        (levels_full[1], 2, width, 0, cells_x),
+        (high, 0, width + cells_x, 0, width),
+    ]
+    coarse = offset_image(pieces, offsets, HMAX, cells_x + 8)
     summed = group_sum_windows(coarse, "shot")
     window = jnp.pad(summed, ((0, 0), (0, 0), (0, 0), (1, 1)))
     return conv_apply(window, conv_weight, conv_bias)

time: 85.7 us -> 84 us (0.980)
  other arithmetic: 8.95 us -> 6.14 us
  waiting for transfers between devices: 34.1 us -> 36.1 us
    ppermute x1, waiting for transfers between devices: 13.2 us -> 14.7 us  [halo_pieces(): low = lax.ppermute(block[:, block.shape[1] - width:], axis, forward)]
    all_to_all x1 -> x0, other arithmetic: 1.43 us -> none  [group_sum_windows(): received = lax.all_to_all(windows, axis, 0, 0, tiled=True)]
    unnamed x51 -> x53, local copies, waits for them, and re-layouts: 5.8 us -> 4.39 us
    concatenate x2 -> x1, other arithmetic: 1.85 us -> 0.43 us  [local(): fields = jnp.concatenate(levels, axis=0)]
    all_to_all x1, local copies, waits for them, and re-layouts: 0.51 us -> 1.51 us  [group_sum_windows(): lax.all_to_all(windows.reshape(count, -1), axis, 0, 0, tiled=True)]
  transfers between devices with their start and end apart: 5 -> 5, of which waited for: 4 -> 4; matrix products, arithmetic and copies ran while one was open for 8% -> 6% of each run, Pallas kernels for 0% -> 0%
where the time goes in v8:
time: 84 us; the launch traced here: 83.5 us
  waiting for transfers between devices  36.1 us (43%)
  starting transfers between devices  21.5 us (26%)
  local copies, waits for them, and re-layouts  9.04 us (11%)
  Pallas kernels  7.57 us (9%)
  other arithmetic  6.14 us (7%)
  matrix products  2.66 us (3%)
    ppermute x1, waiting for transfers between devices, halo_pieces(): low = lax.ppermute(block[:, block.shape[1] - width:], axis, forward)  14.7 us
    all_to_all x1, starting transfers between devices, group_sum_windows(): lax.all_to_all(windows.reshape(count, -1), axis, 0, 0, tiled=True)  9.04 us
    ppermute x1, waiting for transfers between devices, halo_pieces(): high = lax.ppermute(block[:, :width], axis, backward)  8.89 us
    all_to_all x1, waiting for transfers between devices, group_sum_windows(): lax.all_to_all(windows.reshape(count, -1), axis, 0, 0, tiled=True)  8.57 us
    pallas_call x1, Pallas kernels, offset_image(): pl.pallas_call(kernel, grid_spec=pltpu.PrefetchScalarGridSpec(num_scalar_...  7.57 us
    ppermute x1, starting transfers between devices, input_halo(): lax.ppermute(pack(current[:, -2:], previous[:, -1:], courant[-1:]), axis,...  5.3 us
    unnamed x53, local copies, waits for them, and re-layouts  4.39 us
    ppermute x1, waiting for transfers between devices, input_halo(): lax.ppermute(pack(current[:, :2], previous[:, :1], courant[:1]), axis, ba...  3.91 us
  transfers between devices with their start and end apart: 5, of which 4 were waited for; matrix products, arithmetic and copies ran while one was open for 6% of the time, Pallas kernels for 0%

profile of v8, /device:TPU:39, one launch (start us, length us, event | category | flops | bytes accessed | tf_op | source)
XLA Modules:
  0.0 83.5 jit_solution(3229656745779175032)
XLA Ops:
  0.0 1.2 %constant_dynamic-update-slice_fusion.1 = f32[2,16,64,128]{3,2,1,0:T(8,128)S(1)} fusion(f32[1,16,64,128]{3,2,1,0:T(8,128)} %param.13), kind=kLoop, calls=%fused_computation.97 | loop fusion | bytes 1048576
  1.5 0.2 copy-done.4
  1.7 5.3 %collective-permute-start = (f32[7,64,128]{2,1,0:T(8,128)S(1)}, f32[7,64,128]{2,1,0:T(8,128)S(1)}, u32[]{:S(2)}, u32[]{:S(2)}) collective-permute-start(f32[7,64,128]{2,1,0:T(8,128)S(1)} %pad_maximum_fusion.6), channel_id=1, source_target_pairs={{0,1},{1,2},{2,3},{3,4},{4,5},{5,6},{6,7},{7,8},{8,9},{9,10},{10,1... | collective-permute-start | bytes 688136 | tf_op jit(solution)/shard_map/ppermute | solution.py:49
  7.0 1.9 %collective-permute-start.1 = (f32[7,64,128]{2,1,0:T(8,128)S(1)}, f32[7,64,128]{2,1,0:T(8,128)S(1)}, u32[]{:S(2)}, u32[]{:S(2)}) collective-permute-start(f32[7,64,128]{2,1,0:T(8,128)S(1)} %pad_maximum_fusion.7), channel_id=1, source_target_pairs={{1,0},{2,1},{3,2},{4,3},{5,4},{6,5},{7,6},{8,7},{9,8},{10,9},{11,1... | collective-permute-start | bytes 688136 | tf_op jit(solution)/shard_map/ppermute | solution.py:52
  9.0 0.7 and_select_fusion.4
  9.7 0.7 add_bitcast_fusion
  10.4 0.3 reduce-precision_convert_fusion.1
  10.7 0.8 fusion.1
  11.6 0.6 copy-done.11
  12.3 0.4 fusion.23
  12.7 0.8 fusion
  13.6 0.4 fusion.22
  14.1 3.9 %collective-permute-done.1 = f32[7,64,128]{2,1,0:T(8,128)S(1)} collective-permute-done((f32[7,64,128]{2,1,0:T(8,128)S(1)}, f32[7,64,128]{2,1,0:T(8,128)S(1)}, u32[]{:S(2)}, u32[]{:S(2)}) %collective-permute-start.1) | collective-permute-done | bytes 229408 | tf_op jit(solution)/shard_map/ppermute | solution.py:52
  18.2 1.5 %fusion.10.refs_1_ = f32[2,18,64,128]{3,2,1,0:T(8,128)S(1)} fusion(f32[2,18,64,128]{3,2,1,0:T(8,128)S(1)} %pad_maximum_fusion.2, f32[2,1,64,128]{3,2,1,0:T(8,128)S(1)} %slice_bitcast_fusion, f32[2,1,64,128]{3,2,1,0:T(8,128)S(1)} %slice_bitcast_fusion.1, f32[2,2,64,128]{3,2,1,0:T(8,128)S(1)} %bitcast.210, ...), kind=kLoop, calls=%fused_computation.28 | loop fusion | flops 5275648 | bytes 6619136 | tf_op jit(solution)/shard_map/add | solution.py:100
  19.8 0.9 %fusion.21.refs_2_ = f32[2,16,64,128]{3,2,1,0:T(8,128)S(1)} fusion(f32[2,16,64,128]{3,2,1,0:T(8,128)S(1)} %slice.309, f32[1,18,64,128]{3,2,1,0:T(8,128)S(1)} %bitcast.201, f32[1,18,64,128]{3,2,1,0:T(8,128)S(1)} %bitcast.202, f32[2,18,64,128]{3,2,1,0:T(8,128)S(1)} %fusion.10.refs_1_, f32[2,16,64,128]{3,2,1,0:T(8,128)S(1)} %constant_dynamic-update-slice_fusion, ...), kind=kLoop, calls=%fused_computation.44 | loop fusion | flops 3407872 | bytes 6946816 | tf_op jit(solution)/shard_map/add | solution.py:100
  20.7 0.4 pad_maximum_fusion
  21.2 0.6 copy-done.1
  21.8 3.4 %collective-permute-start.2 = (f32[4,12,64,128]{3,2,1,0:T(8,128)S(1)}, f32[4,12,64,128]{3,2,1,0:T(8,128)S(1)}, u32[]{:S(2)}, u32[]{:S(2)}) collective-permute-start(f32[4,12,64,128]{3,2,1,0:T(8,128)S(1)} %get-tuple-element.6), channel_id=1, source_target_pairs={{0,1},{1,2},{2,3},{3,4},{4,5},{5,6},{6,7},{7,8},{8,9},{9,10},{10,1... | collective-permute-start | bytes 4718600 | tf_op jit(solution)/shard_map/ppermute | solution.py:28
  25.1 1.9 %collective-permute-start.3 = (f32[4,12,64,128]{3,2,1,0:T(8,128)S(1)}, f32[4,12,64,128]{3,2,1,0:T(8,128)}, u32[]{:S(2)}, u32[]{:S(2)}) collective-permute-start(f32[4,12,64,128]{3,2,1,0:T(8,128)S(1)} %get-tuple-element.5), channel_id=1, source_target_pairs={{1,0},{2,1},{3,2},{4,3},{5,4},{6,5},{7,6},{8,7},{9,8},{10,9},{11,1... | collective-permute-start | bytes 4718600 | tf_op jit(solution)/shard_map/ppermute | solution.py:29
  27.1 0.7 fusion.44.refs_4_
  27.8 14.7 %collective-permute-done.2.refs_0_ = f32[4,12,64,128]{3,2,1,0:T(8,128)S(1)} collective-permute-done((f32[4,12,64,128]{3,2,1,0:T(8,128)S(1)}, f32[4,12,64,128]{3,2,1,0:T(8,128)S(1)}, u32[]{:S(2)}, u32[]{:S(2)}) %collective-permute-start.2) | collective-permute-done | bytes 1572896 | tf_op jit(solution)/shard_map/ppermute | solution.py:28
  42.5 8.9 %collective-permute-done.3.refs_3_ = f32[4,12,64,128]{3,2,1,0:T(8,128)} collective-permute-done((f32[4,12,64,128]{3,2,1,0:T(8,128)S(1)}, f32[4,12,64,128]{3,2,1,0:T(8,128)}, u32[]{:S(2)}, u32[]{:S(2)}) %collective-permute-start.3) | collective-permute-done | bytes 1572896 | tf_op jit(solution)/shard_map/ppermute | solution.py:29
  51.4 7.6 %shard_map.118 = f32[9,6,16,32]{3,2,1,0:T(8,128)} custom-call(s32[9]{0:T(128)} %offsets_ref.1, f32[4,12,64,128]{3,2,1,0:T(8,128)} %copy-done.6, f32[2,18,64,128]{3,2,1,0:T(8,128)} %copy-done, f32[2,16,64,128]{3,2,1,0:T(8,128)} %copy-done.1, f32[4,12,64,128]{3,2,1,0:T(8,128)} %collective-permute-done.3.refs_3_, f32[128,32]{1,0:T(8,128)} %fusion.44.refs_4_), custom_call_target="tpu_custom_call" | custom-call | tf_op jit(solution)/shard_map/pallas_call | solution.py:166
  59.0 1.3 %fusion.24 = (f32[1,9,6,16,32]{4,3,2,1,0:T(8,128)S(1)}, f32[1,9,6,16,32]{4,3,2,1,0:T(8,128)S(1)}) fusion(f32[9,6,16,32]{3,2,1,0:T(8,128)} %shard_map.118), kind=kLoop, calls=%fused_computation.61 | loop fusion | bytes 331776 | tf_op jit(solution)/shard_map/stack | solution.py:209
  60.4 0.4 copy.51
  60.9 1.5 %all_to_all.8 = f32[16,1,5184]{2,1,0:T(1,128)} reshape(f32[16,3,9,6,32]{4,3,2,1,0:T(8,128)S(1)} %copy.51) | data formatting | bytes 663552 | tf_op jit(solution)/shard_map/all_to_all | solution.py:214
  62.4 9.0 %all-to-all-start = ((f32[16,1,5184]{2,1,0:T(1,128)}), f32[16,1,5184]{2,1,0:T(1,128)S(1)}, u32[]{:S(2)}, u32[]{:S(2)}) async-start(f32[16,1,5184]{2,1,0:T(1,128)} %all_to_all.8), calls=%async_computation | async-start | bytes 671744 | tf_op jit(solution)/shard_map/all_to_all | solution.py:214
  71.5 8.6 %all-to-all-done = f32[16,1,5184]{2,1,0:T(1,128)S(1)} async-done(((f32[16,1,5184]{2,1,0:T(1,128)}), f32[16,1,5184]{2,1,0:T(1,128)S(1)}, u32[]{:S(2)}, u32[]{:S(2)}) %all-to-all-start) | async-done | bytes 331808 | tf_op jit(solution)/shard_map/all_to_all | solution.py:214
  80.1 0.2 reduce_sum.9
  82.2 0.2 reshape.165
  82.4 0.4 fusion.13
  82.8 0.7 copy.79
  (79 shorter events, 3.0 us)
Async XLA Ops:
  0.0 1.3 %copy-start.7 = (f32[1,16,64,128]{3,2,1,0:T(8,128)S(1)}, f32[1,16,64,128]{3,2,1,0:T(8,128)}, u32[]{:S(2)}) copy-start(f32[1,16,64,128]{3,2,1,0:T(8,128)} %param.15) | copy-start | bytes 1572868
  0.0 1.4 %copy-start.3 = (f32[16,64,128]{2,1,0:T(8,128)S(1)}, f32[16,64,128]{2,1,0:T(8,128)}, u32[]{:S(2)}) copy-start(f32[16,64,128]{2,1,0:T(8,128)} %param.16) | copy-start | bytes 1572868
  0.0 1.5 %copy-start.5 = (f32[1,16,64,128]{3,2,1,0:T(8,128)S(1)}, f32[1,16,64,128]{3,2,1,0:T(8,128)}, u32[]{:S(2)}) copy-start(f32[1,16,64,128]{3,2,1,0:T(8,128)} %param.12) | copy-start | bytes 1572868
  0.0 1.7 %copy-start.4 = (f32[1,16,64,128]{3,2,1,0:T(8,128)S(1)}, f32[1,16,64,128]{3,2,1,0:T(8,128)}, u32[]{:S(2)}) copy-start(f32[1,16,64,128]{3,2,1,0:T(8,128)} %param.14) | copy-start | bytes 1572868
  1.4 7.6 %copy-start.10 = (f32[1,2,512]{2,1,0:T(2,128)S(1)}, f32[1,2,512]{2,1,0:T(2,128)}, u32[]{:S(2)}) copy-start(f32[1,2,512]{2,1,0:T(2,128)} %param.20) | copy-start | bytes 12292
  1.4 9.0 %copy-start.9 = (s32[1,512]{1,0:T(1,128)S(1)}, s32[1,512]{1,0:T(1,128)}, u32[]{:S(2)}) copy-start(s32[1,512]{1,0:T(1,128)} %param.19) | copy-start | bytes 6148
  1.7 12.3 %collective-permute-start = (f32[7,64,128]{2,1,0:T(8,128)S(1)}, f32[7,64,128]{2,1,0:T(8,128)S(1)}, u32[]{:S(2)}, u32[]{:S(2)}) collective-permute-start(f32[7,64,128]{2,1,0:T(8,128)S(1)} %pad_maximum_fusion.6), channel_id=1, source_target_pairs={{0,1},{1,2},{2,3},{3,4},{4,5},{5,6},{6,7},{7,8},{8,9},{9,10},{10,1... | collective-permute-start | bytes 688136 | tf_op jit(solution)/shard_map/ppermute | solution.py:49
  7.0 11.0 %collective-permute-start.1 = (f32[7,64,128]{2,1,0:T(8,128)S(1)}, f32[7,64,128]{2,1,0:T(8,128)S(1)}, u32[]{:S(2)}, u32[]{:S(2)}) collective-permute-start(f32[7,64,128]{2,1,0:T(8,128)S(1)} %pad_maximum_fusion.7), channel_id=1, source_target_pairs={{1,0},{2,1},{3,2},{4,3},{5,4},{6,5},{7,6},{8,7},{9,8},{10,9},{11,1... | collective-permute-start | bytes 688136 | tf_op jit(solution)/shard_map/ppermute | solution.py:52
  11.5 0.7 copy-start.11
  19.7 1.0 %copy-start = (f32[2,18,64,128]{3,2,1,0:T(8,128)}, f32[2,18,64,128]{3,2,1,0:T(8,128)S(1)}, u32[]{:S(2)}) copy-start(f32[2,18,64,128]{3,2,1,0:T(8,128)S(1)} %fusion.10.refs_1_) | copy-start | bytes 3538948
  20.7 1.0 %copy-start.1 = (f32[2,16,64,128]{3,2,1,0:T(8,128)}, f32[2,16,64,128]{3,2,1,0:T(8,128)S(1)}, u32[]{:S(2)}) copy-start(f32[2,16,64,128]{3,2,1,0:T(8,128)S(1)} %fusion.21.refs_2_) | copy-start | bytes 3145732
  21.8 20.7 %collective-permute-start.2 = (f32[4,12,64,128]{3,2,1,0:T(8,128)S(1)}, f32[4,12,64,128]{3,2,1,0:T(8,128)S(1)}, u32[]{:S(2)}, u32[]{:S(2)}) collective-permute-start(f32[4,12,64,128]{3,2,1,0:T(8,128)S(1)} %get-tuple-element.6), channel_id=1, source_target_pairs={{0,1},{1,2},{2,3},{3,4},{4,5},{5,6},{6,7},{7,8},{8,9},{9,10},{10,1... | collective-permute-start | bytes 4718600 | tf_op jit(solution)/shard_map/ppermute | solution.py:28
  25.1 26.2 %collective-permute-start.3 = (f32[4,12,64,128]{3,2,1,0:T(8,128)S(1)}, f32[4,12,64,128]{3,2,1,0:T(8,128)}, u32[]{:S(2)}, u32[]{:S(2)}) collective-permute-start(f32[4,12,64,128]{3,2,1,0:T(8,128)S(1)} %get-tuple-element.5), channel_id=1, source_target_pairs={{1,0},{2,1},{3,2},{4,3},{5,4},{6,5},{7,6},{8,7},{9,8},{10,9},{11,1... | collective-permute-start | bytes 4718600 | tf_op jit(solution)/shard_map/ppermute | solution.py:29
  42.5 8.9 %copy-start.6 = (f32[4,12,64,128]{3,2,1,0:T(8,128)}, f32[4,12,64,128]{3,2,1,0:T(8,128)S(1)}, u32[]{:S(2)}) copy-start(f32[4,12,64,128]{3,2,1,0:T(8,128)S(1)} %collective-permute-done.2.refs_0_) | copy-start | bytes 4718596
  58.9 1.3 %copy-start.2 = (f32[9,6,16,32]{3,2,1,0:T(8,128)S(1)}, f32[9,6,16,32]{3,2,1,0:T(8,128)}, u32[]{:S(2)}) copy-start(f32[9,6,16,32]{3,2,1,0:T(8,128)} %shard_map.118) | copy-start | bytes 331780
  60.9 10.6 %copy-start.8 = (f32[64,9,3,3,3]{0,4,3,2,1:T(4,128)S(1)}, f32[64,9,3,3,3]{0,4,3,2,1:T(4,128)}, u32[]{:S(2)}) copy-start(f32[64,9,3,3,3]{0,4,3,2,1:T(4,128)} %param.22) | copy-start | bytes 186628
  62.4 17.7 %all-to-all-start = ((f32[16,1,5184]{2,1,0:T(1,128)}), f32[16,1,5184]{2,1,0:T(1,128)S(1)}, u32[]{:S(2)}, u32[]{:S(2)}) async-start(f32[16,1,5184]{2,1,0:T(1,128)} %all_to_all.8), calls=%async_computation | async-start | bytes 671744 | tf_op jit(solution)/shard_map/all_to_all | solution.py:214
  80.9 1.5 %copy-start.12 = (f32[64]{0:T(128)S(1)}, f32[64]{0:T(128)}, u32[]{:S(2)}) copy-start(f32[64]{0:T(128)} %param.23) | copy-start | bytes 772

commit v9 on v8

--- a/solution.py
+++ b/solution.py
@@ -161,7 +161,7 @@
             out_ref[index] = (pooled * (1.0 / 64.0)).reshape(blocks_x, blocks_y, blocks_z)
             return carry
 
-        lax.fori_loop(0, count, per_offset, 0)
+        lax.fori_loop(0, count, per_offset, 0, unroll=True)
 
     return pl.pallas_call(
         kernel,

time: 84 us -> 82.9 us (0.987)
  Pallas kernels: 7.57 us -> 6.55 us
    pallas_call x1, Pallas kernels: 7.57 us -> 6.55 us  [offset_image(): pl.pallas_call(kernel, grid_spec=pltpu.PrefetchScalarGridSpec(num_scalar_...]
where the time goes in v9:
time: 82.9 us; the launch traced here: 82.5 us
  waiting for transfers between devices  36.3 us (44%)
  starting transfers between devices  21.3 us (26%)
  local copies, waits for them, and re-layouts  9.04 us (11%)
  Pallas kernels  6.55 us (8%)
  other arithmetic  6.14 us (7%)
  matrix products  2.66 us (3%)
    ppermute x1, waiting for transfers between devices, halo_pieces(): low = lax.ppermute(block[:, block.shape[1] - width:], axis, forward)  14.7 us
    ppermute x1, waiting for transfers between devices, halo_pieces(): high = lax.ppermute(block[:, :width], axis, backward)  9.17 us
    all_to_all x1, starting transfers between devices, group_sum_windows(): lax.all_to_all(windows.reshape(count, -1), axis, 0, 0, tiled=True)  8.76 us
    all_to_all x1, waiting for transfers between devices, group_sum_windows(): lax.all_to_all(windows.reshape(count, -1), axis, 0, 0, tiled=True)  8.57 us
    pallas_call x1, Pallas kernels, offset_image(): pl.pallas_call(kernel, grid_spec=pltpu.PrefetchScalarGridSpec(num_scalar_...  6.55 us
    ppermute x1, starting transfers between devices, input_halo(): lax.ppermute(pack(current[:, -2:], previous[:, -1:], courant[-1:]), axis,...  5.3 us
    unnamed x53, local copies, waits for them, and re-layouts  4.39 us
    ppermute x1, waiting for transfers between devices, input_halo(): lax.ppermute(pack(current[:, :2], previous[:, :1], courant[:1]), axis, ba...  3.91 us
  transfers between devices with their start and end apart: 5, of which 4 were waited for; matrix products, arithmetic and copies ran while one was open for 6% of the time, Pallas kernels for 0%

profile of v9, /device:TPU:39, one launch (start us, length us, event | category | flops | bytes accessed | tf_op | source)
XLA Modules:
  0.0 82.5 jit_solution(13508845310016945579)
XLA Ops:
  0.0 1.2 %constant_dynamic-update-slice_fusion.1 = f32[2,16,64,128]{3,2,1,0:T(8,128)S(1)} fusion(f32[1,16,64,128]{3,2,1,0:T(8,128)} %param.13), kind=kLoop, calls=%fused_computation.97 | loop fusion | bytes 1048576
  1.5 0.2 copy-done.4
  1.7 5.3 %collective-permute-start = (f32[7,64,128]{2,1,0:T(8,128)S(1)}, f32[7,64,128]{2,1,0:T(8,128)S(1)}, u32[]{:S(2)}, u32[]{:S(2)}) collective-permute-start(f32[7,64,128]{2,1,0:T(8,128)S(1)} %pad_maximum_fusion.6), channel_id=1, source_target_pairs={{0,1},{1,2},{2,3},{3,4},{4,5},{5,6},{6,7},{7,8},{8,9},{9,10},{10,1... | collective-permute-start | bytes 688136 | tf_op jit(solution)/shard_map/ppermute | solution.py:49
  7.0 1.9 %collective-permute-start.1 = (f32[7,64,128]{2,1,0:T(8,128)S(1)}, f32[7,64,128]{2,1,0:T(8,128)S(1)}, u32[]{:S(2)}, u32[]{:S(2)}) collective-permute-start(f32[7,64,128]{2,1,0:T(8,128)S(1)} %pad_maximum_fusion.7), channel_id=1, source_target_pairs={{1,0},{2,1},{3,2},{4,3},{5,4},{6,5},{7,6},{8,7},{9,8},{10,9},{11,1... | collective-permute-start | bytes 688136 | tf_op jit(solution)/shard_map/ppermute | solution.py:52
  9.0 0.7 and_select_fusion.4
  9.7 0.7 add_bitcast_fusion
  10.4 0.3 reduce-precision_convert_fusion.1
  10.7 0.8 fusion.1
  11.6 0.6 copy-done.11
  12.3 0.4 fusion.23
  12.7 0.8 fusion
  13.6 0.4 fusion.22
  14.1 3.9 %collective-permute-done.1 = f32[7,64,128]{2,1,0:T(8,128)S(1)} collective-permute-done((f32[7,64,128]{2,1,0:T(8,128)S(1)}, f32[7,64,128]{2,1,0:T(8,128)S(1)}, u32[]{:S(2)}, u32[]{:S(2)}) %collective-permute-start.1) | collective-permute-done | bytes 229408 | tf_op jit(solution)/shard_map/ppermute | solution.py:52
  18.2 1.5 %fusion.10.refs_1_ = f32[2,18,64,128]{3,2,1,0:T(8,128)S(1)} fusion(f32[2,18,64,128]{3,2,1,0:T(8,128)S(1)} %pad_maximum_fusion.2, f32[2,1,64,128]{3,2,1,0:T(8,128)S(1)} %slice_bitcast_fusion, f32[2,1,64,128]{3,2,1,0:T(8,128)S(1)} %slice_bitcast_fusion.1, f32[2,2,64,128]{3,2,1,0:T(8,128)S(1)} %bitcast.210, ...), kind=kLoop, calls=%fused_computation.28 | loop fusion | flops 5275648 | bytes 6619136 | tf_op jit(solution)/shard_map/add | solution.py:100
  19.8 0.9 %fusion.21.refs_2_ = f32[2,16,64,128]{3,2,1,0:T(8,128)S(1)} fusion(f32[2,16,64,128]{3,2,1,0:T(8,128)S(1)} %slice.309, f32[1,18,64,128]{3,2,1,0:T(8,128)S(1)} %bitcast.201, f32[1,18,64,128]{3,2,1,0:T(8,128)S(1)} %bitcast.202, f32[2,18,64,128]{3,2,1,0:T(8,128)S(1)} %fusion.10.refs_1_, f32[2,16,64,128]{3,2,1,0:T(8,128)S(1)} %constant_dynamic-update-slice_fusion, ...), kind=kLoop, calls=%fused_computation.44 | loop fusion | flops 3407872 | bytes 6946816 | tf_op jit(solution)/shard_map/add | solution.py:100
  20.7 0.4 pad_maximum_fusion
  21.2 0.6 copy-done.1
  21.8 3.4 %collective-permute-start.2 = (f32[4,12,64,128]{3,2,1,0:T(8,128)S(1)}, f32[4,12,64,128]{3,2,1,0:T(8,128)S(1)}, u32[]{:S(2)}, u32[]{:S(2)}) collective-permute-start(f32[4,12,64,128]{3,2,1,0:T(8,128)S(1)} %get-tuple-element.6), channel_id=1, source_target_pairs={{0,1},{1,2},{2,3},{3,4},{4,5},{5,6},{6,7},{7,8},{8,9},{9,10},{10,1... | collective-permute-start | bytes 4718600 | tf_op jit(solution)/shard_map/ppermute | solution.py:28
  25.1 1.9 %collective-permute-start.3 = (f32[4,12,64,128]{3,2,1,0:T(8,128)S(1)}, f32[4,12,64,128]{3,2,1,0:T(8,128)}, u32[]{:S(2)}, u32[]{:S(2)}) collective-permute-start(f32[4,12,64,128]{3,2,1,0:T(8,128)S(1)} %get-tuple-element.5), channel_id=1, source_target_pairs={{1,0},{2,1},{3,2},{4,3},{5,4},{6,5},{7,6},{8,7},{9,8},{10,9},{11,1... | collective-permute-start | bytes 4718600 | tf_op jit(solution)/shard_map/ppermute | solution.py:29
  27.1 0.7 fusion.44.refs_4_
  27.8 14.7 %collective-permute-done.2.refs_0_ = f32[4,12,64,128]{3,2,1,0:T(8,128)S(1)} collective-permute-done((f32[4,12,64,128]{3,2,1,0:T(8,128)S(1)}, f32[4,12,64,128]{3,2,1,0:T(8,128)S(1)}, u32[]{:S(2)}, u32[]{:S(2)}) %collective-permute-start.2) | collective-permute-done | bytes 1572896 | tf_op jit(solution)/shard_map/ppermute | solution.py:28
  42.5 9.2 %collective-permute-done.3.refs_3_ = f32[4,12,64,128]{3,2,1,0:T(8,128)} collective-permute-done((f32[4,12,64,128]{3,2,1,0:T(8,128)S(1)}, f32[4,12,64,128]{3,2,1,0:T(8,128)}, u32[]{:S(2)}, u32[]{:S(2)}) %collective-permute-start.3) | collective-permute-done | bytes 1572896 | tf_op jit(solution)/shard_map/ppermute | solution.py:29
  51.6 6.5 %shard_map.118 = f32[9,6,16,32]{3,2,1,0:T(8,128)} custom-call(s32[9]{0:T(128)} %offsets_ref.1, f32[4,12,64,128]{3,2,1,0:T(8,128)} %copy-done.6, f32[2,18,64,128]{3,2,1,0:T(8,128)} %copy-done, f32[2,16,64,128]{3,2,1,0:T(8,128)} %copy-done.1, f32[4,12,64,128]{3,2,1,0:T(8,128)} %collective-permute-done.3.refs_3_, f32[128,32]{1,0:T(8,128)} %fusion.44.refs_4_), custom_call_target="tpu_custom_call" | custom-call | tf_op jit(solution)/shard_map/pallas_call | solution.py:166
  58.2 1.3 %fusion.24 = (f32[1,9,6,16,32]{4,3,2,1,0:T(8,128)S(1)}, f32[1,9,6,16,32]{4,3,2,1,0:T(8,128)S(1)}) fusion(f32[9,6,16,32]{3,2,1,0:T(8,128)} %shard_map.118), kind=kLoop, calls=%fused_computation.61 | loop fusion | bytes 331776 | tf_op jit(solution)/shard_map/stack | solution.py:209
  59.7 0.4 copy.51
  60.1 1.5 %all_to_all.8 = f32[16,1,5184]{2,1,0:T(1,128)} reshape(f32[16,3,9,6,32]{4,3,2,1,0:T(8,128)S(1)} %copy.51) | data formatting | bytes 663552 | tf_op jit(solution)/shard_map/all_to_all | solution.py:214
  61.6 8.8 %all-to-all-start = ((f32[16,1,5184]{2,1,0:T(1,128)}), f32[16,1,5184]{2,1,0:T(1,128)S(1)}, u32[]{:S(2)}, u32[]{:S(2)}) async-start(f32[16,1,5184]{2,1,0:T(1,128)} %all_to_all.8), calls=%async_computation | async-start | bytes 671744 | tf_op jit(solution)/shard_map/all_to_all | solution.py:214
  70.5 8.6 %all-to-all-done = f32[16,1,5184]{2,1,0:T(1,128)S(1)} async-done(((f32[16,1,5184]{2,1,0:T(1,128)}), f32[16,1,5184]{2,1,0:T(1,128)S(1)}, u32[]{:S(2)}, u32[]{:S(2)}) %all-to-all-start) | async-done | bytes 331808 | tf_op jit(solution)/shard_map/all_to_all | solution.py:214
  79.0 0.2 reduce_sum.9
  81.1 0.2 reshape.165
  81.4 0.4 fusion.13
  81.8 0.7 copy.79
  (79 shorter events, 3.0 us)
Async XLA Ops:
  0.0 1.3 %copy-start.7 = (f32[1,16,64,128]{3,2,1,0:T(8,128)S(1)}, f32[1,16,64,128]{3,2,1,0:T(8,128)}, u32[]{:S(2)}) copy-start(f32[1,16,64,128]{3,2,1,0:T(8,128)} %param.15) | copy-start | bytes 1572868
  0.0 1.4 %copy-start.3 = (f32[16,64,128]{2,1,0:T(8,128)S(1)}, f32[16,64,128]{2,1,0:T(8,128)}, u32[]{:S(2)}) copy-start(f32[16,64,128]{2,1,0:T(8,128)} %param.16) | copy-start | bytes 1572868
  0.0 1.5 %copy-start.5 = (f32[1,16,64,128]{3,2,1,0:T(8,128)S(1)}, f32[1,16,64,128]{3,2,1,0:T(8,128)}, u32[]{:S(2)}) copy-start(f32[1,16,64,128]{3,2,1,0:T(8,128)} %param.12) | copy-start | bytes 1572868
  0.0 1.7 %copy-start.4 = (f32[1,16,64,128]{3,2,1,0:T(8,128)S(1)}, f32[1,16,64,128]{3,2,1,0:T(8,128)}, u32[]{:S(2)}) copy-start(f32[1,16,64,128]{3,2,1,0:T(8,128)} %param.14) | copy-start | bytes 1572868
  1.4 7.6 %copy-start.10 = (f32[1,2,512]{2,1,0:T(2,128)S(1)}, f32[1,2,512]{2,1,0:T(2,128)}, u32[]{:S(2)}) copy-start(f32[1,2,512]{2,1,0:T(2,128)} %param.20) | copy-start | bytes 12292
  1.4 9.0 %copy-start.9 = (s32[1,512]{1,0:T(1,128)S(1)}, s32[1,512]{1,0:T(1,128)}, u32[]{:S(2)}) copy-start(s32[1,512]{1,0:T(1,128)} %param.19) | copy-start | bytes 6148
  1.7 12.3 %collective-permute-start = (f32[7,64,128]{2,1,0:T(8,128)S(1)}, f32[7,64,128]{2,1,0:T(8,128)S(1)}, u32[]{:S(2)}, u32[]{:S(2)}) collective-permute-start(f32[7,64,128]{2,1,0:T(8,128)S(1)} %pad_maximum_fusion.6), channel_id=1, source_target_pairs={{0,1},{1,2},{2,3},{3,4},{4,5},{5,6},{6,7},{7,8},{8,9},{9,10},{10,1... | collective-permute-start | bytes 688136 | tf_op jit(solution)/shard_map/ppermute | solution.py:49
  7.0 11.0 %collective-permute-start.1 = (f32[7,64,128]{2,1,0:T(8,128)S(1)}, f32[7,64,128]{2,1,0:T(8,128)S(1)}, u32[]{:S(2)}, u32[]{:S(2)}) collective-permute-start(f32[7,64,128]{2,1,0:T(8,128)S(1)} %pad_maximum_fusion.7), channel_id=1, source_target_pairs={{1,0},{2,1},{3,2},{4,3},{5,4},{6,5},{7,6},{8,7},{9,8},{10,9},{11,1... | collective-permute-start | bytes 688136 | tf_op jit(solution)/shard_map/ppermute | solution.py:52
  11.5 0.7 copy-start.11
  19.7 1.0 %copy-start = (f32[2,18,64,128]{3,2,1,0:T(8,128)}, f32[2,18,64,128]{3,2,1,0:T(8,128)S(1)}, u32[]{:S(2)}) copy-start(f32[2,18,64,128]{3,2,1,0:T(8,128)S(1)} %fusion.10.refs_1_) | copy-start | bytes 3538948
  20.7 1.0 %copy-start.1 = (f32[2,16,64,128]{3,2,1,0:T(8,128)}, f32[2,16,64,128]{3,2,1,0:T(8,128)S(1)}, u32[]{:S(2)}) copy-start(f32[2,16,64,128]{3,2,1,0:T(8,128)S(1)} %fusion.21.refs_2_) | copy-start | bytes 3145732
  21.8 20.7 %collective-permute-start.2 = (f32[4,12,64,128]{3,2,1,0:T(8,128)S(1)}, f32[4,12,64,128]{3,2,1,0:T(8,128)S(1)}, u32[]{:S(2)}, u32[]{:S(2)}) collective-permute-start(f32[4,12,64,128]{3,2,1,0:T(8,128)S(1)} %get-tuple-element.6), channel_id=1, source_target_pairs={{0,1},{1,2},{2,3},{3,4},{4,5},{5,6},{6,7},{7,8},{8,9},{9,10},{10,1... | collective-permute-start | bytes 4718600 | tf_op jit(solution)/shard_map/ppermute | solution.py:28
  25.1 26.5 %collective-permute-start.3 = (f32[4,12,64,128]{3,2,1,0:T(8,128)S(1)}, f32[4,12,64,128]{3,2,1,0:T(8,128)}, u32[]{:S(2)}, u32[]{:S(2)}) collective-permute-start(f32[4,12,64,128]{3,2,1,0:T(8,128)S(1)} %get-tuple-element.5), channel_id=1, source_target_pairs={{1,0},{2,1},{3,2},{4,3},{5,4},{6,5},{7,6},{8,7},{9,8},{10,9},{11,1... | collective-permute-start | bytes 4718600 | tf_op jit(solution)/shard_map/ppermute | solution.py:29
  42.5 9.2 %copy-start.6 = (f32[4,12,64,128]{3,2,1,0:T(8,128)}, f32[4,12,64,128]{3,2,1,0:T(8,128)S(1)}, u32[]{:S(2)}) copy-start(f32[4,12,64,128]{3,2,1,0:T(8,128)S(1)} %collective-permute-done.2.refs_0_) | copy-start | bytes 4718596
  58.2 1.3 %copy-start.2 = (f32[9,6,16,32]{3,2,1,0:T(8,128)S(1)}, f32[9,6,16,32]{3,2,1,0:T(8,128)}, u32[]{:S(2)}) copy-start(f32[9,6,16,32]{3,2,1,0:T(8,128)} %shard_map.118) | copy-start | bytes 331780
  60.1 10.3 %copy-start.8 = (f32[64,9,3,3,3]{0,4,3,2,1:T(4,128)S(1)}, f32[64,9,3,3,3]{0,4,3,2,1:T(4,128)}, u32[]{:S(2)}) copy-start(f32[64,9,3,3,3]{0,4,3,2,1:T(4,128)} %param.22) | copy-start | bytes 186628
  61.6 17.4 %all-to-all-start = ((f32[16,1,5184]{2,1,0:T(1,128)}), f32[16,1,5184]{2,1,0:T(1,128)S(1)}, u32[]{:S(2)}, u32[]{:S(2)}) async-start(f32[16,1,5184]{2,1,0:T(1,128)} %all_to_all.8), calls=%async_computation | async-start | bytes 671744 | tf_op jit(solution)/shard_map/all_to_all | solution.py:214
  79.9 1.5 %copy-start.12 = (f32[64]{0:T(128)S(1)}, f32[64]{0:T(128)}, u32[]{:S(2)}) copy-start(f32[64]{0:T(128)} %param.23) | copy-start | bytes 772

commit v10 on v9

--- a/solution.py
+++ b/solution.py
@@ -250,7 +250,7 @@
     levels_full = list(levels)
     levels[0] = levels[0][:, 1:-1]
     fields = jnp.concatenate(levels, axis=0)
-    width = HMAX + 4
+    width = HMAX
     low, high = halo_pieces(fields, "gx", width)
     pieces = [
         (low, 0, 0, 0, width),
@@ -258,9 +258,10 @@
         (levels_full[1], 2, width, 0, cells_x),
         (high, 0, width + cells_x, 0, width),
     ]
-    coarse = offset_image(pieces, offsets, HMAX, cells_x + 8)
+    coarse = offset_image(pieces, offsets, HMAX, cells_x)
     summed = group_sum_windows(coarse, "shot")
-    window = jnp.pad(summed, ((0, 0), (0, 0), (0, 0), (1, 1)))
+    rimmed = padded_2(summed, (("gx", 1),), 1)
+    window = jnp.pad(rimmed, ((0, 0), (0, 0), (0, 0), (1, 1)))
     return conv_apply(window, conv_weight, conv_bias)
 
 

time: 82.9 us -> 86.3 us (1.041)
  blocking collectives: 0 us -> 16.2 us
  waiting for transfers between devices: 36.3 us -> 27.6 us
  starting transfers between devices: 21.3 us -> 17.8 us
  other arithmetic: 6.14 us -> 7.1 us
  Pallas kernels: 6.55 us -> 5.62 us
    all_to_all x0 -> x1, blocking collectives: none -> 16.2 us  [group_sum_windows(): lax.all_to_all(windows.reshape(count, -1), axis, 0, 0, tiled=True)]
    all_to_all x1 -> x0, starting transfers between devices: 8.76 us -> none  [group_sum_windows(): lax.all_to_all(windows.reshape(count, -1), axis, 0, 0, tiled=True)]
    all_to_all x1 -> x0, waiting for transfers between devices: 8.57 us -> none  [group_sum_windows(): lax.all_to_all(windows.reshape(count, -1), axis, 0, 0, tiled=True)]
    ppermute x0 -> x2, waiting for transfers between devices: none -> 6.63 us  [the longest x1 6.63 us: padded_2(): lax.ppermute(lax.slice_in_dim(block, 0, width, axis=dim), axis, backward)]
    ppermute x1, waiting for transfers between devices: 14.7 us -> 9.07 us  [halo_pieces(): low = lax.ppermute(block[:, block.shape[1] - width:], axis, forward)]
    ppermute x0 -> x2, starting transfers between devices: none -> 5.31 us  [the longest x1 3.39 us: padded_2(): lax.ppermute(lax.slice_in_dim(block, block.shape[dim] - width, None, axis...]
    ppermute x1, waiting for transfers between devices: 9.17 us -> 8.01 us  [halo_pieces(): high = lax.ppermute(block[:, :width], axis, backward)]
    all_to_all x1, local copies, waits for them, and re-layouts: 1.51 us -> 0.57 us  [group_sum_windows(): lax.all_to_all(windows.reshape(count, -1), axis, 0, 0, tiled=True)]
  transfers between devices with their start and end apart: 5 -> 6, of which waited for: 4 -> 4; matrix products, arithmetic and copies ran while one was open for 6% -> 6% of each run, Pallas kernels for 0% -> 0%
where the time goes in v10:
time: 86.3 us; the launch traced here: 85.8 us
  waiting for transfers between devices  27.6 us (32%)
  starting transfers between devices  17.8 us (21%)
  blocking collectives  16.2 us (19%)
  local copies, waits for them, and re-layouts  8.26 us (10%)
  other arithmetic  7.1 us (8%)
  Pallas kernels  5.62 us (7%)
  matrix products  2.66 us (3%)
    all_to_all x1, blocking collectives, group_sum_windows(): lax.all_to_all(windows.reshape(count, -1), axis, 0, 0, tiled=True)  16.2 us
    ppermute x1, waiting for transfers between devices, halo_pieces(): low = lax.ppermute(block[:, block.shape[1] - width:], axis, forward)  9.07 us
    ppermute x1, waiting for transfers between devices, halo_pieces(): high = lax.ppermute(block[:, :width], axis, backward)  8.01 us
    ppermute x1, waiting for transfers between devices, padded_2(): lax.ppermute(lax.slice_in_dim(block, 0, width, axis=dim), axis, backward)  6.63 us
    pallas_call x1, Pallas kernels, offset_image(): pl.pallas_call(kernel, grid_spec=pltpu.PrefetchScalarGridSpec(num_scalar_...  5.62 us
    ppermute x1, starting transfers between devices, input_halo(): lax.ppermute(pack(current[:, -2:], previous[:, -1:], courant[-1:]), axis,...  5.3 us
    unnamed x47, local copies, waits for them, and re-layouts  4.8 us
    ppermute x1, waiting for transfers between devices, input_halo(): lax.ppermute(pack(current[:, :2], previous[:, :1], courant[:1]), axis, ba...  3.91 us
  transfers between devices with their start and end apart: 6, of which 4 were waited for; matrix products, arithmetic and copies ran while one was open for 6% of the time, Pallas kernels for 0%

profile of v10, /device:TPU:39, one launch (start us, length us, event | category | flops | bytes accessed | tf_op | source)
XLA Modules:
  0.0 85.8 jit_solution(14938380634564277971)
XLA Ops:
  0.0 1.2 %constant_dynamic-update-slice_fusion.1 = f32[2,16,64,128]{3,2,1,0:T(8,128)S(1)} fusion(f32[1,16,64,128]{3,2,1,0:T(8,128)} %param.13), kind=kLoop, calls=%fused_computation.102 | loop fusion | bytes 1048576
  1.7 5.3 %collective-permute-start = (f32[7,64,128]{2,1,0:T(8,128)S(1)}, f32[7,64,128]{2,1,0:T(8,128)S(1)}, u32[]{:S(2)}, u32[]{:S(2)}) collective-permute-start(f32[7,64,128]{2,1,0:T(8,128)S(1)} %pad_maximum_fusion.6), channel_id=1, source_target_pairs={{0,1},{1,2},{2,3},{3,4},{4,5},{5,6},{6,7},{7,8},{8,9},{9,10},{10,1... | collective-permute-start | bytes 688136 | tf_op jit(solution)/shard_map/ppermute | solution.py:49
  7.0 1.9 %collective-permute-start.1 = (f32[7,64,128]{2,1,0:T(8,128)S(1)}, f32[7,64,128]{2,1,0:T(8,128)S(1)}, u32[]{:S(2)}, u32[]{:S(2)}) collective-permute-start(f32[7,64,128]{2,1,0:T(8,128)S(1)} %pad_maximum_fusion.7), channel_id=1, source_target_pairs={{1,0},{2,1},{3,2},{4,3},{5,4},{6,5},{7,6},{8,7},{9,8},{10,9},{11,1... | collective-permute-start | bytes 688136 | tf_op jit(solution)/shard_map/ppermute | solution.py:52
  9.0 0.7 and_select_fusion.4
  9.7 0.7 add_bitcast_fusion
  10.4 0.3 reduce-precision_convert_fusion.1
  10.7 0.8 fusion.1
  11.6 0.6 copy-done.11
  12.3 0.4 fusion.23
  12.7 0.8 fusion
  13.6 0.4 fusion.22
  14.1 3.9 %collective-permute-done.1 = f32[7,64,128]{2,1,0:T(8,128)S(1)} collective-permute-done((f32[7,64,128]{2,1,0:T(8,128)S(1)}, f32[7,64,128]{2,1,0:T(8,128)S(1)}, u32[]{:S(2)}, u32[]{:S(2)}) %collective-permute-start.1) | collective-permute-done | bytes 229408 | tf_op jit(solution)/shard_map/ppermute | solution.py:52
  18.2 1.5 %fusion.9.refs_1_ = f32[2,18,64,128]{3,2,1,0:T(8,128)S(1)} fusion(f32[2,18,64,128]{3,2,1,0:T(8,128)S(1)} %pad_maximum_fusion.1, f32[2,1,64,128]{3,2,1,0:T(8,128)S(1)} %slice_bitcast_fusion, f32[2,1,64,128]{3,2,1,0:T(8,128)S(1)} %slice_bitcast_fusion.1, f32[2,2,64,128]{3,2,1,0:T(8,128)S(1)} %bitcast.230, ...), kind=kLoop, calls=%fused_computation.25 | loop fusion | flops 5275648 | bytes 6619136 | tf_op jit(solution)/shard_map/add | solution.py:100
  19.8 0.9 %fusion.21.refs_2_ = f32[2,16,64,128]{3,2,1,0:T(8,128)S(1)} fusion(f32[2,16,64,128]{3,2,1,0:T(8,128)S(1)} %slice.326, f32[1,18,64,128]{3,2,1,0:T(8,128)S(1)} %bitcast.221, f32[1,18,64,128]{3,2,1,0:T(8,128)S(1)} %bitcast.222, f32[2,18,64,128]{3,2,1,0:T(8,128)S(1)} %fusion.9.refs_1_, f32[2,16,64,128]{3,2,1,0:T(8,128)S(1)} %constant_dynamic-update-slice_fusion, ...), kind=kLoop, calls=%fused_computation.42 | loop fusion | flops 3407872 | bytes 6946816 | tf_op jit(solution)/shard_map/add | solution.py:100
  21.0 0.8 copy-done.1
  21.8 3.4 %collective-permute-start.2 = (f32[4,8,64,128]{3,2,1,0:T(8,128)S(1)}, f32[4,8,64,128]{3,2,1,0:T(8,128)S(1)}, u32[]{:S(2)}, u32[]{:S(2)}) collective-permute-start(f32[4,8,64,128]{3,2,1,0:T(8,128)S(1)} %get-tuple-element.6), channel_id=1, source_target_pairs={{0,1},{1,2},{2,3},{3,4},{4,5},{5,6},{6,7},{7,8},{8,9},{9,10},{10,1... | collective-permute-start | bytes 3145736 | tf_op jit(solution)/shard_map/ppermute | solution.py:28
  25.2 1.9 %collective-permute-start.3 = (f32[4,8,64,128]{3,2,1,0:T(8,128)S(1)}, f32[4,8,64,128]{3,2,1,0:T(8,128)S(1)}, u32[]{:S(2)}, u32[]{:S(2)}) collective-permute-start(f32[4,8,64,128]{3,2,1,0:T(8,128)S(1)} %get-tuple-element.5), channel_id=1, source_target_pairs={{1,0},{2,1},{3,2},{4,3},{5,4},{6,5},{7,6},{8,7},{9,8},{10,9},{11,1... | collective-permute-start | bytes 3145736 | tf_op jit(solution)/shard_map/ppermute | solution.py:29
  27.1 0.7 fusion.45.refs_4_
  27.8 9.1 %collective-permute-done.2.refs_0_ = f32[4,8,64,128]{3,2,1,0:T(8,128)S(1)} collective-permute-done((f32[4,8,64,128]{3,2,1,0:T(8,128)S(1)}, f32[4,8,64,128]{3,2,1,0:T(8,128)S(1)}, u32[]{:S(2)}, u32[]{:S(2)}) %collective-permute-start.2) | collective-permute-done | bytes 1048608 | tf_op jit(solution)/shard_map/ppermute | solution.py:28
  36.9 8.0 %collective-permute-done.3.refs_3_ = f32[4,8,64,128]{3,2,1,0:T(8,128)S(1)} collective-permute-done((f32[4,8,64,128]{3,2,1,0:T(8,128)S(1)}, f32[4,8,64,128]{3,2,1,0:T(8,128)S(1)}, u32[]{:S(2)}, u32[]{:S(2)}) %collective-permute-start.3) | collective-permute-done | bytes 1048608 | tf_op jit(solution)/shard_map/ppermute | solution.py:29
  44.9 1.0 %copy-done.6 = f32[4,8,64,128]{3,2,1,0:T(8,128)} copy-done((f32[4,8,64,128]{3,2,1,0:T(8,128)}, f32[4,8,64,128]{3,2,1,0:T(8,128)S(1)}, u32[]{:S(2)}) %copy-start.6) | copy-done | bytes 1048600
  45.9 5.6 %shard_map.118 = f32[9,4,16,32]{3,2,1,0:T(8,128)} custom-call(s32[9]{0:T(128)} %offsets_ref.1, f32[4,8,64,128]{3,2,1,0:T(8,128)} %copy-done.5, f32[2,18,64,128]{3,2,1,0:T(8,128)} %copy-done, f32[2,16,64,128]{3,2,1,0:T(8,128)} %copy-done.1, f32[4,8,64,128]{3,2,1,0:T(8,128)} %copy-done.6, f32[128,32]{1,0:T(8,128)} %fusion.45.refs_4_), custom_call_target="tpu_custom_call" | custom-call | tf_op jit(solution)/shard_map/pallas_call | solution.py:166
  51.5 1.1 %fusion.34 = (f32[1,9,4,16,32]{4,3,2,1,0:T(8,128)S(1)}, f32[1,9,4,16,32]{4,3,2,1,0:T(8,128)S(1)}) fusion(f32[9,4,16,32]{3,2,1,0:T(8,128)} %shard_map.118), kind=kLoop, calls=%fused_computation.79 | loop fusion | bytes 221184 | tf_op jit(solution)/shard_map/stack | solution.py:209
  52.6 1.1 %maximum_bitcast_fusion = f32[16,3,9,4,32]{4,0,3,2,1:T(8,128)S(1)} fusion(f32[1,9,4,16,32]{4,3,2,1,0:T(8,128)S(1)} %get-tuple-element.14, f32[1,9,4,16,32]{4,3,2,1,0:T(8,128)} %bitcast.218, f32[1,9,4,16,32]{4,3,2,1,0:T(8,128)S(1)} %get-tuple-element.13), kind=kLoop, calls=%fused_computation.46 | loop fusion | flops 110592 | bytes 442368 | tf_op jit(solution)/shard_map/transpose | solution.py:212
  53.7 0.3 copy.51
  54.1 0.6 all_to_all.8
  54.6 16.2 %all_to_all.10 = f32[16,1,3456]{2,1,0:T(1,128)S(1)} all-to-all(f32[16,1,3456]{2,1,0:T(1,128)S(1)} %all_to_all.8), channel_id=1, replica_groups=mesh['shot'=16,'gx'=16] {'shot'}, dimensions={0} | all-to-all | bytes 442368 | tf_op jit(solution)/shard_map/all_to_all | solution.py:214
  71.1 3.4 %collective-permute-start.4 = (f32[9,1,3,32]{3,1,0,2:T(1,128)S(1)}, f32[9,1,3,32]{3,1,0,2:T(1,128)S(1)}, u32[]{:S(2)}, u32[]{:S(2)}) collective-permute-start(f32[9,1,3,32]{3,1,0,2:T(1,128)S(1)} %get-tuple-element.15), channel_id=1, source_target_pairs={{0,1},{1,2},{2,3},{3,4},{4,5},{5,6},{6,7},{7,8},{8,9},{9,10},{10,1... | collective-permute-start | bytes 10376 | tf_op jit(solution)/shard_map/ppermute | solution.py:16
  74.5 1.9 %collective-permute-start.5 = (f32[9,1,3,32]{3,1,0,2:T(1,128)S(1)}, f32[9,1,3,32]{3,1,0,2:T(1,128)S(1)}, u32[]{:S(2)}, u32[]{:S(2)}) collective-permute-start(f32[9,1,3,32]{3,1,0,2:T(1,128)S(1)} %get-tuple-element.16), channel_id=1, source_target_pairs={{1,0},{2,1},{3,2},{4,3},{5,4},{6,5},{7,6},{8,7},{9,8},{10,9},{11,1... | collective-permute-start | bytes 10376 | tf_op jit(solution)/shard_map/ppermute | solution.py:19
  76.5 6.6 %collective-permute-done.5 = f32[9,1,3,32]{3,1,0,2:T(1,128)S(1)} collective-permute-done((f32[9,1,3,32]{3,1,0,2:T(1,128)S(1)}, f32[9,1,3,32]{3,1,0,2:T(1,128)S(1)}, u32[]{:S(2)}, u32[]{:S(2)}) %collective-permute-start.5) | collective-permute-done | bytes 3488 | tf_op jit(solution)/shard_map/ppermute | solution.py:19
  84.7 0.4 fusion.12
  85.1 0.7 copy.79
  (84 shorter events, 3.3 us)
Async XLA Ops:
  0.0 1.3 %copy-start.7 = (f32[1,16,64,128]{3,2,1,0:T(8,128)S(1)}, f32[1,16,64,128]{3,2,1,0:T(8,128)}, u32[]{:S(2)}) copy-start(f32[1,16,64,128]{3,2,1,0:T(8,128)} %param.15) | copy-start | bytes 1572868
  0.0 1.4 %copy-start.2 = (f32[16,64,128]{2,1,0:T(8,128)S(1)}, f32[16,64,128]{2,1,0:T(8,128)}, u32[]{:S(2)}) copy-start(f32[16,64,128]{2,1,0:T(8,128)} %param.16) | copy-start | bytes 1572868
  0.0 1.5 %copy-start.4 = (f32[1,16,64,128]{3,2,1,0:T(8,128)S(1)}, f32[1,16,64,128]{3,2,1,0:T(8,128)}, u32[]{:S(2)}) copy-start(f32[1,16,64,128]{3,2,1,0:T(8,128)} %param.12) | copy-start | bytes 1572868
  0.0 1.7 %copy-start.3 = (f32[1,16,64,128]{3,2,1,0:T(8,128)S(1)}, f32[1,16,64,128]{3,2,1,0:T(8,128)}, u32[]{:S(2)}) copy-start(f32[1,16,64,128]{3,2,1,0:T(8,128)} %param.14) | copy-start | bytes 1572868
  1.4 7.6 %copy-start.10 = (f32[1,2,512]{2,1,0:T(2,128)S(1)}, f32[1,2,512]{2,1,0:T(2,128)}, u32[]{:S(2)}) copy-start(f32[1,2,512]{2,1,0:T(2,128)} %param.20) | copy-start | bytes 12292
  1.4 9.0 %copy-start.9 = (s32[1,512]{1,0:T(1,128)S(1)}, s32[1,512]{1,0:T(1,128)}, u32[]{:S(2)}) copy-start(s32[1,512]{1,0:T(1,128)} %param.19) | copy-start | bytes 6148
  1.7 12.3 %collective-permute-start = (f32[7,64,128]{2,1,0:T(8,128)S(1)}, f32[7,64,128]{2,1,0:T(8,128)S(1)}, u32[]{:S(2)}, u32[]{:S(2)}) collective-permute-start(f32[7,64,128]{2,1,0:T(8,128)S(1)} %pad_maximum_fusion.6), channel_id=1, source_target_pairs={{0,1},{1,2},{2,3},{3,4},{4,5},{5,6},{6,7},{7,8},{8,9},{9,10},{10,1... | collective-permute-start | bytes 688136 | tf_op jit(solution)/shard_map/ppermute | solution.py:49
  7.0 11.0 %collective-permute-start.1 = (f32[7,64,128]{2,1,0:T(8,128)S(1)}, f32[7,64,128]{2,1,0:T(8,128)S(1)}, u32[]{:S(2)}, u32[]{:S(2)}) collective-permute-start(f32[7,64,128]{2,1,0:T(8,128)S(1)} %pad_maximum_fusion.7), channel_id=1, source_target_pairs={{1,0},{2,1},{3,2},{4,3},{5,4},{6,5},{7,6},{8,7},{9,8},{10,9},{11,1... | collective-permute-start | bytes 688136 | tf_op jit(solution)/shard_map/ppermute | solution.py:52
  11.5 0.7 copy-start.11
  19.7 1.1 %copy-start = (f32[2,18,64,128]{3,2,1,0:T(8,128)}, f32[2,18,64,128]{3,2,1,0:T(8,128)S(1)}, u32[]{:S(2)}) copy-start(f32[2,18,64,128]{3,2,1,0:T(8,128)S(1)} %fusion.9.refs_1_) | copy-start | bytes 3538948
  20.8 1.0 %copy-start.1 = (f32[2,16,64,128]{3,2,1,0:T(8,128)}, f32[2,16,64,128]{3,2,1,0:T(8,128)S(1)}, u32[]{:S(2)}) copy-start(f32[2,16,64,128]{3,2,1,0:T(8,128)S(1)} %fusion.21.refs_2_) | copy-start | bytes 3145732
  21.8 15.1 %collective-permute-start.2 = (f32[4,8,64,128]{3,2,1,0:T(8,128)S(1)}, f32[4,8,64,128]{3,2,1,0:T(8,128)S(1)}, u32[]{:S(2)}, u32[]{:S(2)}) collective-permute-start(f32[4,8,64,128]{3,2,1,0:T(8,128)S(1)} %get-tuple-element.6), channel_id=1, source_target_pairs={{0,1},{1,2},{2,3},{3,4},{4,5},{5,6},{6,7},{7,8},{8,9},{9,10},{10,1... | collective-permute-start | bytes 3145736 | tf_op jit(solution)/shard_map/ppermute | solution.py:28
  25.2 19.7 %collective-permute-start.3 = (f32[4,8,64,128]{3,2,1,0:T(8,128)S(1)}, f32[4,8,64,128]{3,2,1,0:T(8,128)S(1)}, u32[]{:S(2)}, u32[]{:S(2)}) collective-permute-start(f32[4,8,64,128]{3,2,1,0:T(8,128)S(1)} %get-tuple-element.5), channel_id=1, source_target_pairs={{1,0},{2,1},{3,2},{4,3},{5,4},{6,5},{7,6},{8,7},{9,8},{10,9},{11,1... | collective-permute-start | bytes 3145736 | tf_op jit(solution)/shard_map/ppermute | solution.py:29
  36.9 8.0 %copy-start.5 = (f32[4,8,64,128]{3,2,1,0:T(8,128)}, f32[4,8,64,128]{3,2,1,0:T(8,128)S(1)}, u32[]{:S(2)}) copy-start(f32[4,8,64,128]{3,2,1,0:T(8,128)S(1)} %collective-permute-done.2.refs_0_) | copy-start | bytes 3145732
  44.9 1.0 %copy-start.6 = (f32[4,8,64,128]{3,2,1,0:T(8,128)}, f32[4,8,64,128]{3,2,1,0:T(8,128)S(1)}, u32[]{:S(2)}) copy-start(f32[4,8,64,128]{3,2,1,0:T(8,128)S(1)} %collective-permute-done.3.refs_3_) | copy-start | bytes 3145732
  54.0 22.4 %copy-start.8 = (f32[64,9,3,3,3]{0,4,3,2,1:T(4,128)S(1)}, f32[64,9,3,3,3]{0,4,3,2,1:T(4,128)}, u32[]{:S(2)}) copy-start(f32[64,9,3,3,3]{0,4,3,2,1:T(4,128)} %param.22) | copy-start | bytes 186628
  71.1 5.4 %collective-permute-start.4 = (f32[9,1,3,32]{3,1,0,2:T(1,128)S(1)}, f32[9,1,3,32]{3,1,0,2:T(1,128)S(1)}, u32[]{:S(2)}, u32[]{:S(2)}) collective-permute-start(f32[9,1,3,32]{3,1,0,2:T(1,128)S(1)} %get-tuple-element.15), channel_id=1, source_target_pairs={{0,1},{1,2},{2,3},{3,4},{4,5},{5,6},{6,7},{7,8},{8,9},{9,10},{10,1... | collective-permute-start | bytes 10376 | tf_op jit(solution)/shard_map/ppermute | solution.py:16
  74.5 10.2 %copy-start.12 = (f32[64]{0:T(128)S(1)}, f32[64]{0:T(128)}, u32[]{:S(2)}) copy-start(f32[64]{0:T(128)} %param.23) | copy-start | bytes 772
  74.5 8.6 %collective-permute-start.5 = (f32[9,1,3,32]{3,1,0,2:T(1,128)S(1)}, f32[9,1,3,32]{3,1,0,2:T(1,128)S(1)}, u32[]{:S(2)}, u32[]{:S(2)}) collective-permute-start(f32[9,1,3,32]{3,1,0,2:T(1,128)S(1)} %get-tuple-element.16), channel_id=1, source_target_pairs={{1,0},{2,1},{3,2},{4,3},{5,4},{6,5},{7,6},{8,7},{9,8},{10,9},{11,1... | collective-permute-start | bytes 10376 | tf_op jit(solution)/shard_map/ppermute | solution.py:19

commit v11 on v9

--- a/solution.py
+++ b/solution.py
@@ -181,25 +181,18 @@
     )(offsets, *[piece[0] for piece in pieces], pool_z)
 
 
-def conv_apply(padded, conv_weight, conv_bias):
-    channels, span_x, span_y, span_z = padded.shape
-    size_x, size_y, size_z = (span_x - 2, span_y - 2, span_z - 2)
-    patches = jnp.stack(
-        [
-            padded[:, step_x : step_x + size_x, step_y : step_y + size_y, step_z : step_z + size_z]
-            for step_x in range(3)
-            for step_y in range(3)
-            for step_z in range(3)
-        ],
-        axis=1,
-    )
-    patches = patches.reshape(channels * 27, size_x * size_y * size_z)
-    matrix = conv_weight.reshape(conv_weight.shape[0], channels * 27)
-    result = jnp.dot(
-        matrix, patches, precision=lax.Precision.HIGHEST, preferred_element_type=jnp.float32
-    )
-    result = result + conv_bias[:, None]
-    return result.reshape(conv_weight.shape[0], size_x, size_y * size_z)
+def conv_apply(window, conv_weight, conv_bias):
+    result = lax.conv_general_dilated(
+        window[None],
+        conv_weight,
+        window_strides=(1, 1, 1),
+        padding=((0, 0), (0, 0), (1, 1)),
+        dimension_numbers=("NCDHW", "OIDHW", "NCDHW"),
+        precision=lax.Precision.HIGHEST,
+        preferred_element_type=jnp.float32,
+    )[0]
+    result = result + conv_bias[:, None, None, None]
+    return result.reshape(conv_weight.shape[0], result.shape[1], result.shape[2] * result.shape[3])
 
 
 def group_sum_windows(coarse, axis):
@@ -260,8 +253,7 @@
     ]
     coarse = offset_image(pieces, offsets, HMAX, cells_x + 8)
     summed = group_sum_windows(coarse, "shot")
-    window = jnp.pad(summed, ((0, 0), (0, 0), (0, 0), (1, 1)))
-    return conv_apply(window, conv_weight, conv_bias)
+    return conv_apply(summed, conv_weight, conv_bias)
 
 
 def solution(mesh):

time: 82.9 us -> 83.6 us (level)
  blocking collectives: 0 us -> 16.9 us
  starting transfers between devices: 21.3 us -> 11.5 us
  waiting for transfers between devices: 36.3 us -> 29.1 us
  other arithmetic: 6.14 us -> 4.9 us
  local copies, waits for them, and re-layouts: 9.04 us -> 10.1 us
    all_to_all x0 -> x1, blocking collectives: none -> 16.9 us  [group_sum_windows(): lax.all_to_all(windows.reshape(count, -1), axis, 0, 0, tiled=True)]
    all_to_all x1 -> x0, starting transfers between devices: 8.76 us -> none  [group_sum_windows(): lax.all_to_all(windows.reshape(count, -1), axis, 0, 0, tiled=True)]
    all_to_all x1 -> x0, waiting for transfers between devices: 8.57 us -> none  [group_sum_windows(): lax.all_to_all(windows.reshape(count, -1), axis, 0, 0, tiled=True)]
    unnamed x53 -> x31, local copies, waits for them, and re-layouts: 4.39 us -> 2.79 us
    ppermute x1, starting transfers between devices: 3.35 us -> 1.95 us  [halo_pieces(): low = lax.ppermute(block[:, block.shape[1] - width:], axis, forward)]
    ppermute x1, waiting for transfers between devices: 3.91 us -> 5.31 us  [input_halo(): lax.ppermute(pack(current[:, :2], previous[:, :1], courant[:1]), axis, ba...]
    conv_general_dilated x0 -> x4, local copies, waits for them, and re-layouts: none -> 1.31 us  [conv_apply(): lax.conv_general_dilated(window[None], conv_weight, window_strides=(1, 1,...]
    conv_general_dilated x0 -> x1, matrix products: none -> 1.15 us  [conv_apply(): lax.conv_general_dilated(window[None], conv_weight, window_strides=(1, 1,...]
  transfers between devices with their start and end apart: 5 -> 4, of which waited for: 4 -> 3; matrix products, arithmetic and copies ran while one was open for 6% -> 5% of each run, Pallas kernels for 0% -> 0%
where the time goes in v11:
time: 83.6 us; the launch traced here: 83.1 us
  waiting for transfers between devices  29.1 us (35%)
  blocking collectives  16.9 us (20%)
  starting transfers between devices  11.5 us (14%)
  local copies, waits for them, and re-layouts  10.1 us (12%)
  Pallas kernels  6.6 us (8%)
  other arithmetic  4.9 us (6%)
  matrix products  3.44 us (4%)
    all_to_all x1, blocking collectives, group_sum_windows(): lax.all_to_all(windows.reshape(count, -1), axis, 0, 0, tiled=True)  16.9 us
    ppermute x1, waiting for transfers between devices, halo_pieces(): low = lax.ppermute(block[:, block.shape[1] - width:], axis, forward)  14.2 us
    ppermute x1, waiting for transfers between devices, halo_pieces(): high = lax.ppermute(block[:, :width], axis, backward)  9.56 us
    pallas_call x1, Pallas kernels, offset_image(): pl.pallas_call(kernel, grid_spec=pltpu.PrefetchScalarGridSpec(num_scalar_...  6.6 us
    ppermute x1, waiting for transfers between devices, input_halo(): lax.ppermute(pack(current[:, :2], previous[:, :1], courant[:1]), axis, ba...  5.31 us
    ppermute x1, starting transfers between devices, input_halo(): lax.ppermute(pack(current[:, -2:], previous[:, -1:], courant[-1:]), axis,...  5.3 us
    unnamed x31, local copies, waits for them, and re-layouts  2.79 us
    add x2, other arithmetic, laplace_step(): return 2.0 * center - previous + courant * laplace + sources  2.43 us
  transfers between devices with their start and end apart: 4, of which 3 were waited for; matrix products, arithmetic and copies ran while one was open for 5% of the time, Pallas kernels for 0%

profile of v11, /device:TPU:39, one launch (start us, length us, event | category | flops | bytes accessed | tf_op | source)
XLA Modules:
  0.0 83.1 jit_solution(2862032411950092120)
XLA Ops:
  0.0 1.2 %constant_dynamic-update-slice_fusion.1 = f32[2,16,64,128]{3,2,1,0:T(8,128)S(1)} fusion(f32[1,16,64,128]{3,2,1,0:T(8,128)} %param.13), kind=kLoop, calls=%fused_computation.109 | loop fusion | bytes 1048576
  1.8 5.3 %collective-permute-start = (f32[7,64,128]{2,1,0:T(8,128)S(1)}, f32[7,64,128]{2,1,0:T(8,128)S(1)}, u32[]{:S(2)}, u32[]{:S(2)}) collective-permute-start(f32[7,64,128]{2,1,0:T(8,128)S(1)} %pad_maximum_fusion.6), channel_id=1, source_target_pairs={{0,1},{1,2},{2,3},{3,4},{4,5},{5,6},{6,7},{7,8},{8,9},{9,10},{10,1... | collective-permute-start | bytes 688136 | tf_op jit(solution)/shard_map/ppermute | solution.py:49
  7.1 1.9 %collective-permute-start.1 = (f32[7,64,128]{2,1,0:T(8,128)S(1)}, f32[7,64,128]{2,1,0:T(8,128)}, u32[]{:S(2)}, u32[]{:S(2)}) collective-permute-start(f32[7,64,128]{2,1,0:T(8,128)S(1)} %pad_maximum_fusion.7), channel_id=1, source_target_pairs={{1,0},{2,1},{3,2},{4,3},{5,4},{6,5},{7,6},{8,7},{9,8},{10,9},{11,1... | collective-permute-start | bytes 688136 | tf_op jit(solution)/shard_map/ppermute | solution.py:52
  9.2 0.3 reduce-precision_convert_fusion.1
  9.5 0.8 fusion.1
  10.3 0.6 copy-done.11
  11.0 0.4 fusion.22
  11.5 0.8 fusion
  12.3 0.4 fusion.21
  12.8 5.3 %collective-permute-done.1 = f32[7,64,128]{2,1,0:T(8,128)} collective-permute-done((f32[7,64,128]{2,1,0:T(8,128)S(1)}, f32[7,64,128]{2,1,0:T(8,128)}, u32[]{:S(2)}, u32[]{:S(2)}) %collective-permute-start.1) | collective-permute-done | bytes 229408 | tf_op jit(solution)/shard_map/ppermute | solution.py:52
  18.1 0.9 %slice.183 = f32[4,64,128]{2,1,0:T(8,128)S(1)} slice(f32[7,64,128]{2,1,0:T(8,128)} %collective-permute-done.1), slice={[0:4], [0:64], [0:128]} | slice | bytes 262144 | tf_op jit(solution)/shard_map/slice | solution.py:45
  19.2 0.8 slice.187
  20.0 0.8 %slice_bitcast_fusion.1 = f32[2,1,64,128]{3,2,1,0:T(8,128)S(1)} fusion(f32[7,64,128]{2,1,0:T(8,128)} %collective-permute-done.1), kind=kLoop, calls=%fused_computation.99 | loop fusion | bytes 131072 | tf_op jit(solution)/shard_map/reshape | solution.py:46
  20.9 1.5 %fusion.10.refs_1_ = f32[2,18,64,128]{3,2,1,0:T(8,128)S(1)} fusion(f32[2,18,64,128]{3,2,1,0:T(8,128)S(1)} %pad_maximum_fusion.2, f32[2,1,64,128]{3,2,1,0:T(8,128)S(1)} %slice_bitcast_fusion.1, f32[2,1,64,128]{3,2,1,0:T(8,128)S(1)} %slice_bitcast_fusion.2, f32[2,2,64,128]{3,2,1,0:T(8,128)S(1)} %bitcast.64, ...), kind=kLoop, calls=%fused_computation.28 | loop fusion | flops 5275648 | bytes 6619136 | tf_op jit(solution)/shard_map/add | solution.py:100
  22.5 0.9 %fusion.20.refs_2_ = f32[2,16,64,128]{3,2,1,0:T(8,128)S(1)} fusion(f32[2,16,64,128]{3,2,1,0:T(8,128)S(1)} %slice.194, f32[1,18,64,128]{3,2,1,0:T(8,128)S(1)} %bitcast.55, f32[1,18,64,128]{3,2,1,0:T(8,128)S(1)} %bitcast.56, f32[2,18,64,128]{3,2,1,0:T(8,128)S(1)} %fusion.10.refs_1_, f32[2,16,64,128]{3,2,1,0:T(8,128)S(1)} %constant_dynamic-update-slice_fusion, ...), kind=kLoop, calls=%fused_computation.43 | loop fusion | flops 3407872 | bytes 6946816 | tf_op jit(solution)/shard_map/add | solution.py:100
  23.4 0.4 pad_maximum_fusion
  23.8 0.6 copy-done.2
  24.4 2.0 %collective-permute-start.2 = (f32[4,12,64,128]{3,2,1,0:T(8,128)S(1)}, f32[4,12,64,128]{3,2,1,0:T(8,128)S(1)}, u32[]{:S(2)}, u32[]{:S(2)}) collective-permute-start(f32[4,12,64,128]{3,2,1,0:T(8,128)S(1)} %get-tuple-element.6), channel_id=1, source_target_pairs={{0,1},{1,2},{2,3},{3,4},{4,5},{5,6},{6,7},{7,8},{8,9},{9,10},{10,1... | collective-permute-start | bytes 4718600 | tf_op jit(solution)/shard_map/ppermute | solution.py:28
  26.4 2.4 %collective-permute-start.3 = (f32[4,12,64,128]{3,2,1,0:T(8,128)S(1)}, f32[4,12,64,128]{3,2,1,0:T(8,128)}, u32[]{:S(2)}, u32[]{:S(2)}) collective-permute-start(f32[4,12,64,128]{3,2,1,0:T(8,128)S(1)} %get-tuple-element.5), channel_id=1, source_target_pairs={{1,0},{2,1},{3,2},{4,3},{5,4},{6,5},{7,6},{8,7},{9,8},{10,9},{11,1... | collective-permute-start | bytes 4718600 | tf_op jit(solution)/shard_map/ppermute | solution.py:29
  28.8 0.7 fusion.51.refs_4_
  29.5 14.2 %collective-permute-done.2.refs_0_ = f32[4,12,64,128]{3,2,1,0:T(8,128)S(1)} collective-permute-done((f32[4,12,64,128]{3,2,1,0:T(8,128)S(1)}, f32[4,12,64,128]{3,2,1,0:T(8,128)S(1)}, u32[]{:S(2)}, u32[]{:S(2)}) %collective-permute-start.2) | collective-permute-done | bytes 1572896 | tf_op jit(solution)/shard_map/ppermute | solution.py:28
  43.7 9.6 %collective-permute-done.3.refs_3_ = f32[4,12,64,128]{3,2,1,0:T(8,128)} collective-permute-done((f32[4,12,64,128]{3,2,1,0:T(8,128)S(1)}, f32[4,12,64,128]{3,2,1,0:T(8,128)}, u32[]{:S(2)}, u32[]{:S(2)}) %collective-permute-start.3) | collective-permute-done | bytes 1572896 | tf_op jit(solution)/shard_map/ppermute | solution.py:29
  53.3 6.6 %shard_map.118 = f32[9,6,16,32]{3,2,1,0:T(8,128)} custom-call(s32[9]{0:T(128)} %offsets_ref.1, f32[4,12,64,128]{3,2,1,0:T(8,128)} %copy-done.7, f32[2,18,64,128]{3,2,1,0:T(8,128)} %copy-done.1, f32[2,16,64,128]{3,2,1,0:T(8,128)} %copy-done.2, f32[4,12,64,128]{3,2,1,0:T(8,128)} %collective-permute-done.3.refs_3_, f32[128,32]{1,0:T(8,128)} %fusion.51.refs_4_), custom_call_target="tpu_custom_call" | custom-call | tf_op jit(solution)/shard_map/pallas_call | solution.py:166
  59.9 1.3 %fusion.27 = (f32[1,9,6,16,32]{4,3,2,1,0:T(8,128)S(1)}, f32[1,9,6,16,32]{4,3,2,1,0:T(8,128)S(1)}) fusion(f32[9,6,16,32]{3,2,1,0:T(8,128)} %shard_map.118), kind=kLoop, calls=%fused_computation.65 | loop fusion | bytes 331776 | tf_op jit(solution)/shard_map/stack | solution.py:202
  61.4 0.4 copy.39
  61.8 0.8 all_to_all.8
  62.6 16.9 %all_to_all.10 = f32[16,1,5184]{2,1,0:T(1,128)S(1)} all-to-all(f32[16,1,5184]{2,1,0:T(1,128)S(1)} %all_to_all.8), channel_id=1, replica_groups=mesh['shot'=16,'gx'=16] {'shot'}, dimensions={0} | all-to-all | bytes 663552 | tf_op jit(solution)/shard_map/all_to_all | solution.py:207
  79.5 0.2 reduce_sum.9
  79.9 0.2 reshape.175
  80.1 1.0 %copy.43 = f32[9,6,3,1,8,5]{0,4,5,2,1,3:T(8,128)S(1)} copy(f32[9,6,3,1,8,5]{5,4,1,0,2,3:T(8,128)S(1)} %reshape.175) | data formatting | bytes 51840 | tf_op jit(solution)/shard_map/conv_general_dilated | solution.py:185
  81.2 1.2 %convolution_select_fusion = f32[4,1,8,5,64]{4,2,3,1,0:T(8,128)S(1)} fusion(f32[9,6,3,1,7,2]{0,4,5,2,1,3:T(8,128)S(1)} %slice.205, f32[9,6,3,1,8,5]{0,4,5,2,1,3:T(8,128)S(1)} %copy.43, f32[64,9,3,3,3]{0,4,3,2,1:T(4,128)S(1)} %copy-done, pred[8,5]{0,1:T(8,128)(4,1)S(1)} %copy-done.14), kind=kOutput, calls=%fused_computation.35 | convolution fusion | flops 29897296 | bytes 138200 | tf_op jit(solution)/shard_map/conv_general_dilated | solution.py:185
  82.4 0.6 copy.46
  (59 shorter events, 1.6 us)
Async XLA Ops:
  0.0 81.2 %copy-start = (f32[64,9,3,3,3]{0,4,3,2,1:T(4,128)S(1)}, f32[64,9,3,3,3]{0,4,3,2,1:T(4,128)}, u32[]{:S(2)}) copy-start(f32[64,9,3,3,3]{0,4,3,2,1:T(4,128)} %param.22) | copy-start | bytes 186628
  0.0 1.3 %copy-start.8 = (f32[1,16,64,128]{3,2,1,0:T(8,128)S(1)}, f32[1,16,64,128]{3,2,1,0:T(8,128)}, u32[]{:S(2)}) copy-start(f32[1,16,64,128]{3,2,1,0:T(8,128)} %param.15) | copy-start | bytes 1572868
  0.0 1.4 %copy-start.4 = (f32[16,64,128]{2,1,0:T(8,128)S(1)}, f32[16,64,128]{2,1,0:T(8,128)}, u32[]{:S(2)}) copy-start(f32[16,64,128]{2,1,0:T(8,128)} %param.16) | copy-start | bytes 1572868
  0.0 1.5 %copy-start.6 = (f32[1,16,64,128]{3,2,1,0:T(8,128)S(1)}, f32[1,16,64,128]{3,2,1,0:T(8,128)}, u32[]{:S(2)}) copy-start(f32[1,16,64,128]{3,2,1,0:T(8,128)} %param.12) | copy-start | bytes 1572868
  0.0 1.7 %copy-start.5 = (f32[1,16,64,128]{3,2,1,0:T(8,128)S(1)}, f32[1,16,64,128]{3,2,1,0:T(8,128)}, u32[]{:S(2)}) copy-start(f32[1,16,64,128]{3,2,1,0:T(8,128)} %param.14) | copy-start | bytes 1572868
  1.4 7.6 %copy-start.10 = (f32[1,2,512]{2,1,0:T(2,128)S(1)}, f32[1,2,512]{2,1,0:T(2,128)}, u32[]{:S(2)}) copy-start(f32[1,2,512]{2,1,0:T(2,128)} %param.20) | copy-start | bytes 12292
  1.4 7.6 %copy-start.13 = (s32[1,8]{1,0:T(1,128)S(1)}, s32[1,8]{1,0:T(1,128)}, u32[]{:S(2)}) copy-start(s32[1,8]{1,0:T(1,128)} %param.17) | copy-start | bytes 100
  1.4 7.7 %copy-start.9 = (s32[1,512]{1,0:T(1,128)S(1)}, s32[1,512]{1,0:T(1,128)}, u32[]{:S(2)}) copy-start(s32[1,512]{1,0:T(1,128)} %param.19) | copy-start | bytes 6148
  1.8 11.1 %collective-permute-start = (f32[7,64,128]{2,1,0:T(8,128)S(1)}, f32[7,64,128]{2,1,0:T(8,128)S(1)}, u32[]{:S(2)}, u32[]{:S(2)}) collective-permute-start(f32[7,64,128]{2,1,0:T(8,128)S(1)} %pad_maximum_fusion.6), channel_id=1, source_target_pairs={{0,1},{1,2},{2,3},{3,4},{4,5},{5,6},{6,7},{7,8},{8,9},{9,10},{10,1... | collective-permute-start | bytes 688136 | tf_op jit(solution)/shard_map/ppermute | solution.py:49
  7.1 11.1 %collective-permute-start.1 = (f32[7,64,128]{2,1,0:T(8,128)S(1)}, f32[7,64,128]{2,1,0:T(8,128)}, u32[]{:S(2)}, u32[]{:S(2)}) collective-permute-start(f32[7,64,128]{2,1,0:T(8,128)S(1)} %pad_maximum_fusion.7), channel_id=1, source_target_pairs={{1,0},{2,1},{3,2},{4,3},{5,4},{6,5},{7,6},{8,7},{9,8},{10,9},{11,1... | collective-permute-start | bytes 688136 | tf_op jit(solution)/shard_map/ppermute | solution.py:52
  10.2 0.7 copy-start.11
  22.4 1.0 %copy-start.1 = (f32[2,18,64,128]{3,2,1,0:T(8,128)}, f32[2,18,64,128]{3,2,1,0:T(8,128)S(1)}, u32[]{:S(2)}) copy-start(f32[2,18,64,128]{3,2,1,0:T(8,128)S(1)} %fusion.10.refs_1_) | copy-start | bytes 3538948
  23.4 1.0 %copy-start.2 = (f32[2,16,64,128]{3,2,1,0:T(8,128)}, f32[2,16,64,128]{3,2,1,0:T(8,128)S(1)}, u32[]{:S(2)}) copy-start(f32[2,16,64,128]{3,2,1,0:T(8,128)S(1)} %fusion.20.refs_2_) | copy-start | bytes 3145732
  24.4 19.3 %collective-permute-start.2 = (f32[4,12,64,128]{3,2,1,0:T(8,128)S(1)}, f32[4,12,64,128]{3,2,1,0:T(8,128)S(1)}, u32[]{:S(2)}, u32[]{:S(2)}) collective-permute-start(f32[4,12,64,128]{3,2,1,0:T(8,128)S(1)} %get-tuple-element.6), channel_id=1, source_target_pairs={{0,1},{1,2},{2,3},{3,4},{4,5},{5,6},{6,7},{7,8},{8,9},{9,10},{10,1... | collective-permute-start | bytes 4718600 | tf_op jit(solution)/shard_map/ppermute | solution.py:28
  26.4 26.9 %collective-permute-start.3 = (f32[4,12,64,128]{3,2,1,0:T(8,128)S(1)}, f32[4,12,64,128]{3,2,1,0:T(8,128)}, u32[]{:S(2)}, u32[]{:S(2)}) collective-permute-start(f32[4,12,64,128]{3,2,1,0:T(8,128)S(1)} %get-tuple-element.5), channel_id=1, source_target_pairs={{1,0},{2,1},{3,2},{4,3},{5,4},{6,5},{7,6},{8,7},{9,8},{10,9},{11,1... | collective-permute-start | bytes 4718600 | tf_op jit(solution)/shard_map/ppermute | solution.py:29
  43.7 9.6 %copy-start.7 = (f32[4,12,64,128]{3,2,1,0:T(8,128)}, f32[4,12,64,128]{3,2,1,0:T(8,128)S(1)}, u32[]{:S(2)}) copy-start(f32[4,12,64,128]{3,2,1,0:T(8,128)S(1)} %collective-permute-done.2.refs_0_) | copy-start | bytes 4718596
  59.9 1.3 %copy-start.3 = (f32[9,6,16,32]{3,2,1,0:T(8,128)S(1)}, f32[9,6,16,32]{3,2,1,0:T(8,128)}, u32[]{:S(2)}) copy-start(f32[9,6,16,32]{3,2,1,0:T(8,128)} %shard_map.118) | copy-start | bytes 331780
  79.8 1.4 %copy-start.14 = (pred[8,5]{0,1:T(8,128)(4,1)S(1)}, pred[8,5]{0,1:T(8,128)(4,1)}, u32[]{:S(2)}) copy-start(pred[8,5]{0,1:T(8,128)(4,1)} %constant.135) | copy-start | bytes 124
  80.1 2.3 %copy-start.12 = (f32[64]{0:T(128)S(1)}, f32[64]{0:T(128)}, u32[]{:S(2)}) copy-start(f32[64]{0:T(128)} %param.23) | copy-start | bytes 772

commit v12 on v9

--- a/solution.py
+++ b/solution.py
@@ -232,32 +232,51 @@
     cells_x, size_y, size_z = courant.shape
     slab_index = lax.axis_index("gx")
     first_x = slab_index * cells_x
-    previous = jnp.stack([source_prev[0], receiver_prev[0]])
-    current = jnp.stack([source_now[0], receiver_now[0]])
-    current_wide, previous_wide, courant_wide = input_halo(current, previous, courant, "gx")
-    source_fields = inject(cells_x + 2, first_x - 1, source_cells[0], wavelet[0], size_y, size_z)
-    receiver_fields = inject(cells_x + 2, first_x - 1, receiver_cells[0], receiver_data[0], size_y, size_z)
-    levels = []
-    for step_index in range(2):
-        sources = jnp.stack([source_fields[step_index], receiver_fields[step_index]])
-        if step_index == 0:
-            step_previous, step_extended, step_courant = previous_wide, current_wide, courant_wide
-        else:
-            sources = sources[:, 1:-1]
-            step_previous, step_extended, step_courant = current, levels[0], courant
-        advanced = laplace_step(step_previous, step_extended, step_courant, sources)
-        levels.append(advanced)
-    levels_full = list(levels)
-    levels[0] = levels[0][:, 1:-1]
-    fields = jnp.concatenate(levels, axis=0)
+    prev_list = [source_prev[0], receiver_prev[0]]
+    now_list = [source_now[0], receiver_now[0]]
+    count = lax.axis_size("gx")
+    forward = [(i, i + 1) for i in range(count - 1)]
+    backward = [(target, source) for source, target in forward]
+    low = lax.ppermute(
+        jnp.concatenate([now[-2:] for now in now_list] + [prev[-1:] for prev in prev_list] + [courant[-1:]]),
+        "gx",
+        forward,
+    )
+    high = lax.ppermute(
+        jnp.concatenate([now[:2] for now in now_list] + [prev[:1] for prev in prev_list] + [courant[:1]]),
+        "gx",
+        backward,
+    )
+    fields = len(now_list)
+    courant_wide = jnp.concatenate([low[3 * fields :], courant, high[3 * fields :]])
+    injected = [
+        inject(cells_x + 2, first_x - 1, source_cells[0], wavelet[0], size_y, size_z),
+        inject(cells_x + 2, first_x - 1, receiver_cells[0], receiver_data[0], size_y, size_z),
+    ]
+    first_levels = []
+    second_levels = []
+    for field in range(fields):
+        now_wide = jnp.concatenate(
+            [low[2 * field : 2 * field + 2], now_list[field], high[2 * field : 2 * field + 2]]
+        )
+        prev_wide = jnp.concatenate(
+            [
+                low[2 * fields + field : 2 * fields + field + 1],
+                prev_list[field],
+                high[2 * fields + field : 2 * fields + field + 1],
+            ]
+        )
+        first = laplace_step(prev_wide[None], now_wide[None], courant_wide, injected[field][0][None])
+        second = laplace_step(now_list[field][None], first, courant, injected[field][1][None, 1:-1])
+        first_levels.append(first)
+        second_levels.append(second)
     width = HMAX + 4
-    low, high = halo_pieces(fields, "gx", width)
-    pieces = [
-        (low, 0, 0, 0, width),
-        (levels_full[0], 0, width, 1, cells_x),
-        (levels_full[1], 2, width, 0, cells_x),
-        (high, 0, width + cells_x, 0, width),
-    ]
+    slab = jnp.concatenate([level[:, 1:-1] for level in first_levels] + second_levels)
+    low_halo, high_halo = halo_pieces(slab, "gx", width)
+    pieces = [(low_halo, 0, 0, 0, width)]
+    pieces += [(level, field, width, 1, cells_x) for field, level in enumerate(first_levels)]
+    pieces += [(level, fields + field, width, 0, cells_x) for field, level in enumerate(second_levels)]
+    pieces += [(high_halo, 0, width + cells_x, 0, width)]
     coarse = offset_image(pieces, offsets, HMAX, cells_x + 8)
     summed = group_sum_windows(coarse, "shot")
     window = jnp.pad(summed, ((0, 0), (0, 0), (0, 0), (1, 1)))

time: 82.9 us -> 93.5 us (1.13)
  local copies, waits for them, and re-layouts: 9.04 us -> 16.5 us
  starting transfers between devices: 21.3 us -> 25.1 us
  waiting for transfers between devices: 36.3 us -> 33.3 us
  other arithmetic: 6.14 us -> 7.95 us
    unnamed x53 -> x58, local copies, waits for them, and re-layouts: 4.39 us -> 9.6 us
    ppermute x1, starting transfers between devices: 3.35 us -> 6.74 us  [halo_pieces(): low = lax.ppermute(block[:, block.shape[1] - width:], axis, forward)]
    ppermute x2, waiting for transfers between devices: 3.91 us -> 1.53 us  [the longest x1 1.53 us: local(): lax.ppermute(jnp.concatenate([now[:2] for now in now_list] + [prev[:1] fo...]
    transpose x1, other arithmetic: 0.12 us -> 1.13 us  [group_sum_windows(): windows = jnp.moveaxis(windows, 3, 0)]
    add x2 -> x3, other arithmetic: 2.37 us -> 2.1 us  [laplace_step(): return 2.0 * center - previous + courant * laplace + sources]
  transfers between devices with their start and end apart: 5 -> 5, of which waited for: 4 -> 4; matrix products, arithmetic and copies ran while one was open for 6% -> 8% of each run, Pallas kernels for 0% -> 0%
where the time goes in v12:
time: 93.5 us; the launch traced here: 92.6 us
  waiting for transfers between devices  33.3 us (36%)
  starting transfers between devices  25.1 us (27%)
  local copies, waits for them, and re-layouts  16.5 us (18%)
  other arithmetic  7.95 us (9%)
  Pallas kernels  6.54 us (7%)
  matrix products  2.66 us (3%)
    ppermute x1, waiting for transfers between devices, halo_pieces(): low = lax.ppermute(block[:, block.shape[1] - width:], axis, forward)  14.7 us
    unnamed x58, local copies, waits for them, and re-layouts  9.6 us
    all_to_all x1, starting transfers between devices, group_sum_windows(): lax.all_to_all(windows.reshape(count, -1), axis, 0, 0, tiled=True)  9.26 us
    all_to_all x1, waiting for transfers between devices, group_sum_windows(): lax.all_to_all(windows.reshape(count, -1), axis, 0, 0, tiled=True)  8.57 us
    ppermute x1, waiting for transfers between devices, halo_pieces(): high = lax.ppermute(block[:, :width], axis, backward)  8.56 us
    ppermute x1, starting transfers between devices, halo_pieces(): low = lax.ppermute(block[:, block.shape[1] - width:], axis, forward)  6.74 us
    pallas_call x1, Pallas kernels, offset_image(): pl.pallas_call(kernel, grid_spec=pltpu.PrefetchScalarGridSpec(num_scalar_...  6.54 us
    ppermute x1, starting transfers between devices, local(): lax.ppermute(jnp.concatenate([now[-2:] for now in now_list] + [prev[-1:]...  5.29 us
  transfers between devices with their start and end apart: 5, of which 4 were waited for; matrix products, arithmetic and copies ran while one was open for 8% of the time, Pallas kernels for 0%

profile of v12, /device:TPU:39, one launch (start us, length us, event | category | flops | bytes accessed | tf_op | source)
XLA Modules:
  0.0 92.6 jit_solution(13216679239684363005)
XLA Ops:
  0.0 0.9 constant_dynamic-update-slice_fusion.4
  0.9 0.9 constant_dynamic-update-slice_fusion.3
  1.8 0.8 constant_dynamic-update-slice_fusion.2
  2.6 0.8 constant_dynamic-update-slice_fusion.1
  3.3 0.8 constant_dynamic-update-slice_fusion
  4.1 5.3 %collective-permute-start = (f32[7,64,128]{2,1,0:T(8,128)S(1)}, f32[7,64,128]{2,1,0:T(8,128)S(1)}, u32[]{:S(2)}, u32[]{:S(2)}) collective-permute-start(f32[7,64,128]{2,1,0:T(8,128)S(1)} %get-tuple-element.15), channel_id=1, source_target_pairs={{0,1},{1,2},{2,3},{3,4},{4,5},{5,6},{6,7},{7,8},{8,9},{9,10},{10,1... | collective-permute-start | bytes 688136 | tf_op jit(solution)/shard_map/ppermute | solution.py:240
  9.4 1.9 %collective-permute-start.1 = (f32[7,64,128]{2,1,0:T(8,128)S(1)}, f32[7,64,128]{2,1,0:T(8,128)S(1)}, u32[]{:S(2)}, u32[]{:S(2)}) collective-permute-start(f32[7,64,128]{2,1,0:T(8,128)S(1)} %get-tuple-element.16), channel_id=1, source_target_pairs={{1,0},{2,1},{3,2},{4,3},{5,4},{6,5},{7,6},{8,7},{9,8},{10,9},{11,1... | collective-permute-start | bytes 688136 | tf_op jit(solution)/shard_map/ppermute | solution.py:245
  11.3 0.8 fusion.86
  12.1 0.7 and_select_fusion.4
  12.8 0.7 add_bitcast_fusion
  13.5 0.7 fusion.72
  14.2 0.7 add_select_fusion
  15.2 0.8 fusion.1
  17.2 0.8 fusion
  18.8 1.5 %collective-permute-done.1 = f32[7,64,128]{2,1,0:T(8,128)S(1)} collective-permute-done((f32[7,64,128]{2,1,0:T(8,128)S(1)}, f32[7,64,128]{2,1,0:T(8,128)S(1)}, u32[]{:S(2)}, u32[]{:S(2)}) %collective-permute-start.1) | collective-permute-done | bytes 229408 | tf_op jit(solution)/shard_map/ppermute | solution.py:245
  20.6 0.8 copy-done.2
  21.6 0.6 fusion.20.refs_2_
  22.3 1.1 %copy-done.10 = f32[1,16,64,128]{3,2,1,0:T(8,128)S(1)} copy-done((f32[1,16,64,128]{3,2,1,0:T(8,128)S(1)}, f32[1,16,64,128]{3,2,1,0:T(8,128)}, u32[]{:S(2)}) %copy-start.10) | copy-done | bytes 524312
  24.1 0.9 fusion.32
  26.5 6.7 %collective-permute-start.2 = (f32[4,12,64,128]{3,2,1,0:T(8,128)S(1)}, f32[4,12,64,128]{3,2,1,0:T(8,128)S(1)}, u32[]{:S(2)}, u32[]{:S(2)}) collective-permute-start(f32[4,12,64,128]{3,2,1,0:T(8,128)S(1)} %get-tuple-element.6), channel_id=1, source_target_pairs={{0,1},{1,2},{2,3},{3,4},{4,5},{5,6},{6,7},{7,8},{8,9},{9,10},{10,1... | collective-permute-start | bytes 4718600 | tf_op jit(solution)/shard_map/ppermute | solution.py:28
  33.3 1.9 %collective-permute-start.3 = (f32[4,12,64,128]{3,2,1,0:T(8,128)S(1)}, f32[4,12,64,128]{3,2,1,0:T(8,128)S(1)}, u32[]{:S(2)}, u32[]{:S(2)}) collective-permute-start(f32[4,12,64,128]{3,2,1,0:T(8,128)S(1)} %get-tuple-element.5), channel_id=1, source_target_pairs={{1,0},{2,1},{3,2},{4,3},{5,4},{6,5},{7,6},{8,7},{9,8},{10,9},{11,1... | collective-permute-start | bytes 4718600 | tf_op jit(solution)/shard_map/ppermute | solution.py:29
  35.2 0.7 fusion.57.refs_6_
  35.9 14.7 %collective-permute-done.2.refs_0_ = f32[4,12,64,128]{3,2,1,0:T(8,128)S(1)} collective-permute-done((f32[4,12,64,128]{3,2,1,0:T(8,128)S(1)}, f32[4,12,64,128]{3,2,1,0:T(8,128)S(1)}, u32[]{:S(2)}, u32[]{:S(2)}) %collective-permute-start.2) | collective-permute-done | bytes 1572896 | tf_op jit(solution)/shard_map/ppermute | solution.py:28
  50.6 8.6 %collective-permute-done.3.refs_5_ = f32[4,12,64,128]{3,2,1,0:T(8,128)S(1)} collective-permute-done((f32[4,12,64,128]{3,2,1,0:T(8,128)S(1)}, f32[4,12,64,128]{3,2,1,0:T(8,128)S(1)}, u32[]{:S(2)}, u32[]{:S(2)}) %collective-permute-start.3) | collective-permute-done | bytes 1572896 | tf_op jit(solution)/shard_map/ppermute | solution.py:29
  59.2 1.1 %copy-done.8 = f32[4,12,64,128]{3,2,1,0:T(8,128)} copy-done((f32[4,12,64,128]{3,2,1,0:T(8,128)}, f32[4,12,64,128]{3,2,1,0:T(8,128)S(1)}, u32[]{:S(2)}) %copy-start.8) | copy-done | bytes 1572888
  60.3 6.5 %shard_map.118 = f32[9,6,16,32]{3,2,1,0:T(8,128)} custom-call(s32[9]{0:T(128)} %offsets_ref.1, f32[4,12,64,128]{3,2,1,0:T(8,128)} %copy-done.7, f32[1,18,64,128]{3,2,1,0:T(8,128)} %copy-done.1, f32[1,18,64,128]{3,2,1,0:T(8,128)} %copy-done, f32[1,16,64,128]{3,2,1,0:T(8,128)} %copy-done.3, f32[1,16,64,128]{3,2,1,0:T(8,128)} %copy-done.4, ...), custom_call_target="tpu_custom_call" | custom-call | tf_op jit(solution)/shard_map/pallas_call | solution.py:166
  66.8 1.3 %fusion.41 = (f32[1,9,6,16,32]{4,3,2,1,0:T(8,128)S(1)}, f32[1,9,6,16,32]{4,3,2,1,0:T(8,128)S(1)}) fusion(f32[9,6,16,32]{3,2,1,0:T(8,128)} %shard_map.118), kind=kLoop, calls=%fused_computation.81 | loop fusion | bytes 331776 | tf_op jit(solution)/shard_map/stack | solution.py:209
  68.1 1.1 %maximum_bitcast_fusion = f32[16,3,9,6,32]{4,0,3,2,1:T(8,128)S(1)} fusion(f32[1,9,6,16,32]{4,3,2,1,0:T(8,128)S(1)} %get-tuple-element.26, f32[1,9,6,16,32]{4,3,2,1,0:T(8,128)} %bitcast.229, f32[1,9,6,16,32]{4,3,2,1,0:T(8,128)S(1)} %get-tuple-element.25), kind=kLoop, calls=%fused_computation.20 | loop fusion | flops 165888 | bytes 663552 | tf_op jit(solution)/shard_map/transpose | solution.py:212
  69.7 1.5 %all_to_all.8 = f32[16,1,5184]{2,1,0:T(1,128)} reshape(f32[16,3,9,6,32]{4,3,2,1,0:T(8,128)S(1)} %copy.42) | data formatting | bytes 663552 | tf_op jit(solution)/shard_map/all_to_all | solution.py:214
  71.2 9.3 %all-to-all-start = ((f32[16,1,5184]{2,1,0:T(1,128)}), f32[16,1,5184]{2,1,0:T(1,128)S(1)}, u32[]{:S(2)}, u32[]{:S(2)}) async-start(f32[16,1,5184]{2,1,0:T(1,128)} %all_to_all.8), calls=%async_computation | async-start | bytes 671744 | tf_op jit(solution)/shard_map/all_to_all | solution.py:214
  80.6 8.6 %all-to-all-done = f32[16,1,5184]{2,1,0:T(1,128)S(1)} async-done(((f32[16,1,5184]{2,1,0:T(1,128)}), f32[16,1,5184]{2,1,0:T(1,128)S(1)}, u32[]{:S(2)}, u32[]{:S(2)}) %all-to-all-start) | async-done | bytes 331808 | tf_op jit(solution)/shard_map/all_to_all | solution.py:214
  91.9 0.7 copy.70
  (83 shorter events, 7.9 us)
Async XLA Ops:
  4.1 14.7 %collective-permute-start = (f32[7,64,128]{2,1,0:T(8,128)S(1)}, f32[7,64,128]{2,1,0:T(8,128)S(1)}, u32[]{:S(2)}, u32[]{:S(2)}) collective-permute-start(f32[7,64,128]{2,1,0:T(8,128)S(1)} %get-tuple-element.15), channel_id=1, source_target_pairs={{0,1},{1,2},{2,3},{3,4},{4,5},{5,6},{6,7},{7,8},{8,9},{9,10},{10,1... | collective-permute-start | bytes 688136 | tf_op jit(solution)/shard_map/ppermute | solution.py:240
  9.4 11.0 %collective-permute-start.1 = (f32[7,64,128]{2,1,0:T(8,128)S(1)}, f32[7,64,128]{2,1,0:T(8,128)S(1)}, u32[]{:S(2)}, u32[]{:S(2)}) collective-permute-start(f32[7,64,128]{2,1,0:T(8,128)S(1)} %get-tuple-element.16), channel_id=1, source_target_pairs={{1,0},{2,1},{3,2},{4,3},{5,4},{6,5},{7,6},{8,7},{9,8},{10,9},{11,1... | collective-permute-start | bytes 688136 | tf_op jit(solution)/shard_map/ppermute | solution.py:245
  16.0 0.7 copy-start.12
  18.7 1.7 %copy-start.5 = (f32[1,16,64,128]{3,2,1,0:T(8,128)S(1)}, f32[1,16,64,128]{3,2,1,0:T(8,128)}, u32[]{:S(2)}) copy-start(f32[1,16,64,128]{3,2,1,0:T(8,128)} %param.13) | copy-start | bytes 1572868
  18.7 1.7 %copy-start.6 = (f32[1,16,64,128]{3,2,1,0:T(8,128)S(1)}, f32[1,16,64,128]{3,2,1,0:T(8,128)}, u32[]{:S(2)}) copy-start(f32[1,16,64,128]{3,2,1,0:T(8,128)} %param.15) | copy-start | bytes 1572868
  20.4 1.0 %copy-start.2 = (f32[16,64,128]{2,1,0:T(8,128)S(1)}, f32[16,64,128]{2,1,0:T(8,128)}, u32[]{:S(2)}) copy-start(f32[16,64,128]{2,1,0:T(8,128)} %param.16) | copy-start | bytes 1572868
  20.4 1.2 %copy-start.9 = (f32[1,16,64,128]{3,2,1,0:T(8,128)S(1)}, f32[1,16,64,128]{3,2,1,0:T(8,128)}, u32[]{:S(2)}) copy-start(f32[1,16,64,128]{3,2,1,0:T(8,128)} %param.14) | copy-start | bytes 1572868
  22.2 1.9 %copy-start = (f32[1,18,64,128]{3,2,1,0:T(8,128)}, f32[1,18,64,128]{3,2,1,0:T(8,128)S(1)}, u32[]{:S(2)}) copy-start(f32[1,18,64,128]{3,2,1,0:T(8,128)S(1)} %fusion.20.refs_2_) | copy-start | bytes 1769476
  22.2 1.3 %copy-start.10 = (f32[1,16,64,128]{3,2,1,0:T(8,128)S(1)}, f32[1,16,64,128]{3,2,1,0:T(8,128)}, u32[]{:S(2)}) copy-start(f32[1,16,64,128]{3,2,1,0:T(8,128)} %param.12) | copy-start | bytes 1572868
  24.1 1.0 %copy-start.1 = (f32[1,18,64,128]{3,2,1,0:T(8,128)}, f32[1,18,64,128]{3,2,1,0:T(8,128)S(1)}, u32[]{:S(2)}) copy-start(f32[1,18,64,128]{3,2,1,0:T(8,128)S(1)} %fusion.12.refs_1_) | copy-start | bytes 1769476
  25.1 0.8 copy-start.3
  25.1 1.0 %copy-start.4 = (f32[1,16,64,128]{3,2,1,0:T(8,128)}, f32[1,16,64,128]{3,2,1,0:T(8,128)S(1)}, u32[]{:S(2)}) copy-start(f32[1,16,64,128]{3,2,1,0:T(8,128)S(1)} %get-tuple-element.14.refs_4_) | copy-start | bytes 1572868
  26.5 24.1 %collective-permute-start.2 = (f32[4,12,64,128]{3,2,1,0:T(8,128)S(1)}, f32[4,12,64,128]{3,2,1,0:T(8,128)S(1)}, u32[]{:S(2)}, u32[]{:S(2)}) collective-permute-start(f32[4,12,64,128]{3,2,1,0:T(8,128)S(1)} %get-tuple-element.6), channel_id=1, source_target_pairs={{0,1},{1,2},{2,3},{3,4},{4,5},{5,6},{6,7},{7,8},{8,9},{9,10},{10,1... | collective-permute-start | bytes 4718600 | tf_op jit(solution)/shard_map/ppermute | solution.py:28
  33.3 25.9 %collective-permute-start.3 = (f32[4,12,64,128]{3,2,1,0:T(8,128)S(1)}, f32[4,12,64,128]{3,2,1,0:T(8,128)S(1)}, u32[]{:S(2)}, u32[]{:S(2)}) collective-permute-start(f32[4,12,64,128]{3,2,1,0:T(8,128)S(1)} %get-tuple-element.5), channel_id=1, source_target_pairs={{1,0},{2,1},{3,2},{4,3},{5,4},{6,5},{7,6},{8,7},{9,8},{10,9},{11,1... | collective-permute-start | bytes 4718600 | tf_op jit(solution)/shard_map/ppermute | solution.py:29
  50.6 8.6 %copy-start.7 = (f32[4,12,64,128]{3,2,1,0:T(8,128)}, f32[4,12,64,128]{3,2,1,0:T(8,128)S(1)}, u32[]{:S(2)}) copy-start(f32[4,12,64,128]{3,2,1,0:T(8,128)S(1)} %collective-permute-done.2.refs_0_) | copy-start | bytes 4718596
  59.2 1.1 %copy-start.8 = (f32[4,12,64,128]{3,2,1,0:T(8,128)}, f32[4,12,64,128]{3,2,1,0:T(8,128)S(1)}, u32[]{:S(2)}) copy-start(f32[4,12,64,128]{3,2,1,0:T(8,128)S(1)} %collective-permute-done.3.refs_5_) | copy-start | bytes 4718596
  69.7 10.8 %copy-start.11 = (f32[64,9,3,3,3]{0,4,3,2,1:T(4,128)S(1)}, f32[64,9,3,3,3]{0,4,3,2,1:T(4,128)}, u32[]{:S(2)}) copy-start(f32[64,9,3,3,3]{0,4,3,2,1:T(4,128)} %param.22) | copy-start | bytes 186628
  71.2 17.9 %all-to-all-start = ((f32[16,1,5184]{2,1,0:T(1,128)}), f32[16,1,5184]{2,1,0:T(1,128)S(1)}, u32[]{:S(2)}, u32[]{:S(2)}) async-start(f32[16,1,5184]{2,1,0:T(1,128)} %all_to_all.8), calls=%async_computation | async-start | bytes 671744 | tf_op jit(solution)/shard_map/all_to_all | solution.py:214
  89.4 2.1 %copy-start.13 = (f32[64]{0:T(128)S(1)}, f32[64]{0:T(128)}, u32[]{:S(2)}) copy-start(f32[64]{0:T(128)} %param.23) | copy-start | bytes 772

commit v13 on v9

--- a/solution.py
+++ b/solution.py
@@ -136,32 +136,41 @@
             copies.append(pltpu.make_async_copy(source, target, semaphores.at[k]))
         for copy in copies:
             copy.start()
-        for copy in copies:
+        high_at = max(at for _, _, at, _, _ in pieces)
+        early = [block for block in range(blocks_x) if 4 * block + 3 + 2 * margin <= high_at - 1]
+        late = [block for block in range(blocks_x) if block not in early]
+        waited = [copy for copy, piece in zip(copies, pieces) if piece[2] < high_at]
+        for copy in waited:
             copy.wait()
 
-        def per_offset(index, carry):
-            offset_value = offsets_ref[index]
-            forward = margin + offset_value
-            backward = margin - offset_value
-            for block in range(blocks_x):
-                total = None
-                for step in range(4):
-                    x = block * 4 + step
-                    term = (
-                        wide_ref[0, forward + x] * wide_ref[1, backward + x]
-                        + wide_ref[2, forward + x] * wide_ref[3, backward + x]
-                    )
-                    total = term if total is None else total + term
-                sum_ref[block * size_y : (block + 1) * size_y, :] = total
+        def products(block_list):
+            for index in range(count):
+                offset_value = offsets_ref[index]
+                forward = margin + offset_value
+                backward = margin - offset_value
+                for block in block_list:
+                    total = None
+                    for step in range(4):
+                        x = block * 4 + step
+                        term = (
+                            wide_ref[0, forward + x] * wide_ref[1, backward + x]
+                            + wide_ref[2, forward + x] * wide_ref[3, backward + x]
+                        )
+                        total = term if total is None else total + term
+                    sum_ref[index, block * size_y : (block + 1) * size_y, :] = total
+
+        products(early)
+        for copy, piece in zip(copies, pieces):
+            if piece[2] >= high_at:
+                copy.wait()
+        products(late)
+        for index in range(count):
             pooled_y = None
             for step in range(4):
-                rows = sum_ref[pl.ds(step, blocks_x * blocks_y, stride=4), :]
+                rows = sum_ref.at[index][pl.ds(step, blocks_x * blocks_y, stride=4), :]
                 pooled_y = rows if pooled_y is None else pooled_y + rows
             pooled = split_dot(pooled_y, pool_z_ref[...], True)
             out_ref[index] = (pooled * (1.0 / 64.0)).reshape(blocks_x, blocks_y, blocks_z)
-            return carry
-
-        lax.fori_loop(0, count, per_offset, 0, unroll=True)
 
     return pl.pallas_call(
         kernel,
@@ -173,7 +182,7 @@
             out_specs=pl.BlockSpec((count, blocks_x, blocks_y, blocks_z), lambda i, offsets_ref: (0, 0, 0, 0)),
             scratch_shapes=[
                 pltpu.VMEM((fields, span_x, size_y, size_z), jnp.float32),
-                pltpu.VMEM((blocks_x * size_y, size_z), jnp.float32),
+                pltpu.VMEM((count, blocks_x * size_y, size_z), jnp.float32),
                 pltpu.SemaphoreType.DMA((len(pieces),)),
             ],
         ),

time: 82.9 us -> 82.3 us (level)
  no operation moved by 1% of the time
where the time goes in v13:
time: 82.3 us; the launch traced here: 81.9 us
  waiting for transfers between devices  36.7 us (45%)
  starting transfers between devices  20.9 us (25%)
  local copies, waits for them, and re-layouts  9.04 us (11%)
  other arithmetic  6.14 us (7%)
  Pallas kernels  5.96 us (7%)
  matrix products  2.66 us (3%)
    ppermute x1, waiting for transfers between devices, halo_pieces(): low = lax.ppermute(block[:, block.shape[1] - width:], axis, forward)  14.7 us
    ppermute x1, waiting for transfers between devices, halo_pieces(): high = lax.ppermute(block[:, :width], axis, backward)  9.56 us
    all_to_all x1, waiting for transfers between devices, group_sum_windows(): lax.all_to_all(windows.reshape(count, -1), axis, 0, 0, tiled=True)  8.57 us
    all_to_all x1, starting transfers between devices, group_sum_windows(): lax.all_to_all(windows.reshape(count, -1), axis, 0, 0, tiled=True)  8.36 us
    pallas_call x1, Pallas kernels, offset_image(): pl.pallas_call(kernel, grid_spec=pltpu.PrefetchScalarGridSpec(num_scalar_...  5.96 us
    ppermute x1, starting transfers between devices, input_halo(): lax.ppermute(pack(current[:, -2:], previous[:, -1:], courant[-1:]), axis,...  5.3 us
    unnamed x53, local copies, waits for them, and re-layouts  4.39 us
    ppermute x1, waiting for transfers between devices, input_halo(): lax.ppermute(pack(current[:, :2], previous[:, :1], courant[:1]), axis, ba...  3.91 us
  transfers between devices with their start and end apart: 5, of which 4 were waited for; matrix products, arithmetic and copies ran while one was open for 6% of the time, Pallas kernels for 0%

profile of v13, /device:TPU:39, one launch (start us, length us, event | category | flops | bytes accessed | tf_op | source)
XLA Modules:
  0.0 81.9 jit_solution(6419991225509647768)
XLA Ops:
  0.0 1.2 %constant_dynamic-update-slice_fusion.1 = f32[2,16,64,128]{3,2,1,0:T(8,128)S(1)} fusion(f32[1,16,64,128]{3,2,1,0:T(8,128)} %param.13), kind=kLoop, calls=%fused_computation.97 | loop fusion | bytes 1048576
  1.5 0.2 copy-done.4
  1.7 5.3 %collective-permute-start = (f32[7,64,128]{2,1,0:T(8,128)S(1)}, f32[7,64,128]{2,1,0:T(8,128)S(1)}, u32[]{:S(2)}, u32[]{:S(2)}) collective-permute-start(f32[7,64,128]{2,1,0:T(8,128)S(1)} %pad_maximum_fusion.6), channel_id=1, source_target_pairs={{0,1},{1,2},{2,3},{3,4},{4,5},{5,6},{6,7},{7,8},{8,9},{9,10},{10,1... | collective-permute-start | bytes 688136 | tf_op jit(solution)/shard_map/ppermute | solution.py:49
  7.0 1.9 %collective-permute-start.1 = (f32[7,64,128]{2,1,0:T(8,128)S(1)}, f32[7,64,128]{2,1,0:T(8,128)S(1)}, u32[]{:S(2)}, u32[]{:S(2)}) collective-permute-start(f32[7,64,128]{2,1,0:T(8,128)S(1)} %pad_maximum_fusion.7), channel_id=1, source_target_pairs={{1,0},{2,1},{3,2},{4,3},{5,4},{6,5},{7,6},{8,7},{9,8},{10,9},{11,1... | collective-permute-start | bytes 688136 | tf_op jit(solution)/shard_map/ppermute | solution.py:52
  9.0 0.7 and_select_fusion.4
  9.7 0.7 add_bitcast_fusion
  10.4 0.3 reduce-precision_convert_fusion.1
  10.7 0.8 fusion.1
  11.6 0.6 copy-done.11
  12.3 0.4 fusion.23
  12.7 0.8 fusion
  13.6 0.4 fusion.22
  14.1 3.9 %collective-permute-done.1 = f32[7,64,128]{2,1,0:T(8,128)S(1)} collective-permute-done((f32[7,64,128]{2,1,0:T(8,128)S(1)}, f32[7,64,128]{2,1,0:T(8,128)S(1)}, u32[]{:S(2)}, u32[]{:S(2)}) %collective-permute-start.1) | collective-permute-done | bytes 229408 | tf_op jit(solution)/shard_map/ppermute | solution.py:52
  18.2 1.5 %fusion.10.refs_1_ = f32[2,18,64,128]{3,2,1,0:T(8,128)S(1)} fusion(f32[2,18,64,128]{3,2,1,0:T(8,128)S(1)} %pad_maximum_fusion.2, f32[2,1,64,128]{3,2,1,0:T(8,128)S(1)} %slice_bitcast_fusion, f32[2,1,64,128]{3,2,1,0:T(8,128)S(1)} %slice_bitcast_fusion.1, f32[2,2,64,128]{3,2,1,0:T(8,128)S(1)} %bitcast.210, ...), kind=kLoop, calls=%fused_computation.28 | loop fusion | flops 5275648 | bytes 6619136 | tf_op jit(solution)/shard_map/add | solution.py:100
  19.8 0.9 %fusion.21.refs_2_ = f32[2,16,64,128]{3,2,1,0:T(8,128)S(1)} fusion(f32[2,16,64,128]{3,2,1,0:T(8,128)S(1)} %slice.309, f32[1,18,64,128]{3,2,1,0:T(8,128)S(1)} %bitcast.201, f32[1,18,64,128]{3,2,1,0:T(8,128)S(1)} %bitcast.202, f32[2,18,64,128]{3,2,1,0:T(8,128)S(1)} %fusion.10.refs_1_, f32[2,16,64,128]{3,2,1,0:T(8,128)S(1)} %constant_dynamic-update-slice_fusion, ...), kind=kLoop, calls=%fused_computation.44 | loop fusion | flops 3407872 | bytes 6946816 | tf_op jit(solution)/shard_map/add | solution.py:100
  20.7 0.4 pad_maximum_fusion
  21.2 0.6 copy-done.1
  21.8 3.4 %collective-permute-start.2 = (f32[4,12,64,128]{3,2,1,0:T(8,128)S(1)}, f32[4,12,64,128]{3,2,1,0:T(8,128)S(1)}, u32[]{:S(2)}, u32[]{:S(2)}) collective-permute-start(f32[4,12,64,128]{3,2,1,0:T(8,128)S(1)} %get-tuple-element.6), channel_id=1, source_target_pairs={{0,1},{1,2},{2,3},{3,4},{4,5},{5,6},{6,7},{7,8},{8,9},{9,10},{10,1... | collective-permute-start | bytes 4718600 | tf_op jit(solution)/shard_map/ppermute | solution.py:28
  25.1 1.9 %collective-permute-start.3 = (f32[4,12,64,128]{3,2,1,0:T(8,128)S(1)}, f32[4,12,64,128]{3,2,1,0:T(8,128)}, u32[]{:S(2)}, u32[]{:S(2)}) collective-permute-start(f32[4,12,64,128]{3,2,1,0:T(8,128)S(1)} %get-tuple-element.5), channel_id=1, source_target_pairs={{1,0},{2,1},{3,2},{4,3},{5,4},{6,5},{7,6},{8,7},{9,8},{10,9},{11,1... | collective-permute-start | bytes 4718600 | tf_op jit(solution)/shard_map/ppermute | solution.py:29
  27.1 0.7 fusion.44.refs_4_
  27.8 14.7 %collective-permute-done.2.refs_0_ = f32[4,12,64,128]{3,2,1,0:T(8,128)S(1)} collective-permute-done((f32[4,12,64,128]{3,2,1,0:T(8,128)S(1)}, f32[4,12,64,128]{3,2,1,0:T(8,128)S(1)}, u32[]{:S(2)}, u32[]{:S(2)}) %collective-permute-start.2) | collective-permute-done | bytes 1572896 | tf_op jit(solution)/shard_map/ppermute | solution.py:28
  42.5 9.6 %collective-permute-done.3.refs_3_ = f32[4,12,64,128]{3,2,1,0:T(8,128)} collective-permute-done((f32[4,12,64,128]{3,2,1,0:T(8,128)S(1)}, f32[4,12,64,128]{3,2,1,0:T(8,128)}, u32[]{:S(2)}, u32[]{:S(2)}) %collective-permute-start.3) | collective-permute-done | bytes 1572896 | tf_op jit(solution)/shard_map/ppermute | solution.py:29
  52.0 6.0 %shard_map.118 = f32[9,6,16,32]{3,2,1,0:T(8,128)} custom-call(s32[9]{0:T(128)} %offsets_ref.1, f32[4,12,64,128]{3,2,1,0:T(8,128)} %copy-done.6, f32[2,18,64,128]{3,2,1,0:T(8,128)} %copy-done, f32[2,16,64,128]{3,2,1,0:T(8,128)} %copy-done.1, f32[4,12,64,128]{3,2,1,0:T(8,128)} %collective-permute-done.3.refs_3_, f32[128,32]{1,0:T(8,128)} %fusion.44.refs_4_), custom_call_target="tpu_custom_call" | custom-call | tf_op jit(solution)/shard_map/pallas_call | solution.py:175
  58.0 1.3 %fusion.24 = (f32[1,9,6,16,32]{4,3,2,1,0:T(8,128)S(1)}, f32[1,9,6,16,32]{4,3,2,1,0:T(8,128)S(1)}) fusion(f32[9,6,16,32]{3,2,1,0:T(8,128)} %shard_map.118), kind=kLoop, calls=%fused_computation.61 | loop fusion | bytes 331776 | tf_op jit(solution)/shard_map/stack | solution.py:218
  59.5 0.4 copy.51
  59.9 1.5 %all_to_all.8 = f32[16,1,5184]{2,1,0:T(1,128)} reshape(f32[16,3,9,6,32]{4,3,2,1,0:T(8,128)S(1)} %copy.51) | data formatting | bytes 663552 | tf_op jit(solution)/shard_map/all_to_all | solution.py:223
  61.4 8.4 %all-to-all-start = ((f32[16,1,5184]{2,1,0:T(1,128)}), f32[16,1,5184]{2,1,0:T(1,128)S(1)}, u32[]{:S(2)}, u32[]{:S(2)}) async-start(f32[16,1,5184]{2,1,0:T(1,128)} %all_to_all.8), calls=%async_computation | async-start | bytes 671744 | tf_op jit(solution)/shard_map/all_to_all | solution.py:223
  69.9 8.6 %all-to-all-done = f32[16,1,5184]{2,1,0:T(1,128)S(1)} async-done(((f32[16,1,5184]{2,1,0:T(1,128)}), f32[16,1,5184]{2,1,0:T(1,128)S(1)}, u32[]{:S(2)}, u32[]{:S(2)}) %all-to-all-start) | async-done | bytes 331808 | tf_op jit(solution)/shard_map/all_to_all | solution.py:223
  78.5 0.2 reduce_sum.9
  80.5 0.2 reshape.165
  80.8 0.4 fusion.13
  81.2 0.7 copy.79
  (79 shorter events, 3.0 us)
Async XLA Ops:
  0.0 1.3 %copy-start.7 = (f32[1,16,64,128]{3,2,1,0:T(8,128)S(1)}, f32[1,16,64,128]{3,2,1,0:T(8,128)}, u32[]{:S(2)}) copy-start(f32[1,16,64,128]{3,2,1,0:T(8,128)} %param.15) | copy-start | bytes 1572868
  0.0 1.4 %copy-start.3 = (f32[16,64,128]{2,1,0:T(8,128)S(1)}, f32[16,64,128]{2,1,0:T(8,128)}, u32[]{:S(2)}) copy-start(f32[16,64,128]{2,1,0:T(8,128)} %param.16) | copy-start | bytes 1572868
  0.0 1.5 %copy-start.5 = (f32[1,16,64,128]{3,2,1,0:T(8,128)S(1)}, f32[1,16,64,128]{3,2,1,0:T(8,128)}, u32[]{:S(2)}) copy-start(f32[1,16,64,128]{3,2,1,0:T(8,128)} %param.12) | copy-start | bytes 1572868
  0.0 1.7 %copy-start.4 = (f32[1,16,64,128]{3,2,1,0:T(8,128)S(1)}, f32[1,16,64,128]{3,2,1,0:T(8,128)}, u32[]{:S(2)}) copy-start(f32[1,16,64,128]{3,2,1,0:T(8,128)} %param.14) | copy-start | bytes 1572868
  1.4 7.6 %copy-start.10 = (f32[1,2,512]{2,1,0:T(2,128)S(1)}, f32[1,2,512]{2,1,0:T(2,128)}, u32[]{:S(2)}) copy-start(f32[1,2,512]{2,1,0:T(2,128)} %param.20) | copy-start | bytes 12292
  1.4 9.0 %copy-start.9 = (s32[1,512]{1,0:T(1,128)S(1)}, s32[1,512]{1,0:T(1,128)}, u32[]{:S(2)}) copy-start(s32[1,512]{1,0:T(1,128)} %param.19) | copy-start | bytes 6148
  1.7 12.3 %collective-permute-start = (f32[7,64,128]{2,1,0:T(8,128)S(1)}, f32[7,64,128]{2,1,0:T(8,128)S(1)}, u32[]{:S(2)}, u32[]{:S(2)}) collective-permute-start(f32[7,64,128]{2,1,0:T(8,128)S(1)} %pad_maximum_fusion.6), channel_id=1, source_target_pairs={{0,1},{1,2},{2,3},{3,4},{4,5},{5,6},{6,7},{7,8},{8,9},{9,10},{10,1... | collective-permute-start | bytes 688136 | tf_op jit(solution)/shard_map/ppermute | solution.py:49
  7.0 11.0 %collective-permute-start.1 = (f32[7,64,128]{2,1,0:T(8,128)S(1)}, f32[7,64,128]{2,1,0:T(8,128)S(1)}, u32[]{:S(2)}, u32[]{:S(2)}) collective-permute-start(f32[7,64,128]{2,1,0:T(8,128)S(1)} %pad_maximum_fusion.7), channel_id=1, source_target_pairs={{1,0},{2,1},{3,2},{4,3},{5,4},{6,5},{7,6},{8,7},{9,8},{10,9},{11,1... | collective-permute-start | bytes 688136 | tf_op jit(solution)/shard_map/ppermute | solution.py:52
  11.5 0.7 copy-start.11
  19.7 1.0 %copy-start = (f32[2,18,64,128]{3,2,1,0:T(8,128)}, f32[2,18,64,128]{3,2,1,0:T(8,128)S(1)}, u32[]{:S(2)}) copy-start(f32[2,18,64,128]{3,2,1,0:T(8,128)S(1)} %fusion.10.refs_1_) | copy-start | bytes 3538948
  20.7 1.0 %copy-start.1 = (f32[2,16,64,128]{3,2,1,0:T(8,128)}, f32[2,16,64,128]{3,2,1,0:T(8,128)S(1)}, u32[]{:S(2)}) copy-start(f32[2,16,64,128]{3,2,1,0:T(8,128)S(1)} %fusion.21.refs_2_) | copy-start | bytes 3145732
  21.8 20.7 %collective-permute-start.2 = (f32[4,12,64,128]{3,2,1,0:T(8,128)S(1)}, f32[4,12,64,128]{3,2,1,0:T(8,128)S(1)}, u32[]{:S(2)}, u32[]{:S(2)}) collective-permute-start(f32[4,12,64,128]{3,2,1,0:T(8,128)S(1)} %get-tuple-element.6), channel_id=1, source_target_pairs={{0,1},{1,2},{2,3},{3,4},{4,5},{5,6},{6,7},{7,8},{8,9},{9,10},{10,1... | collective-permute-start | bytes 4718600 | tf_op jit(solution)/shard_map/ppermute | solution.py:28
  25.1 26.9 %collective-permute-start.3 = (f32[4,12,64,128]{3,2,1,0:T(8,128)S(1)}, f32[4,12,64,128]{3,2,1,0:T(8,128)}, u32[]{:S(2)}, u32[]{:S(2)}) collective-permute-start(f32[4,12,64,128]{3,2,1,0:T(8,128)S(1)} %get-tuple-element.5), channel_id=1, source_target_pairs={{1,0},{2,1},{3,2},{4,3},{5,4},{6,5},{7,6},{8,7},{9,8},{10,9},{11,1... | collective-permute-start | bytes 4718600 | tf_op jit(solution)/shard_map/ppermute | solution.py:29
  42.5 9.6 %copy-start.6 = (f32[4,12,64,128]{3,2,1,0:T(8,128)}, f32[4,12,64,128]{3,2,1,0:T(8,128)S(1)}, u32[]{:S(2)}) copy-start(f32[4,12,64,128]{3,2,1,0:T(8,128)S(1)} %collective-permute-done.2.refs_0_) | copy-start | bytes 4718596
  58.0 1.3 %copy-start.2 = (f32[9,6,16,32]{3,2,1,0:T(8,128)S(1)}, f32[9,6,16,32]{3,2,1,0:T(8,128)}, u32[]{:S(2)}) copy-start(f32[9,6,16,32]{3,2,1,0:T(8,128)} %shard_map.118) | copy-start | bytes 331780
  59.9 9.9 %copy-start.8 = (f32[64,9,3,3,3]{0,4,3,2,1:T(4,128)S(1)}, f32[64,9,3,3,3]{0,4,3,2,1:T(4,128)}, u32[]{:S(2)}) copy-start(f32[64,9,3,3,3]{0,4,3,2,1:T(4,128)} %param.22) | copy-start | bytes 186628
  61.4 17.0 %all-to-all-start = ((f32[16,1,5184]{2,1,0:T(1,128)}), f32[16,1,5184]{2,1,0:T(1,128)S(1)}, u32[]{:S(2)}, u32[]{:S(2)}) async-start(f32[16,1,5184]{2,1,0:T(1,128)} %all_to_all.8), calls=%async_computation | async-start | bytes 671744 | tf_op jit(solution)/shard_map/all_to_all | solution.py:223
  79.3 1.5 %copy-start.12 = (f32[64]{0:T(128)S(1)}, f32[64]{0:T(128)}, u32[]{:S(2)}) copy-start(f32[64]{0:T(128)} %param.23) | copy-start | bytes 772

commit v14 on v13

--- a/solution.py
+++ b/solution.py
@@ -170,7 +170,9 @@
                 rows = sum_ref.at[index][pl.ds(step, blocks_x * blocks_y, stride=4), :]
                 pooled_y = rows if pooled_y is None else pooled_y + rows
             pooled = split_dot(pooled_y, pool_z_ref[...], True)
-            out_ref[index] = (pooled * (1.0 / 64.0)).reshape(blocks_x, blocks_y, blocks_z)
+            out_ref[index, :, 1 : blocks_y + 1] = (pooled * (1.0 / 64.0)).reshape(blocks_x, blocks_y, blocks_z)
+            out_ref[index, :, 0:1] = jnp.zeros((blocks_x, 1, blocks_z), jnp.float32)
+            out_ref[index, :, blocks_y + 1 :] = jnp.zeros((blocks_x, 1, blocks_z), jnp.float32)
 
     return pl.pallas_call(
         kernel,
@@ -179,14 +181,14 @@
             grid=(1,),
             in_specs=[pl.BlockSpec(memory_space=pl.ANY) for _ in pieces]
             + [pl.BlockSpec((size_z, blocks_z), lambda i, offsets_ref: (0, 0))],
-            out_specs=pl.BlockSpec((count, blocks_x, blocks_y, blocks_z), lambda i, offsets_ref: (0, 0, 0, 0)),
+            out_specs=pl.BlockSpec((count, blocks_x, blocks_y + 2, blocks_z), lambda i, offsets_ref: (0, 0, 0, 0)),
             scratch_shapes=[
                 pltpu.VMEM((fields, span_x, size_y, size_z), jnp.float32),
                 pltpu.VMEM((count, blocks_x * size_y, size_z), jnp.float32),
                 pltpu.SemaphoreType.DMA((len(pieces),)),
             ],
         ),
-        out_shape=jax.ShapeDtypeStruct((count, blocks_x, blocks_y, blocks_z), jnp.float32),
+        out_shape=jax.ShapeDtypeStruct((count, blocks_x, blocks_y + 2, blocks_z), jnp.float32),
     )(offsets, *[piece[0] for piece in pieces], pool_z)
 
 
@@ -213,8 +215,8 @@
 
 def group_sum_windows(coarse, axis):
     count = lax.axis_size(axis)
-    rows = coarse.shape[2] // count
-    rimmed = jnp.pad(coarse, ((0, 0), (0, 0), (1, 1), (0, 0)))
+    rimmed = coarse
+    rows = (coarse.shape[2] - 2) // count
     windows = jnp.stack(
         [lax.slice_in_dim(rimmed, k, k + (count - 1) * rows + 1, stride=rows, axis=2) for k in range(rows + 2)]
     )

time: 82.3 us -> 82.8 us (level)
    unnamed x53 -> x51, local copies, waits for them, and re-layouts: 4.39 us -> 4.38 us
where the time goes in v14:
time: 82.8 us; the launch traced here: 82.3 us
  waiting for transfers between devices  36.7 us (44%)
  starting transfers between devices  20.9 us (25%)
  local copies, waits for them, and re-layouts  9.42 us (11%)
  other arithmetic  6.14 us (7%)
  Pallas kernels  6.03 us (7%)
  matrix products  2.66 us (3%)
    ppermute x1, waiting for transfers between devices, halo_pieces(): low = lax.ppermute(block[:, block.shape[1] - width:], axis, forward)  14.7 us
    ppermute x1, waiting for transfers between devices, halo_pieces(): high = lax.ppermute(block[:, :width], axis, backward)  9.51 us
    all_to_all x1, waiting for transfers between devices, group_sum_windows(): lax.all_to_all(windows.reshape(count, -1), axis, 0, 0, tiled=True)  8.57 us
    all_to_all x1, starting transfers between devices, group_sum_windows(): lax.all_to_all(windows.reshape(count, -1), axis, 0, 0, tiled=True)  8.41 us
    pallas_call x1, Pallas kernels, offset_image(): pl.pallas_call(kernel, grid_spec=pltpu.PrefetchScalarGridSpec(num_scalar_...  6.03 us
    ppermute x1, starting transfers between devices, input_halo(): lax.ppermute(pack(current[:, -2:], previous[:, -1:], courant[-1:]), axis,...  5.3 us
    unnamed x51, local copies, waits for them, and re-layouts  4.38 us
    ppermute x1, waiting for transfers between devices, input_halo(): lax.ppermute(pack(current[:, :2], previous[:, :1], courant[:1]), axis, ba...  3.91 us
  transfers between devices with their start and end apart: 5, of which 4 were waited for; matrix products, arithmetic and copies ran while one was open for 6% of the time, Pallas kernels for 0%

profile of v14, /device:TPU:39, one launch (start us, length us, event | category | flops | bytes accessed | tf_op | source)
XLA Modules:
  0.0 82.3 jit_solution(14666623232591448996)
XLA Ops:
  0.0 1.2 %constant_dynamic-update-slice_fusion.1 = f32[2,16,64,128]{3,2,1,0:T(8,128)S(1)} fusion(f32[1,16,64,128]{3,2,1,0:T(8,128)} %param.13), kind=kLoop, calls=%fused_computation.96 | loop fusion | bytes 1048576
  1.5 0.2 copy-done.3
  1.7 5.3 %collective-permute-start = (f32[7,64,128]{2,1,0:T(8,128)S(1)}, f32[7,64,128]{2,1,0:T(8,128)S(1)}, u32[]{:S(2)}, u32[]{:S(2)}) collective-permute-start(f32[7,64,128]{2,1,0:T(8,128)S(1)} %pad_maximum_fusion.6), channel_id=1, source_target_pairs={{0,1},{1,2},{2,3},{3,4},{4,5},{5,6},{6,7},{7,8},{8,9},{9,10},{10,1... | collective-permute-start | bytes 688136 | tf_op jit(solution)/shard_map/ppermute | solution.py:49
  7.0 1.9 %collective-permute-start.1 = (f32[7,64,128]{2,1,0:T(8,128)S(1)}, f32[7,64,128]{2,1,0:T(8,128)S(1)}, u32[]{:S(2)}, u32[]{:S(2)}) collective-permute-start(f32[7,64,128]{2,1,0:T(8,128)S(1)} %pad_maximum_fusion.7), channel_id=1, source_target_pairs={{1,0},{2,1},{3,2},{4,3},{5,4},{6,5},{7,6},{8,7},{9,8},{10,9},{11,1... | collective-permute-start | bytes 688136 | tf_op jit(solution)/shard_map/ppermute | solution.py:52
  9.0 0.7 and_select_fusion.4
  9.7 0.7 add_bitcast_fusion
  10.4 0.3 reduce-precision_convert_fusion.1
  10.7 0.8 fusion.1
  11.6 0.6 copy-done.10
  12.3 0.4 fusion.23
  12.7 0.8 fusion
  13.6 0.4 fusion.22
  14.1 3.9 %collective-permute-done.1 = f32[7,64,128]{2,1,0:T(8,128)S(1)} collective-permute-done((f32[7,64,128]{2,1,0:T(8,128)S(1)}, f32[7,64,128]{2,1,0:T(8,128)S(1)}, u32[]{:S(2)}, u32[]{:S(2)}) %collective-permute-start.1) | collective-permute-done | bytes 229408 | tf_op jit(solution)/shard_map/ppermute | solution.py:52
  18.2 1.5 %fusion.10.refs_1_ = f32[2,18,64,128]{3,2,1,0:T(8,128)S(1)} fusion(f32[2,18,64,128]{3,2,1,0:T(8,128)S(1)} %pad_maximum_fusion.2, f32[2,1,64,128]{3,2,1,0:T(8,128)S(1)} %slice_bitcast_fusion.3, f32[2,1,64,128]{3,2,1,0:T(8,128)S(1)} %slice_bitcast_fusion.4, f32[2,2,64,128]{3,2,1,0:T(8,128)S(1)} %bitcast.210, ...), kind=kLoop, calls=%fused_computation.28 | loop fusion | flops 5275648 | bytes 6619136 | tf_op jit(solution)/shard_map/add | solution.py:100
  19.8 0.9 %fusion.21.refs_2_ = f32[2,16,64,128]{3,2,1,0:T(8,128)S(1)} fusion(f32[2,16,64,128]{3,2,1,0:T(8,128)S(1)} %slice.312, f32[1,18,64,128]{3,2,1,0:T(8,128)S(1)} %bitcast.201, f32[1,18,64,128]{3,2,1,0:T(8,128)S(1)} %bitcast.202, f32[2,18,64,128]{3,2,1,0:T(8,128)S(1)} %fusion.10.refs_1_, f32[2,16,64,128]{3,2,1,0:T(8,128)S(1)} %constant_dynamic-update-slice_fusion, ...), kind=kLoop, calls=%fused_computation.44 | loop fusion | flops 3407872 | bytes 6946816 | tf_op jit(solution)/shard_map/add | solution.py:100
  20.8 0.4 pad_maximum_fusion
  21.2 0.6 copy-done.1
  21.8 3.4 %collective-permute-start.2 = (f32[4,12,64,128]{3,2,1,0:T(8,128)S(1)}, f32[4,12,64,128]{3,2,1,0:T(8,128)S(1)}, u32[]{:S(2)}, u32[]{:S(2)}) collective-permute-start(f32[4,12,64,128]{3,2,1,0:T(8,128)S(1)} %get-tuple-element.6), channel_id=1, source_target_pairs={{0,1},{1,2},{2,3},{3,4},{4,5},{5,6},{6,7},{7,8},{8,9},{9,10},{10,1... | collective-permute-start | bytes 4718600 | tf_op jit(solution)/shard_map/ppermute | solution.py:28
  25.1 1.9 %collective-permute-start.3 = (f32[4,12,64,128]{3,2,1,0:T(8,128)S(1)}, f32[4,12,64,128]{3,2,1,0:T(8,128)}, u32[]{:S(2)}, u32[]{:S(2)}) collective-permute-start(f32[4,12,64,128]{3,2,1,0:T(8,128)S(1)} %get-tuple-element.5), channel_id=1, source_target_pairs={{1,0},{2,1},{3,2},{4,3},{5,4},{6,5},{7,6},{8,7},{9,8},{10,9},{11,1... | collective-permute-start | bytes 4718600 | tf_op jit(solution)/shard_map/ppermute | solution.py:29
  27.1 0.7 fusion.42.refs_4_
  27.8 14.7 %collective-permute-done.2.refs_0_ = f32[4,12,64,128]{3,2,1,0:T(8,128)S(1)} collective-permute-done((f32[4,12,64,128]{3,2,1,0:T(8,128)S(1)}, f32[4,12,64,128]{3,2,1,0:T(8,128)S(1)}, u32[]{:S(2)}, u32[]{:S(2)}) %collective-permute-start.2) | collective-permute-done | bytes 1572896 | tf_op jit(solution)/shard_map/ppermute | solution.py:28
  42.5 9.5 %collective-permute-done.3.refs_3_ = f32[4,12,64,128]{3,2,1,0:T(8,128)} collective-permute-done((f32[4,12,64,128]{3,2,1,0:T(8,128)S(1)}, f32[4,12,64,128]{3,2,1,0:T(8,128)}, u32[]{:S(2)}, u32[]{:S(2)}) %collective-permute-start.3) | collective-permute-done | bytes 1572896 | tf_op jit(solution)/shard_map/ppermute | solution.py:29
  52.0 6.0 %shard_map.118 = f32[9,6,18,32]{3,2,1,0:T(8,128)} custom-call(s32[9]{0:T(128)} %offsets_ref.1, f32[4,12,64,128]{3,2,1,0:T(8,128)} %copy-done.5, f32[2,18,64,128]{3,2,1,0:T(8,128)} %copy-done, f32[2,16,64,128]{3,2,1,0:T(8,128)} %copy-done.1, f32[4,12,64,128]{3,2,1,0:T(8,128)} %collective-permute-done.3.refs_3_, f32[128,32]{1,0:T(8,128)} %fusion.42.refs_4_), custom_call_target="tpu_custom_call" | custom-call | tf_op jit(solution)/shard_map/pallas_call | solution.py:177
  58.0 1.7 %slice_bitcast_fusion.2 = (f32[1,9,6,16,32]{4,3,2,1,0:T(8,128)S(1)}, f32[1,9,6,16,32]{4,3,2,1,0:T(8,128)S(1)}, f32[1,9,6,16,32]{4,3,2,1,0:T(8,128)S(1)}) fusion(f32[9,6,18,32]{3,2,1,0:T(8,128)} %shard_map.118), kind=kLoop, calls=%fused_computation.61 | loop fusion | bytes 663552 | tf_op jit(solution)/shard_map/stack | solution.py:220
  59.9 0.4 copy.51
  60.3 1.5 %all_to_all.8 = f32[16,1,5184]{2,1,0:T(1,128)} reshape(f32[16,3,9,6,32]{4,3,2,1,0:T(8,128)S(1)} %copy.51) | data formatting | bytes 663552 | tf_op jit(solution)/shard_map/all_to_all | solution.py:225
  61.8 8.4 %all-to-all-start = ((f32[16,1,5184]{2,1,0:T(1,128)}), f32[16,1,5184]{2,1,0:T(1,128)S(1)}, u32[]{:S(2)}, u32[]{:S(2)}) async-start(f32[16,1,5184]{2,1,0:T(1,128)} %all_to_all.8), calls=%async_computation | async-start | bytes 671744 | tf_op jit(solution)/shard_map/all_to_all | solution.py:225
  70.3 8.6 %all-to-all-done = f32[16,1,5184]{2,1,0:T(1,128)S(1)} async-done(((f32[16,1,5184]{2,1,0:T(1,128)}), f32[16,1,5184]{2,1,0:T(1,128)S(1)}, u32[]{:S(2)}, u32[]{:S(2)}) %all-to-all-start) | async-done | bytes 331808 | tf_op jit(solution)/shard_map/all_to_all | solution.py:225
  78.9 0.2 reduce_sum.9
  81.0 0.2 reshape.165
  81.2 0.4 fusion.13
  81.6 0.7 copy.79
  (77 shorter events, 3.0 us)
Async XLA Ops:
  0.0 1.3 %copy-start.6 = (f32[1,16,64,128]{3,2,1,0:T(8,128)S(1)}, f32[1,16,64,128]{3,2,1,0:T(8,128)}, u32[]{:S(2)}) copy-start(f32[1,16,64,128]{3,2,1,0:T(8,128)} %param.15) | copy-start | bytes 1572868
  0.0 1.4 %copy-start.2 = (f32[16,64,128]{2,1,0:T(8,128)S(1)}, f32[16,64,128]{2,1,0:T(8,128)}, u32[]{:S(2)}) copy-start(f32[16,64,128]{2,1,0:T(8,128)} %param.16) | copy-start | bytes 1572868
  0.0 1.5 %copy-start.4 = (f32[1,16,64,128]{3,2,1,0:T(8,128)S(1)}, f32[1,16,64,128]{3,2,1,0:T(8,128)}, u32[]{:S(2)}) copy-start(f32[1,16,64,128]{3,2,1,0:T(8,128)} %param.12) | copy-start | bytes 1572868
  0.0 1.7 %copy-start.3 = (f32[1,16,64,128]{3,2,1,0:T(8,128)S(1)}, f32[1,16,64,128]{3,2,1,0:T(8,128)}, u32[]{:S(2)}) copy-start(f32[1,16,64,128]{3,2,1,0:T(8,128)} %param.14) | copy-start | bytes 1572868
  1.4 7.6 %copy-start.9 = (f32[1,2,512]{2,1,0:T(2,128)S(1)}, f32[1,2,512]{2,1,0:T(2,128)}, u32[]{:S(2)}) copy-start(f32[1,2,512]{2,1,0:T(2,128)} %param.20) | copy-start | bytes 12292
  1.4 9.0 %copy-start.8 = (s32[1,512]{1,0:T(1,128)S(1)}, s32[1,512]{1,0:T(1,128)}, u32[]{:S(2)}) copy-start(s32[1,512]{1,0:T(1,128)} %param.19) | copy-start | bytes 6148
  1.7 12.3 %collective-permute-start = (f32[7,64,128]{2,1,0:T(8,128)S(1)}, f32[7,64,128]{2,1,0:T(8,128)S(1)}, u32[]{:S(2)}, u32[]{:S(2)}) collective-permute-start(f32[7,64,128]{2,1,0:T(8,128)S(1)} %pad_maximum_fusion.6), channel_id=1, source_target_pairs={{0,1},{1,2},{2,3},{3,4},{4,5},{5,6},{6,7},{7,8},{8,9},{9,10},{10,1... | collective-permute-start | bytes 688136 | tf_op jit(solution)/shard_map/ppermute | solution.py:49
  7.0 11.0 %collective-permute-start.1 = (f32[7,64,128]{2,1,0:T(8,128)S(1)}, f32[7,64,128]{2,1,0:T(8,128)S(1)}, u32[]{:S(2)}, u32[]{:S(2)}) collective-permute-start(f32[7,64,128]{2,1,0:T(8,128)S(1)} %pad_maximum_fusion.7), channel_id=1, source_target_pairs={{1,0},{2,1},{3,2},{4,3},{5,4},{6,5},{7,6},{8,7},{9,8},{10,9},{11,1... | collective-permute-start | bytes 688136 | tf_op jit(solution)/shard_map/ppermute | solution.py:52
  11.5 0.7 copy-start.10
  19.7 1.0 %copy-start = (f32[2,18,64,128]{3,2,1,0:T(8,128)}, f32[2,18,64,128]{3,2,1,0:T(8,128)S(1)}, u32[]{:S(2)}) copy-start(f32[2,18,64,128]{3,2,1,0:T(8,128)S(1)} %fusion.10.refs_1_) | copy-start | bytes 3538948
  20.8 1.0 %copy-start.1 = (f32[2,16,64,128]{3,2,1,0:T(8,128)}, f32[2,16,64,128]{3,2,1,0:T(8,128)S(1)}, u32[]{:S(2)}) copy-start(f32[2,16,64,128]{3,2,1,0:T(8,128)S(1)} %fusion.21.refs_2_) | copy-start | bytes 3145732
  21.8 20.7 %collective-permute-start.2 = (f32[4,12,64,128]{3,2,1,0:T(8,128)S(1)}, f32[4,12,64,128]{3,2,1,0:T(8,128)S(1)}, u32[]{:S(2)}, u32[]{:S(2)}) collective-permute-start(f32[4,12,64,128]{3,2,1,0:T(8,128)S(1)} %get-tuple-element.6), channel_id=1, source_target_pairs={{0,1},{1,2},{2,3},{3,4},{4,5},{5,6},{6,7},{7,8},{8,9},{9,10},{10,1... | collective-permute-start | bytes 4718600 | tf_op jit(solution)/shard_map/ppermute | solution.py:28
  25.1 26.9 %collective-permute-start.3 = (f32[4,12,64,128]{3,2,1,0:T(8,128)S(1)}, f32[4,12,64,128]{3,2,1,0:T(8,128)}, u32[]{:S(2)}, u32[]{:S(2)}) collective-permute-start(f32[4,12,64,128]{3,2,1,0:T(8,128)S(1)} %get-tuple-element.5), channel_id=1, source_target_pairs={{1,0},{2,1},{3,2},{4,3},{5,4},{6,5},{7,6},{8,7},{9,8},{10,9},{11,1... | collective-permute-start | bytes 4718600 | tf_op jit(solution)/shard_map/ppermute | solution.py:29
  42.5 9.5 %copy-start.5 = (f32[4,12,64,128]{3,2,1,0:T(8,128)}, f32[4,12,64,128]{3,2,1,0:T(8,128)S(1)}, u32[]{:S(2)}) copy-start(f32[4,12,64,128]{3,2,1,0:T(8,128)S(1)} %collective-permute-done.2.refs_0_) | copy-start | bytes 4718596
  60.3 9.9 %copy-start.7 = (f32[64,9,3,3,3]{0,4,3,2,1:T(4,128)S(1)}, f32[64,9,3,3,3]{0,4,3,2,1:T(4,128)}, u32[]{:S(2)}) copy-start(f32[64,9,3,3,3]{0,4,3,2,1:T(4,128)} %param.22) | copy-start | bytes 186628
  61.8 17.1 %all-to-all-start = ((f32[16,1,5184]{2,1,0:T(1,128)}), f32[16,1,5184]{2,1,0:T(1,128)S(1)}, u32[]{:S(2)}, u32[]{:S(2)}) async-start(f32[16,1,5184]{2,1,0:T(1,128)} %all_to_all.8), calls=%async_computation | async-start | bytes 671744 | tf_op jit(solution)/shard_map/all_to_all | solution.py:225
  79.8 1.5 %copy-start.11 = (f32[64]{0:T(128)S(1)}, f32[64]{0:T(128)}, u32[]{:S(2)}) copy-start(f32[64]{0:T(128)} %param.23) | copy-start | bytes 772

commit v15 on v13

--- a/solution.py
+++ b/solution.py
@@ -169,7 +169,12 @@
             for step in range(4):
                 rows = sum_ref.at[index][pl.ds(step, blocks_x * blocks_y, stride=4), :]
                 pooled_y = rows if pooled_y is None else pooled_y + rows
-            pooled = split_dot(pooled_y, pool_z_ref[...], True)
+            high = pooled_y.astype(jnp.bfloat16)
+            low = (pooled_y - high.astype(jnp.float32)).astype(jnp.bfloat16)
+            pool_z_values = pool_z_ref[...].astype(jnp.bfloat16)
+            pooled = jnp.dot(high, pool_z_values, preferred_element_type=jnp.float32) + jnp.dot(
+                low, pool_z_values, preferred_element_type=jnp.float32
+            )
             out_ref[index] = (pooled * (1.0 / 64.0)).reshape(blocks_x, blocks_y, blocks_z)
 
     return pl.pallas_call(

time: 82.3 us -> 82.3 us (level)
  no operation moved by 1% of the time
where the time goes in v15:
time: 82.3 us; the launch traced here: 81.9 us
  waiting for transfers between devices  36.7 us (45%)
  starting transfers between devices  20.9 us (25%)
  local copies, waits for them, and re-layouts  9.04 us (11%)
  other arithmetic  6.14 us (7%)
  Pallas kernels  5.9 us (7%)
  matrix products  2.66 us (3%)
    ppermute x1, waiting for transfers between devices, halo_pieces(): low = lax.ppermute(block[:, block.shape[1] - width:], axis, forward)  14.7 us
    ppermute x1, waiting for transfers between devices, halo_pieces(): high = lax.ppermute(block[:, :width], axis, backward)  9.56 us
    all_to_all x1, waiting for transfers between devices, group_sum_windows(): lax.all_to_all(windows.reshape(count, -1), axis, 0, 0, tiled=True)  8.57 us
    all_to_all x1, starting transfers between devices, group_sum_windows(): lax.all_to_all(windows.reshape(count, -1), axis, 0, 0, tiled=True)  8.37 us
    pallas_call x1, Pallas kernels, offset_image(): pl.pallas_call(kernel, grid_spec=pltpu.PrefetchScalarGridSpec(num_scalar_...  5.9 us
    ppermute x1, starting transfers between devices, input_halo(): lax.ppermute(pack(current[:, -2:], previous[:, -1:], courant[-1:]), axis,...  5.3 us
    unnamed x53, local copies, waits for them, and re-layouts  4.39 us
    ppermute x1, waiting for transfers between devices, input_halo(): lax.ppermute(pack(current[:, :2], previous[:, :1], courant[:1]), axis, ba...  3.91 us
  transfers between devices with their start and end apart: 5, of which 4 were waited for; matrix products, arithmetic and copies ran while one was open for 6% of the time, Pallas kernels for 0%

profile of v15, /device:TPU:39, one launch (start us, length us, event | category | flops | bytes accessed | tf_op | source)
XLA Modules:
  0.0 81.9 jit_solution(661647483544966387)
XLA Ops:
  0.0 1.2 %constant_dynamic-update-slice_fusion.1 = f32[2,16,64,128]{3,2,1,0:T(8,128)S(1)} fusion(f32[1,16,64,128]{3,2,1,0:T(8,128)} %param.13), kind=kLoop, calls=%fused_computation.97 | loop fusion | bytes 1048576
  1.5 0.2 copy-done.4
  1.7 5.3 %collective-permute-start = (f32[7,64,128]{2,1,0:T(8,128)S(1)}, f32[7,64,128]{2,1,0:T(8,128)S(1)}, u32[]{:S(2)}, u32[]{:S(2)}) collective-permute-start(f32[7,64,128]{2,1,0:T(8,128)S(1)} %pad_maximum_fusion.6), channel_id=1, source_target_pairs={{0,1},{1,2},{2,3},{3,4},{4,5},{5,6},{6,7},{7,8},{8,9},{9,10},{10,1... | collective-permute-start | bytes 688136 | tf_op jit(solution)/shard_map/ppermute | solution.py:49
  7.0 1.9 %collective-permute-start.1 = (f32[7,64,128]{2,1,0:T(8,128)S(1)}, f32[7,64,128]{2,1,0:T(8,128)S(1)}, u32[]{:S(2)}, u32[]{:S(2)}) collective-permute-start(f32[7,64,128]{2,1,0:T(8,128)S(1)} %pad_maximum_fusion.7), channel_id=1, source_target_pairs={{1,0},{2,1},{3,2},{4,3},{5,4},{6,5},{7,6},{8,7},{9,8},{10,9},{11,1... | collective-permute-start | bytes 688136 | tf_op jit(solution)/shard_map/ppermute | solution.py:52
  9.0 0.7 and_select_fusion.4
  9.7 0.7 add_bitcast_fusion
  10.4 0.3 reduce-precision_convert_fusion.1
  10.7 0.8 fusion.1
  11.6 0.6 copy-done.11
  12.3 0.4 fusion.23
  12.7 0.8 fusion
  13.6 0.4 fusion.22
  14.1 3.9 %collective-permute-done.1 = f32[7,64,128]{2,1,0:T(8,128)S(1)} collective-permute-done((f32[7,64,128]{2,1,0:T(8,128)S(1)}, f32[7,64,128]{2,1,0:T(8,128)S(1)}, u32[]{:S(2)}, u32[]{:S(2)}) %collective-permute-start.1) | collective-permute-done | bytes 229408 | tf_op jit(solution)/shard_map/ppermute | solution.py:52
  18.2 1.5 %fusion.10.refs_1_ = f32[2,18,64,128]{3,2,1,0:T(8,128)S(1)} fusion(f32[2,18,64,128]{3,2,1,0:T(8,128)S(1)} %pad_maximum_fusion.2, f32[2,1,64,128]{3,2,1,0:T(8,128)S(1)} %slice_bitcast_fusion, f32[2,1,64,128]{3,2,1,0:T(8,128)S(1)} %slice_bitcast_fusion.1, f32[2,2,64,128]{3,2,1,0:T(8,128)S(1)} %bitcast.210, ...), kind=kLoop, calls=%fused_computation.28 | loop fusion | flops 5275648 | bytes 6619136 | tf_op jit(solution)/shard_map/add | solution.py:100
  19.8 0.9 %fusion.21.refs_2_ = f32[2,16,64,128]{3,2,1,0:T(8,128)S(1)} fusion(f32[2,16,64,128]{3,2,1,0:T(8,128)S(1)} %slice.309, f32[1,18,64,128]{3,2,1,0:T(8,128)S(1)} %bitcast.201, f32[1,18,64,128]{3,2,1,0:T(8,128)S(1)} %bitcast.202, f32[2,18,64,128]{3,2,1,0:T(8,128)S(1)} %fusion.10.refs_1_, f32[2,16,64,128]{3,2,1,0:T(8,128)S(1)} %constant_dynamic-update-slice_fusion, ...), kind=kLoop, calls=%fused_computation.44 | loop fusion | flops 3407872 | bytes 6946816 | tf_op jit(solution)/shard_map/add | solution.py:100
  20.7 0.4 pad_maximum_fusion
  21.2 0.6 copy-done.1
  21.8 3.4 %collective-permute-start.2 = (f32[4,12,64,128]{3,2,1,0:T(8,128)S(1)}, f32[4,12,64,128]{3,2,1,0:T(8,128)S(1)}, u32[]{:S(2)}, u32[]{:S(2)}) collective-permute-start(f32[4,12,64,128]{3,2,1,0:T(8,128)S(1)} %get-tuple-element.6), channel_id=1, source_target_pairs={{0,1},{1,2},{2,3},{3,4},{4,5},{5,6},{6,7},{7,8},{8,9},{9,10},{10,1... | collective-permute-start | bytes 4718600 | tf_op jit(solution)/shard_map/ppermute | solution.py:28
  25.1 1.9 %collective-permute-start.3 = (f32[4,12,64,128]{3,2,1,0:T(8,128)S(1)}, f32[4,12,64,128]{3,2,1,0:T(8,128)}, u32[]{:S(2)}, u32[]{:S(2)}) collective-permute-start(f32[4,12,64,128]{3,2,1,0:T(8,128)S(1)} %get-tuple-element.5), channel_id=1, source_target_pairs={{1,0},{2,1},{3,2},{4,3},{5,4},{6,5},{7,6},{8,7},{9,8},{10,9},{11,1... | collective-permute-start | bytes 4718600 | tf_op jit(solution)/shard_map/ppermute | solution.py:29
  27.1 0.7 fusion.44.refs_4_
  27.8 14.7 %collective-permute-done.2.refs_0_ = f32[4,12,64,128]{3,2,1,0:T(8,128)S(1)} collective-permute-done((f32[4,12,64,128]{3,2,1,0:T(8,128)S(1)}, f32[4,12,64,128]{3,2,1,0:T(8,128)S(1)}, u32[]{:S(2)}, u32[]{:S(2)}) %collective-permute-start.2) | collective-permute-done | bytes 1572896 | tf_op jit(solution)/shard_map/ppermute | solution.py:28
  42.5 9.6 %collective-permute-done.3.refs_3_ = f32[4,12,64,128]{3,2,1,0:T(8,128)} collective-permute-done((f32[4,12,64,128]{3,2,1,0:T(8,128)S(1)}, f32[4,12,64,128]{3,2,1,0:T(8,128)}, u32[]{:S(2)}, u32[]{:S(2)}) %collective-permute-start.3) | collective-permute-done | bytes 1572896 | tf_op jit(solution)/shard_map/ppermute | solution.py:29
  52.0 5.9 %shard_map.118 = f32[9,6,16,32]{3,2,1,0:T(8,128)} custom-call(s32[9]{0:T(128)} %offsets_ref.1, f32[4,12,64,128]{3,2,1,0:T(8,128)} %copy-done.6, f32[2,18,64,128]{3,2,1,0:T(8,128)} %copy-done, f32[2,16,64,128]{3,2,1,0:T(8,128)} %copy-done.1, f32[4,12,64,128]{3,2,1,0:T(8,128)} %collective-permute-done.3.refs_3_, f32[128,32]{1,0:T(8,128)} %fusion.44.refs_4_), custom_call_target="tpu_custom_call" | custom-call | tf_op jit(solution)/shard_map/pallas_call | solution.py:180
  58.0 1.3 %fusion.24 = (f32[1,9,6,16,32]{4,3,2,1,0:T(8,128)S(1)}, f32[1,9,6,16,32]{4,3,2,1,0:T(8,128)S(1)}) fusion(f32[9,6,16,32]{3,2,1,0:T(8,128)} %shard_map.118), kind=kLoop, calls=%fused_computation.61 | loop fusion | bytes 331776 | tf_op jit(solution)/shard_map/stack | solution.py:223
  59.4 0.4 copy.51
  59.9 1.5 %all_to_all.8 = f32[16,1,5184]{2,1,0:T(1,128)} reshape(f32[16,3,9,6,32]{4,3,2,1,0:T(8,128)S(1)} %copy.51) | data formatting | bytes 663552 | tf_op jit(solution)/shard_map/all_to_all | solution.py:228
  61.4 8.4 %all-to-all-start = ((f32[16,1,5184]{2,1,0:T(1,128)}), f32[16,1,5184]{2,1,0:T(1,128)S(1)}, u32[]{:S(2)}, u32[]{:S(2)}) async-start(f32[16,1,5184]{2,1,0:T(1,128)} %all_to_all.8), calls=%async_computation | async-start | bytes 671744 | tf_op jit(solution)/shard_map/all_to_all | solution.py:228
  69.8 8.6 %all-to-all-done = f32[16,1,5184]{2,1,0:T(1,128)S(1)} async-done(((f32[16,1,5184]{2,1,0:T(1,128)}), f32[16,1,5184]{2,1,0:T(1,128)S(1)}, u32[]{:S(2)}, u32[]{:S(2)}) %all-to-all-start) | async-done | bytes 331808 | tf_op jit(solution)/shard_map/all_to_all | solution.py:228
  78.4 0.2 reduce_sum.9
  80.5 0.2 reshape.165
  80.7 0.4 fusion.13
  81.1 0.7 copy.79
  (79 shorter events, 3.0 us)
Async XLA Ops:
  0.0 1.3 %copy-start.7 = (f32[1,16,64,128]{3,2,1,0:T(8,128)S(1)}, f32[1,16,64,128]{3,2,1,0:T(8,128)}, u32[]{:S(2)}) copy-start(f32[1,16,64,128]{3,2,1,0:T(8,128)} %param.15) | copy-start | bytes 1572868
  0.0 1.4 %copy-start.3 = (f32[16,64,128]{2,1,0:T(8,128)S(1)}, f32[16,64,128]{2,1,0:T(8,128)}, u32[]{:S(2)}) copy-start(f32[16,64,128]{2,1,0:T(8,128)} %param.16) | copy-start | bytes 1572868
  0.0 1.5 %copy-start.5 = (f32[1,16,64,128]{3,2,1,0:T(8,128)S(1)}, f32[1,16,64,128]{3,2,1,0:T(8,128)}, u32[]{:S(2)}) copy-start(f32[1,16,64,128]{3,2,1,0:T(8,128)} %param.12) | copy-start | bytes 1572868
  0.0 1.7 %copy-start.4 = (f32[1,16,64,128]{3,2,1,0:T(8,128)S(1)}, f32[1,16,64,128]{3,2,1,0:T(8,128)}, u32[]{:S(2)}) copy-start(f32[1,16,64,128]{3,2,1,0:T(8,128)} %param.14) | copy-start | bytes 1572868
  1.4 7.6 %copy-start.10 = (f32[1,2,512]{2,1,0:T(2,128)S(1)}, f32[1,2,512]{2,1,0:T(2,128)}, u32[]{:S(2)}) copy-start(f32[1,2,512]{2,1,0:T(2,128)} %param.20) | copy-start | bytes 12292
  1.4 9.0 %copy-start.9 = (s32[1,512]{1,0:T(1,128)S(1)}, s32[1,512]{1,0:T(1,128)}, u32[]{:S(2)}) copy-start(s32[1,512]{1,0:T(1,128)} %param.19) | copy-start | bytes 6148
  1.7 12.3 %collective-permute-start = (f32[7,64,128]{2,1,0:T(8,128)S(1)}, f32[7,64,128]{2,1,0:T(8,128)S(1)}, u32[]{:S(2)}, u32[]{:S(2)}) collective-permute-start(f32[7,64,128]{2,1,0:T(8,128)S(1)} %pad_maximum_fusion.6), channel_id=1, source_target_pairs={{0,1},{1,2},{2,3},{3,4},{4,5},{5,6},{6,7},{7,8},{8,9},{9,10},{10,1... | collective-permute-start | bytes 688136 | tf_op jit(solution)/shard_map/ppermute | solution.py:49
  7.0 11.0 %collective-permute-start.1 = (f32[7,64,128]{2,1,0:T(8,128)S(1)}, f32[7,64,128]{2,1,0:T(8,128)S(1)}, u32[]{:S(2)}, u32[]{:S(2)}) collective-permute-start(f32[7,64,128]{2,1,0:T(8,128)S(1)} %pad_maximum_fusion.7), channel_id=1, source_target_pairs={{1,0},{2,1},{3,2},{4,3},{5,4},{6,5},{7,6},{8,7},{9,8},{10,9},{11,1... | collective-permute-start | bytes 688136 | tf_op jit(solution)/shard_map/ppermute | solution.py:52
  11.5 0.7 copy-start.11
  19.7 1.0 %copy-start = (f32[2,18,64,128]{3,2,1,0:T(8,128)}, f32[2,18,64,128]{3,2,1,0:T(8,128)S(1)}, u32[]{:S(2)}) copy-start(f32[2,18,64,128]{3,2,1,0:T(8,128)S(1)} %fusion.10.refs_1_) | copy-start | bytes 3538948
  20.7 1.0 %copy-start.1 = (f32[2,16,64,128]{3,2,1,0:T(8,128)}, f32[2,16,64,128]{3,2,1,0:T(8,128)S(1)}, u32[]{:S(2)}) copy-start(f32[2,16,64,128]{3,2,1,0:T(8,128)S(1)} %fusion.21.refs_2_) | copy-start | bytes 3145732
  21.8 20.7 %collective-permute-start.2 = (f32[4,12,64,128]{3,2,1,0:T(8,128)S(1)}, f32[4,12,64,128]{3,2,1,0:T(8,128)S(1)}, u32[]{:S(2)}, u32[]{:S(2)}) collective-permute-start(f32[4,12,64,128]{3,2,1,0:T(8,128)S(1)} %get-tuple-element.6), channel_id=1, source_target_pairs={{0,1},{1,2},{2,3},{3,4},{4,5},{5,6},{6,7},{7,8},{8,9},{9,10},{10,1... | collective-permute-start | bytes 4718600 | tf_op jit(solution)/shard_map/ppermute | solution.py:28
  25.1 26.9 %collective-permute-start.3 = (f32[4,12,64,128]{3,2,1,0:T(8,128)S(1)}, f32[4,12,64,128]{3,2,1,0:T(8,128)}, u32[]{:S(2)}, u32[]{:S(2)}) collective-permute-start(f32[4,12,64,128]{3,2,1,0:T(8,128)S(1)} %get-tuple-element.5), channel_id=1, source_target_pairs={{1,0},{2,1},{3,2},{4,3},{5,4},{6,5},{7,6},{8,7},{9,8},{10,9},{11,1... | collective-permute-start | bytes 4718600 | tf_op jit(solution)/shard_map/ppermute | solution.py:29
  42.5 9.6 %copy-start.6 = (f32[4,12,64,128]{3,2,1,0:T(8,128)}, f32[4,12,64,128]{3,2,1,0:T(8,128)S(1)}, u32[]{:S(2)}) copy-start(f32[4,12,64,128]{3,2,1,0:T(8,128)S(1)} %collective-permute-done.2.refs_0_) | copy-start | bytes 4718596
  57.9 1.3 %copy-start.2 = (f32[9,6,16,32]{3,2,1,0:T(8,128)S(1)}, f32[9,6,16,32]{3,2,1,0:T(8,128)}, u32[]{:S(2)}) copy-start(f32[9,6,16,32]{3,2,1,0:T(8,128)} %shard_map.118) | copy-start | bytes 331780
  59.9 9.9 %copy-start.8 = (f32[64,9,3,3,3]{0,4,3,2,1:T(4,128)S(1)}, f32[64,9,3,3,3]{0,4,3,2,1:T(4,128)}, u32[]{:S(2)}) copy-start(f32[64,9,3,3,3]{0,4,3,2,1:T(4,128)} %param.22) | copy-start | bytes 186628
  61.4 17.0 %all-to-all-start = ((f32[16,1,5184]{2,1,0:T(1,128)}), f32[16,1,5184]{2,1,0:T(1,128)S(1)}, u32[]{:S(2)}, u32[]{:S(2)}) async-start(f32[16,1,5184]{2,1,0:T(1,128)} %all_to_all.8), calls=%async_computation | async-start | bytes 671744 | tf_op jit(solution)/shard_map/all_to_all | solution.py:228
  79.3 1.5 %copy-start.12 = (f32[64]{0:T(128)S(1)}, f32[64]{0:T(128)}, u32[]{:S(2)}) copy-start(f32[64]{0:T(128)} %param.23) | copy-start | bytes 772
